TPU v7x, 128 devices: a whole 4x4x4 slice. The times are simulated.
128 devices in a mesh: wide: 16 (over z, y), col: 8 (over x, core).
Axes of the slice: x: 4, y: 4, z: 4, core: 2. Of those that a mesh axis runs over, the one named last changes fastest.
Arguments:
- z_root: float32 [512, 16384], P('col', 'wide'), may hold values from -6 to 6
- z_child: float32 [512, 2, 8192], P('col', None, 'wide'), may hold values from -6 to 6
- z_grand: float32 [512, 4, 4096], P('col', None, 'wide'), may hold values from -6 to 6
- inv_root: float32 [16384, 16384], P('wide', 'col'), as said below
- inv_child: float32 [2, 8192, 8192], P(None, 'wide', 'col'), as said below
- inv_grand: float32 [4, 4096, 4096], P(None, 'wide', 'col'), as said below
- panel_child: float32 [2, 4096, 8192], P(None, 'col', 'wide'), may hold values from -0.046875 to 0.046875
- panel_grand: float32 [4, 2048, 4096], P(None, 'col', 'wide'), may hold values from -0.0625 to 0.0625
- anc_child: int32 [2, 32], P(None, 'col'), may hold values from 0 to 127, as said below
- anc_grand: int32 [4, 16], P(None, 'col'), may hold values from 0 to 255, as said below
Outputs:
- x_root: float32 [512, 16384], P('wide', 'col')
- x_child: float32 [512, 2, 8192], P('wide', None, 'col')
- x_grand: float32 [512, 4, 4096], P('wide', None, 'col')
Inputs may be any that keep to these rules, and one draw needn't show every extreme that they name: inv_root is lower triangular with a positive diagonal (entries above the diagonal are zero). Each inv_child[k] is lower triangular with a positive diagonal. Each inv_grand[g] is lower triangular with a positive diagonal. `anc_child`: each row lists distinct blocks in rising order and always names block 0 and block 127. `anc_grand`: row g lists 2048 // 256 distinct root blocks in rising order, block 0 and block 127 among them, then as many distinct blocks of child g // 2 (numbered 16384 // 128 + (g // 2) * 64 onwards) in rising order, its first and its last among them.
All inputs are finite; a program needn't handle non-finite values.
Results may differ from a plain program's by a relative error of at most 0.000096.
Values sent between devices are 32-bit elements; how exact they have to be, the bound alone decides.
No kernel may reach another device: no remote copies, remote signals or barrier semaphores. Data moves between devices by JAX's collectives and lax.ppermute only.
A program may use at most 128 MiB of HBM per device.

v0:
```python
import jax
import jax.numpy as jnp
from jax import lax
from jax.sharding import PartitionSpec as P

BLK = 128


PRECISE = lax.Precision.HIGHEST


def pick_blocks(source_rows, blocks):
    leading = source_rows.shape[0]
    tiled = source_rows.reshape(leading, source_rows.shape[1] // BLK, BLK)
    selected = jnp.take(tiled, blocks.reshape(-1), axis=1)
    return selected.reshape(leading, blocks.shape[0], blocks.shape[1] * BLK)


def spread_rhs(local_part):
    return lax.all_gather(local_part, "col", axis=0, tiled=True)


def solve_terms(right_rows, inverse):
    return lax.psum_scatter(
        jnp.einsum(
            "ski,kij->skj",
            right_rows,
            inverse,
            precision=PRECISE,
            preferred_element_type=jnp.float32,
        ),
        "wide",
        scatter_dimension=0,
        tiled=True,
    )


def spread_solved(solved_local):
    gathered = lax.all_gather(solved_local, "col", axis=2, tiled=True)
    return gathered.reshape(gathered.shape[0], -1)


def fetch_ancestors(source_rows, blocks):
    return lax.all_gather(pick_blocks(source_rows, blocks), "wide", axis=0, tiled=True)


def finish_level(z_local, inverse, partial_value):
    summed = lax.psum(partial_value, "col")
    right_side = spread_rhs(z_local) - summed
    solved = solve_terms(right_side, inverse)
    return solved


def per_device(
    z_root,
    z_child,
    z_grand,
    inv_root,
    inv_child,
    inv_grand,
    panel_child,
    panel_grand,
    anc_child,
    anc_grand,
):
    root_right = spread_rhs(z_root[:, None, :])
    root_solved = solve_terms(root_right, inv_root[None])
    x_root = root_solved[:, 0, :]
    root_rows = spread_solved(root_solved)
    near_rows = fetch_ancestors(root_rows, anc_child)
    partial_value = jnp.einsum(
        "ska,kaj->skj",
        near_rows,
        panel_child,
        precision=PRECISE,
        preferred_element_type=jnp.float32,
    )
    x_child = finish_level(z_child, inv_child, partial_value)
    child_rows = spread_solved(x_child)
    solved_all = jnp.concatenate([root_rows, child_rows], axis=1)
    far_rows = fetch_ancestors(solved_all, anc_grand)
    partial_grand = jnp.einsum(
        "sga,gaj->sgj", far_rows, panel_grand, precision=PRECISE, preferred_element_type=jnp.float32
    )
    x_grand = finish_level(z_grand, inv_grand, partial_grand)
    return (x_root, x_child, x_grand)


def solution(mesh):
    in_specs = (
        P("col", "wide"),
        P("col", None, "wide"),
        P("col", None, "wide"),
        P("wide", "col"),
        P(None, "wide", "col"),
        P(None, "wide", "col"),
        P(None, "col", "wide"),
        P(None, "col", "wide"),
        P(None, "col"),
        P(None, "col"),
    )
    out_specs = (P("wide", "col"), P("wide", None, "col"), P("wide", None, "col"))
    return jax.shard_map(
        per_device, mesh=mesh, in_specs=in_specs, out_specs=out_specs, check_vma=False
    )
```

profile of v0, /device:TPU:0, one launch (start us, length us, event | category | flops | bytes accessed | tf_op | source)
XLA Modules:
  0.0 726.2 jit_solution(2255232434404925078)
XLA Ops:
  7.2 0.7 all-gather.21.cloned.1.call-update
  8.0 29.4 %all-gather.21.cloned.1.call-done = f32[512,1024]{1,0:T(8,128)} async-done(((f32[64,1024]{1,0:T(8,128)}), f32[512,1024]{1,0:T(8,128)}) %all-gather.21.cloned.1.call-update) | async-done | bytes 2097168 | tf_op jit(solution)/shard_map/all_gather | solution.py:20
  37.4 30.4 %convolution_bitcast_fusion = f32[512,1,2048]{0,2,1:T(8,128)} fusion(f32[1024,2048]{1,0:T(8,128)} %param.13, f32[512,1024]{1,0:T(8,128)} %all-gather.21.cloned.1.call-done), kind=kOutput, calls=%fused_computation.3 | convolution fusion | flops 12884901888 | bytes 14680064 | tf_op jit(solution)/shard_map/ski,kij->skj/dot_general | solution.py:25
  67.8 11.0 %copy.75 = f32[512,1,2048]{2,1,0:T(1,128)} copy(f32[512,1,2048]{0,2,1:T(8,128)} %convolution_bitcast_fusion) | data formatting | bytes 8388608 | tf_op jit(solution)/shard_map/ski,kij->skj/transpose | solution.py:25
  78.8 0.0 all-gather.11.cloned.1.call-start
  78.9 0.6 copy-done.8
  79.5 0.6 dynamic-slice
  80.7 102.2 %all-reduce.9.cloned.1.call-done = f32[512,1,2048]{2,1,0:T(1,128)} async-done(((f32[512,1,2048]{2,1,0:T(1,128)}), f32[512,1,2048]{2,1,0:T(1,128)}) %all-reduce.9.cloned.1.call-update) | async-done | bytes 4194320
  183.0 1.7 constant_dynamic-slice_fusion
  184.7 0.1 reshape.104
  184.8 0.1 broadcast_bitcast_fusion.1
  184.9 25.1 %all-gather.11.cloned.1.call-done = f32[32,1,16384]{2,1,0:T(1,128)} async-done(((f32[32,1,2048]{2,1,0:T(1,128)}), f32[32,1,16384]{2,1,0:T(1,128)}) %all-gather.11.cloned.1.call-update) | async-done | bytes 2097168 | tf_op jit(solution)/shard_map/all_gather | solution.py:39
  210.0 4.2 copy.77
  214.3 2.1 gather_fusion
  216.4 0.1 copy.78
  216.5 0.1 gather.13
  216.6 0.7 copy_select_fusion.1
  217.3 0.8 copy.76
  218.1 0.0 all-reduce.5.cloned.1.call-start
  218.2 44.9 %all-gather.13.cloned.1.call-done = f32[512,2,512]{2,0,1:T(8,128)} async-done(((f32[32,2,512]{2,0,1:T(8,128)}), f32[512,2,512]{2,0,1:T(8,128)}) %all-gather.13.cloned.1.call-update) | async-done | bytes 2097168 | tf_op jit(solution)/shard_map/all_gather | solution.py:44
  263.0 7.0 convolution_bitcast_fusion.4
  270.1 19.4 %all-gather.9.cloned.1.call-done = f32[512,2,512]{2,0,1:T(8,128)} async-done(((f32[64,2,512]{2,0,1:T(8,128)}), f32[512,2,512]{2,0,1:T(8,128)}) %all-gather.9.cloned.1.call-update) | async-done | bytes 2097168 | tf_op jit(solution)/shard_map/all_gather | solution.py:20
  289.6 68.2 %all-reduce.5.cloned.1.call-done = f32[512,2,512]{2,0,1:T(8,128)} async-done(((f32[512,2,512]{2,0,1:T(8,128)}), f32[512,2,512]{2,0,1:T(8,128)}) %all-reduce.5.cloned.1.call-update) | async-done | bytes 2097168 | tf_op jit(solution)/shard_map/psum | solution.py:48
  357.8 12.2 %convolution_bitcast_fusion.2 = f32[512,2,1024]{2,0,1:T(8,128)} fusion(f32[2,512,1024]{2,1,0:T(8,128)} %param.14, f32[512,2,512]{2,0,1:T(8,128)} %all-gather.9.cloned.1.call-done, f32[512,2,512]{2,0,1:T(8,128)} %all-reduce.5.cloned.1.call-done), kind=kOutput, calls=%fused_computation.5 | convolution fusion | flops 6442975232 | bytes 12582912 | tf_op jit(solution)/shard_map/ski,kij->skj/dot_general | solution.py:25
  370.1 77.5 %reduce-scatter.3.cloned.1.call-done = f32[32,2,1024]{2,0,1:T(8,128)} async-done(((f32[512,2,1024]{2,0,1:T(8,128)}), f32[32,2,1024]{2,0,1:T(8,128)}) %reduce-scatter.3.cloned.1.call-update) | async-done | bytes 262160 | tf_op jit(solution)/shard_map/reduce_scatter | solution.py:24
  447.6 0.1 copy.84
  447.7 0.1 reshape.105
  447.9 0.1 broadcast_bitcast_fusion
  447.9 25.8 %all-gather.17.cloned.1.call-done = f32[32,2,8192]{2,0,1:T(8,128)} async-done(((f32[32,2,1024]{2,0,1:T(8,128)}), f32[32,2,8192]{2,0,1:T(8,128)}) %all-gather.17.cloned.1.call-update) | async-done | bytes 2097168 | tf_op jit(solution)/shard_map/all_gather | solution.py:39
  473.7 4.6 copy.81
  478.3 4.0 concatenate.6
  482.3 3.0 copy.83
  485.3 2.4 pad_maximum_fusion
  487.7 2.8 gather_fusion.1
  490.5 0.1 copy.85
  490.6 0.1 gather.15
  490.7 0.7 copy_select_fusion
  491.4 1.7 copy.80
  493.2 43.9 %all-gather.19.cloned.1.call-done = f32[512,4,256]{2,0,1:T(8,128)} async-done(((f32[32,4,256]{2,0,1:T(8,128)}), f32[512,4,256]{2,0,1:T(8,128)}) %all-gather.19.cloned.1.call-update) | async-done | bytes 2097168 | tf_op jit(solution)/shard_map/all_gather | solution.py:44
  537.1 4.9 convolution_bitcast_fusion.3
  542.1 21.7 %all-gather.15.cloned.1.call-done = f32[512,4,256]{2,0,1:T(8,128)} async-done(((f32[64,4,256]{2,0,1:T(8,128)}), f32[512,4,256]{2,0,1:T(8,128)}) %all-gather.15.cloned.1.call-update) | async-done | bytes 2097168 | tf_op jit(solution)/shard_map/all_gather | solution.py:20
  563.8 68.5 %all-reduce.7.cloned.1.call-done = f32[512,4,256]{2,0,1:T(8,128)} async-done(((f32[512,4,256]{2,0,1:T(8,128)}), f32[512,4,256]{2,0,1:T(8,128)}) %all-reduce.7.cloned.1.call-update) | async-done | bytes 2097168 | tf_op jit(solution)/shard_map/psum | solution.py:48
  632.3 7.8 %convolution_bitcast_fusion.1 = f32[512,4,512]{2,0,1:T(8,128)} fusion(f32[4,256,512]{2,1,0:T(8,128)S(1)} %copy-done, f32[512,4,256]{2,0,1:T(8,128)} %all-gather.15.cloned.1.call-done, f32[512,4,256]{2,0,1:T(8,128)} %all-reduce.7.cloned.1.call-done), kind=kOutput, calls=%fused_computation.4 | convolution fusion | flops 3221749760 | bytes 10485760 | tf_op jit(solution)/shard_map/ski,kij->skj/dot_general | solution.py:25
  640.0 0.9 copy-done.2
  641.0 0.8 copy.95
  641.8 0.9 copy.87
  642.7 74.9 %reduce-scatter.5.cloned.1.call-done = f32[32,4,512]{2,0,1:T(8,128)} async-done(((f32[512,4,512]{2,0,1:T(8,128)}), f32[32,4,512]{2,0,1:T(8,128)}) %reduce-scatter.5.cloned.1.call-update) | async-done | bytes 262160 | tf_op jit(solution)/shard_map/reduce_scatter | solution.py:24
  717.6 1.8 copy.88
  (44 shorter events, 0.7 us)
Async XLA Ops:
  7.2 625.1 %copy-start = (f32[4,256,512]{2,1,0:T(8,128)S(1)}, f32[4,256,512]{2,1,0:T(8,128)}, u32[]{:S(2)}) copy-start(f32[4,256,512]{2,1,0:T(8,128)} %param.15) | copy-start | bytes 6291460
  7.2 30.2 %all-gather.21.cloned.1.call-start = ((), (), s32[]{:S(2)}) async-start(), calls=%async_computation.12 | async-start | bytes 2359296 | tf_op jit(solution)/shard_map/all_gather | solution.py:20
  7.9 175.0 %all-reduce.9.cloned.1.call-start = ((), (), s32[]{:S(2)}) async-start(), calls=%async_computation.13 | async-start | bytes 8388608
  78.8 0.7 copy-start.8
  78.8 105.9 %copy-start.7 = (s32[2,4]{1,0:T(2,128)S(1)}, s32[2,4]{1,0:T(2,128)}, u32[]{:S(2)}) copy-start(s32[2,4]{1,0:T(2,128)} %param.18) | copy-start | bytes 100
  78.8 131.2 %all-gather.11.cloned.1.call-start = ((), (), s32[]{:S(2)}) async-start(), calls=%async_computation.3 | async-start | bytes 2359296 | tf_op jit(solution)/shard_map/all_gather | solution.py:39
  184.7 78.4 %all-gather.13.cloned.1.call-start = ((), (), s32[]{:S(2)}) async-start(), calls=%async_computation.4 | async-start | bytes 2228224 | tf_op jit(solution)/shard_map/all_gather | solution.py:44
  210.0 7.3 %copy-start.5 = (f32[64,2,512]{2,1,0:T(2,128)S(1)}, f32[64,2,512]{2,1,0:T(2,128)}, u32[]{:S(2)}) copy-start(f32[64,2,512]{2,1,0:T(2,128)} %param.11) | copy-start | bytes 786436
  217.3 72.3 %all-gather.9.cloned.1.call-start = ((), (), s32[]{:S(2)}) async-start(), calls=%async_computation.2 | async-start | bytes 2359296 | tf_op jit(solution)/shard_map/all_gather | solution.py:20
  218.1 139.7 %all-reduce.5.cloned.1.call-start = ((), (), s32[]{:S(2)}) async-start(), calls=%async_computation.5 | async-start | bytes 4194304 | tf_op jit(solution)/shard_map/psum | solution.py:48
  270.1 177.5 %reduce-scatter.3.cloned.1.call-start = ((), (), s32[]{:S(2)}) async-start(), calls=%async_computation.6 | async-start | bytes 4456448 | tf_op jit(solution)/shard_map/reduce_scatter | solution.py:24
  370.0 77.7 %copy-start.6 = (s32[4,2]{0,1:T(2,128)S(1)}, s32[4,2]{0,1:T(2,128)}, u32[]{:S(2)}) copy-start(s32[4,2]{0,1:T(2,128)} %param.19) | copy-start | bytes 100
  370.0 103.7 %all-gather.17.cloned.1.call-start = ((), (), s32[]{:S(2)}) async-start(), calls=%async_computation.8 | async-start | bytes 2359296 | tf_op jit(solution)/shard_map/all_gather | solution.py:39
  447.6 89.6 %all-gather.19.cloned.1.call-start = ((), (), s32[]{:S(2)}) async-start(), calls=%async_computation.9 | async-start | bytes 2228224 | tf_op jit(solution)/shard_map/all_gather | solution.py:44
  482.3 3.0 copy-start.1
  487.7 49.5 %copy-start.3 = (f32[4,256,256]{2,1,0:T(8,128)S(1)}, f32[4,256,256]{2,1,0:T(8,128)}, u32[]{:S(2)}) copy-start(f32[4,256,256]{2,1,0:T(8,128)} %param.17) | copy-start | bytes 3145732
  491.4 72.4 %all-gather.15.cloned.1.call-start = ((), (), s32[]{:S(2)}) async-start(), calls=%async_computation.7 | async-start | bytes 2359296 | tf_op jit(solution)/shard_map/all_gather | solution.py:20
  493.2 139.1 %all-reduce.7.cloned.1.call-start = ((), (), s32[]{:S(2)}) async-start(), calls=%async_computation.10 | async-start | bytes 4194304 | tf_op jit(solution)/shard_map/psum | solution.py:48
  542.0 175.5 %reduce-scatter.5.cloned.1.call-start = ((), (), s32[]{:S(2)}) async-start(), calls=%async_computation.11 | async-start | bytes 4456448 | tf_op jit(solution)/shard_map/reduce_scatter | solution.py:24
  640.0 0.9 copy-start.2
  640.0 1.7 copy-start.4
Sparse Core Ops, SparseCore 0:
  9.7 27.5 all-gather.20
  79.0 103.9 all-reduce.8
  185.2 24.7 all-gather.10
  217.4 45.5 all-gather.12
  265.2 24.3 all-gather.8
  291.8 65.9 all-reduce.4
  370.1 77.3 reduce-scatter.2
  449.4 24.3 all-gather.16
  491.5 45.5 all-gather.18
  539.4 24.3 all-gather.14
  566.3 65.9 all-reduce.6
  640.2 77.3 reduce-scatter.4
where the time goes:
time: 727 us; the launch traced here: 726 us
  waiting for transfers between devices  602 us (83%)
  matrix products  62.3 us (9%)
  local copies, waits for them, and re-layouts  42.2 us (6%)
  between operations  15 us (2%)
    reduce_scatter x2, waiting for transfers between devices, solve_terms(): lax.psum_scatter(jnp.einsum('ski,kij->skj', right_rows, inverse, precisio...  152 us
    psum x2, waiting for transfers between devices, finish_level(): summed = lax.psum(partial_value, 'col')  137 us
    unnamed x13, waiting for transfers between devices  103 us
    all_gather x2, waiting for transfers between devices, fetch_ancestors(): lax.all_gather(pick_blocks(source_rows, blocks), 'wide', axis=0, tiled=True)  88.8 us
    all_gather x3, waiting for transfers between devices, spread_rhs(): return lax.all_gather(local_part, 'col', axis=0, tiled=True)  70.5 us
    all_gather x2, waiting for transfers between devices, spread_solved(): gathered = lax.all_gather(solved_local, 'col', axis=2, tiled=True)  50.9 us
    dot_general x3, matrix products, solve_terms(): jnp.einsum('ski,kij->skj', right_rows, inverse, precision=PRECISE, prefer...  50.4 us
  transfers between devices with their start and end apart: 12, of which 12 were waited for; matrix products, arithmetic and copies ran while one was open for 2% of the time, Pallas kernels for 0%

commit v1 on v0

v1 whole, which is shorter than its diff:
```python
import jax
import jax.numpy as jnp
from jax import lax
from jax.sharding import PartitionSpec as P

BLK = 128


PRECISE = lax.Precision.HIGHEST


def pick_blocks(source_rows, blocks):
    leading = source_rows.shape[0]
    tiled = source_rows.reshape(leading, source_rows.shape[1] // BLK, BLK)
    selected = jnp.take(tiled, blocks.reshape(-1), axis=1)
    return selected.reshape(leading, blocks.shape[0], blocks.shape[1] * BLK)


def exchange_sum(partial, axis):
    n = lax.axis_size(axis)
    chunk = partial.shape[0] // n
    parts = lax.all_to_all(partial.reshape((n, chunk) + partial.shape[1:]), axis, 0, 0, tiled=False)
    return parts.sum(0)


def exchange_gather(local, axis, dim):
    n = lax.axis_size(axis)
    stacked = jnp.broadcast_to(local[None], (n,) + local.shape)
    parts = lax.all_to_all(stacked, axis, 0, 0, tiled=False)
    parts = jnp.moveaxis(parts, 0, dim)
    return parts.reshape(local.shape[:dim] + (n * local.shape[dim],) + local.shape[dim + 1 :])


def matmul(lhs, rhs, spec):
    return jnp.einsum(spec, lhs, rhs, precision=PRECISE, preferred_element_type=jnp.float32)


def level(z_local, update_partial, inverse):
    update = exchange_sum(update_partial, "col")
    right_side = exchange_gather(z_local - update, "col", 0)
    return exchange_sum(matmul(right_side, inverse, "ski,kij->skj"), "wide")


def per_device(
    z_root,
    z_child,
    z_grand,
    inv_root,
    inv_child,
    inv_grand,
    panel_child,
    panel_grand,
    anc_child,
    anc_grand,
):
    root_right = exchange_gather(z_root, "col", 0)
    x_root = exchange_sum(matmul(root_right, inv_root, "si,ij->sj"), "wide")
    root_rows = exchange_gather(x_root, "col", 1)
    near_rows = exchange_gather(pick_blocks(root_rows, anc_child), "wide", 0)
    x_child = level(z_child, matmul(near_rows, panel_child, "ska,kaj->skj"), inv_child)
    child_rows = exchange_gather(x_child, "col", 2)
    solved_all = jnp.concatenate([root_rows, child_rows.reshape(child_rows.shape[0], -1)], axis=1)
    far_rows = exchange_gather(pick_blocks(solved_all, anc_grand), "wide", 0)
    x_grand = level(z_grand, matmul(far_rows, panel_grand, "sga,gaj->sgj"), inv_grand)
    return (x_root, x_child, x_grand)


def solution(mesh):
    in_specs = (
        P("col", "wide"),
        P("col", None, "wide"),
        P("col", None, "wide"),
        P("wide", "col"),
        P(None, "wide", "col"),
        P(None, "wide", "col"),
        P(None, "col", "wide"),
        P(None, "col", "wide"),
        P(None, "col"),
        P(None, "col"),
    )
    out_specs = (P("wide", "col"), P("wide", None, "col"), P("wide", None, "col"))
    return jax.shard_map(
        per_device, mesh=mesh, in_specs=in_specs, out_specs=out_specs, check_vma=False
    )
```

time: 727 us -> 533 us (0.73)
  waiting for transfers between devices: 602 us -> 53.9 us
  blocking collectives: 0 us -> 382 us
  matrix products: 62.3 us -> 32.3 us
  between operations: 15 us -> 1 us
  other arithmetic: 3.81 us -> 13.8 us
  starting transfers between devices: 0.49 us -> 8.94 us
    all_to_all x0 -> x10, blocking collectives: none -> 382 us  [the longest x5 228 us: exchange_sum(): lax.all_to_all(partial.reshape((n, chunk) + partial.shape[1:]), axis, 0,...]
    all_gather x7 -> x0, waiting for transfers between devices: 210 us -> none  [the longest x2 88.8 us: fetch_ancestors(): lax.all_gather(pick_blocks(source_rows, blocks), 'wide', axis=0, tiled=True)]
    reduce_scatter x2 -> x0, waiting for transfers between devices: 152 us -> none  [solve_terms(): lax.psum_scatter(jnp.einsum('ski,kij->skj', right_rows, inverse, precisio...]
    psum x2 -> x0, waiting for transfers between devices: 137 us -> none  [finish_level(): summed = lax.psum(partial_value, 'col')]
    unnamed x13 -> x0, waiting for transfers between devices: 103 us -> none
    all_to_all x0 -> x2, waiting for transfers between devices: none -> 53.9 us  [exchange_gather(): parts = lax.all_to_all(stacked, axis, 0, 0, tiled=False)]
    dot_general x5, matrix products: 62.3 us -> 32.3 us  [matmul(): jnp.einsum(spec, lhs, rhs, precision=PRECISE, preferred_element_type=jnp....]
    reduce_sum x0 -> x5, other arithmetic: none -> 11.2 us  [exchange_sum(): return parts.sum(0)]
  transfers between devices with their start and end apart: 12 -> 2, of which waited for: 12 -> 2; matrix products, arithmetic and copies ran while one was open for 2% -> 0% of each run, Pallas kernels for 0% -> 0%
where the time goes in v1:
time: 533 us; the launch traced here: 532 us
  blocking collectives  382 us (72%)
  waiting for transfers between devices  53.9 us (10%)
  local copies, waits for them, and re-layouts  40.3 us (8%)
  matrix products  32.3 us (6%)
  other arithmetic  13.8 us (3%)
  starting transfers between devices  8.94 us (2%)
    all_to_all x5, blocking collectives, exchange_sum(): lax.all_to_all(partial.reshape((n, chunk) + partial.shape[1:]), axis, 0,...  228 us
    all_to_all x5, blocking collectives, exchange_gather(): parts = lax.all_to_all(stacked, axis, 0, 0, tiled=False)  154 us
    all_to_all x2, waiting for transfers between devices, exchange_gather(): parts = lax.all_to_all(stacked, axis, 0, 0, tiled=False)  53.9 us
    dot_general x5, matrix products, matmul(): jnp.einsum(spec, lhs, rhs, precision=PRECISE, preferred_element_type=jnp....  32.3 us
    reduce_sum x5, other arithmetic, exchange_sum(): return parts.sum(0)  11.2 us
  transfers between devices with their start and end apart: 2, of which 2 were waited for; matrix products, arithmetic and copies ran while one was open for 0% of the time, Pallas kernels for 0%

profile of v1, /device:TPU:0, one launch (start us, length us, event | category | flops | bytes accessed | tf_op | source)
XLA Modules:
  0.0 532.2 jit_solution(14883836734273515946)
XLA Ops:
  0.6 1.3 broadcast_in_dim.68
  2.0 31.5 %all_to_all.60 = f32[8,64,1024]{2,1,0:T(8,128)S(1)} all-to-all(f32[8,64,1024]{2,1,0:T(8,128)S(1)} %broadcast_in_dim.68), channel_id=1, replica_groups=mesh['wide'=16,'col'=8] {'col'}, dimensions={0} | all-to-all | bytes 4194304 | tf_op jit(solution)/shard_map/all_to_all | solution.py:29
  33.5 16.1 %fusion = f32[16,32,2048]{2,1,0:T(8,128)S(1)} fusion(f32[16,32,1024]{2,1,0:T(8,128)S(1)} %bitcast.48, f32[1024,2048]{1,0:T(8,128)} %param.13), kind=kOutput, calls=%fused_computation.2 | convolution fusion | flops 12884901888 | bytes 14680064 | tf_op jit(solution)/shard_map/si,ij->sj/dot_general | solution.py:35
  49.6 58.6 %all_to_all.61 = f32[16,32,2048]{2,1,0:T(8,128)} all-to-all(f32[16,32,2048]{2,1,0:T(8,128)S(1)} %fusion), channel_id=1, replica_groups=mesh['wide'=16,'col'=8] {'wide'}, dimensions={0} | all-to-all | bytes 8388608 | tf_op jit(solution)/shard_map/all_to_all | solution.py:22
  108.2 2.4 reduce_sum.45
  110.6 1.5 broadcast_in_dim.72
  112.2 4.5 all-to-all-start.2
  116.9 27.0 %all-to-all-done.2 = f32[8,32,2048]{2,1,0:T(8,128)} async-done(((f32[8,32,2048]{2,1,0:T(8,128)}), f32[8,32,2048]{2,1,0:T(8,128)}, u32[]{:S(2)}, u32[]{:S(2)}) %all-to-all-start.2) | async-done | bytes 2097184 | tf_op jit(solution)/shard_map/all_to_all | solution.py:29
  143.9 4.1 copy.36
  148.0 2.7 reshape_reshape.4
  150.7 4.1 copy.37
  154.8 2.1 gather_fusion
  157.3 0.2 broadcast_in_dim.74
  157.5 31.1 %all_to_all.62 = f32[16,32,2,512]{3,1,2,0:T(8,128)S(1)} all-to-all(f32[16,32,2,512]{3,1,2,0:T(8,128)S(1)} %broadcast_in_dim.74), channel_id=1, replica_groups=mesh['wide'=16,'col'=8] {'wide'}, dimensions={0} | all-to-all | bytes 4194304 | tf_op jit(solution)/shard_map/all_to_all | solution.py:29
  188.7 0.2 copy.40
  188.9 1.4 copy-done.3
  190.2 3.5 fusion.4
  194.0 30.7 %all_to_all.63 = f32[8,64,2,512]{3,1,2,0:T(8,128)} all-to-all(f32[8,64,2,512]{3,1,2,0:T(8,128)S(1)} %copy.41), channel_id=1, replica_groups=mesh['wide'=16,'col'=8] {'col'}, dimensions={0} | all-to-all | bytes 4194304 | tf_op jit(solution)/shard_map/all_to_all | solution.py:22
  224.7 1.9 reduce_sum.46
  226.6 0.3 broadcast_in_dim.75
  226.9 30.0 %all_to_all.64 = f32[8,64,2,512]{3,1,2,0:T(8,128)S(1)} all-to-all(f32[8,64,2,512]{3,1,2,0:T(8,128)S(1)} %broadcast_in_dim.75), channel_id=1, replica_groups=mesh['wide'=16,'col'=8] {'col'}, dimensions={0} | all-to-all | bytes 4194304 | tf_op jit(solution)/shard_map/all_to_all | solution.py:29
  257.0 2.0 copy-done.2
  259.0 7.0 %fusion.5 = f32[2,512,1024]{2,1,0:T(8,128)S(1)} fusion(f32[512,2,512]{2,0,1:T(8,128)S(1)} %bitcast.51, f32[2,512,1024]{2,1,0:T(8,128)S(1)} %copy-done.2), kind=kOutput, calls=%fused_computation.23 | convolution fusion | flops 6442450944 | bytes 10485760 | tf_op jit(solution)/shard_map/ski,kij->skj/dot_general | solution.py:35
  266.1 0.6 copy.45
  266.6 54.1 %all_to_all.65 = f32[16,32,2,1024]{3,1,2,0:T(8,128)} all-to-all(f32[16,32,2,1024]{3,1,2,0:T(8,128)S(1)} %copy.45), channel_id=1, replica_groups=mesh['wide'=16,'col'=8] {'wide'}, dimensions={0} | all-to-all | bytes 8388608 | tf_op jit(solution)/shard_map/all_to_all | solution.py:22
  320.8 2.5 reduce_sum.47
  323.5 2.0 broadcast_in_dim.79
  325.5 4.5 all-to-all-start.7
  330.3 26.9 %all-to-all-done.7 = f32[8,32,2,1024]{3,2,1,0:T(2,128)} async-done(((f32[8,32,2,1024]{3,2,1,0:T(2,128)}), f32[8,32,2,1024]{3,2,1,0:T(2,128)}, u32[]{:S(2)}, u32[]{:S(2)}) %all-to-all-start.7) | async-done | bytes 2097184 | tf_op jit(solution)/shard_map/all_to_all | solution.py:29
  357.2 4.1 copy.48
  361.3 2.7 concatenate.6
  364.0 3.0 copy.50
  367.0 2.4 pad_maximum_fusion
  369.4 2.7 gather_fusion.1
  372.4 0.2 broadcast_in_dim.81
  372.6 31.1 %all_to_all.66 = f32[16,32,4,256]{3,1,2,0:T(8,128)S(1)} all-to-all(f32[16,32,4,256]{3,1,2,0:T(8,128)S(1)} %broadcast_in_dim.81), channel_id=1, replica_groups=mesh['wide'=16,'col'=8] {'wide'}, dimensions={0} | all-to-all | bytes 4194304 | tf_op jit(solution)/shard_map/all_to_all | solution.py:29
  403.7 0.2 copy.54
  404.0 1.0 copy-done.4
  405.0 2.0 fusion.6
  407.2 30.7 %all_to_all.67 = f32[8,64,4,256]{3,1,2,0:T(8,128)} all-to-all(f32[8,64,4,256]{3,1,2,0:T(8,128)S(1)} %copy.55), channel_id=1, replica_groups=mesh['wide'=16,'col'=8] {'col'}, dimensions={0} | all-to-all | bytes 4194304 | tf_op jit(solution)/shard_map/all_to_all | solution.py:22
  437.9 1.8 reduce_sum.48
  439.8 0.2 broadcast_in_dim.82
  440.0 30.0 %all_to_all.68 = f32[8,64,4,256]{3,1,2,0:T(8,128)S(1)} all-to-all(f32[8,64,4,256]{3,1,2,0:T(8,128)S(1)} %broadcast_in_dim.82), channel_id=1, replica_groups=mesh['wide'=16,'col'=8] {'col'}, dimensions={0} | all-to-all | bytes 4194304 | tf_op jit(solution)/shard_map/all_to_all | solution.py:29
  470.1 3.6 fusion.7
  473.8 0.8 copy.59
  474.6 54.1 %all_to_all.69 = f32[16,32,4,512]{3,1,2,0:T(8,128)} all-to-all(f32[16,32,4,512]{3,1,2,0:T(8,128)S(1)} %copy.59), channel_id=1, replica_groups=mesh['wide'=16,'col'=8] {'wide'}, dimensions={0} | all-to-all | bytes 8388608 | tf_op jit(solution)/shard_map/all_to_all | solution.py:22
  528.7 2.6 reduce_sum.49
  531.3 0.9 copy.62
  (46 shorter events, 2.0 us)
Async XLA Ops:
  0.6 469.5 %copy-start = (f32[4,256,512]{2,1,0:T(8,128)S(1)}, f32[4,256,512]{2,1,0:T(8,128)}, u32[]{:S(2)}) copy-start(f32[4,256,512]{2,1,0:T(8,128)} %param.15) | copy-start | bytes 6291460
  110.6 1.6 copy-start.5
  112.2 4.5 copy-start.10
  112.2 31.7 %all-to-all-start.2 = ((f32[8,32,2048]{2,1,0:T(8,128)}), f32[8,32,2048]{2,1,0:T(8,128)}, u32[]{:S(2)}, u32[]{:S(2)}) async-start(f32[8,32,2048]{2,1,0:T(8,128)} %broadcast_in_dim.72), calls=%async_computation.2 | async-start | bytes 4194304 | tf_op jit(solution)/shard_map/all_to_all | solution.py:29
  188.7 1.6 copy-start.3
  224.7 1.9 copy-start.7
  256.8 2.2 copy-start.2
  323.5 2.0 copy-start.6
  325.5 4.5 copy-start.9
  325.5 31.7 %all-to-all-start.7 = ((f32[8,32,2,1024]{3,2,1,0:T(2,128)}), f32[8,32,2,1024]{3,2,1,0:T(2,128)}, u32[]{:S(2)}, u32[]{:S(2)}) async-start(f32[8,32,2,1024]{3,2,1,0:T(2,128)} %broadcast_in_dim.79), calls=%async_computation.7 | async-start | bytes 4194304 | tf_op jit(solution)/shard_map/all_to_all | solution.py:29
  364.0 3.0 copy-start.1
  403.7 1.2 copy-start.4
  437.9 1.8 copy-start.8

commit v2 on v1

--- a/solution.py
+++ b/solution.py
@@ -41,7 +41,15 @@
     return exchange_sum(matmul(right_side, inverse, "ski,kij->skj"), "wide")
 
 
-def per_device(
+STREAMS = 2
+
+
+def stream_rows(z_local, stream):
+    rows = z_local.reshape((2, STREAMS, z_local.shape[0] // (2 * STREAMS)) + z_local.shape[1:])[:, stream]
+    return rows.reshape((-1,) + z_local.shape[1:])
+
+
+def one_stream(
     z_root,
     z_child,
     z_grand,
@@ -65,6 +73,14 @@
     return (x_root, x_child, x_grand)
 
 
+def per_device(z_root, z_child, z_grand, *rest):
+    outs = [
+        one_stream(stream_rows(z_root, h), stream_rows(z_child, h), stream_rows(z_grand, h), *rest)
+        for h in range(STREAMS)
+    ]
+    return tuple(jnp.concatenate(parts, axis=0) for parts in zip(*outs))
+
+
 def solution(mesh):
     in_specs = (
         P("col", "wide"),

time: 533 us -> 638 us (1.20); the launches traced: 532 us -> 626 us
  blocking collectives: 382 us -> 20.2 us
  waiting for transfers between devices: 53.9 us -> 347 us
  starting transfers between devices: 8.94 us -> 100 us
  local copies, waits for them, and re-layouts: 40.3 us -> 87.6 us
  other arithmetic: 13.8 us -> 27.4 us
  matrix products: 32.3 us -> 42.4 us
    all_to_all x5 -> x0, blocking collectives: 228 us -> none  [exchange_sum(): lax.all_to_all(partial.reshape((n, chunk) + partial.shape[1:]), axis, 0,...]
    all_to_all x0 -> x10, waiting for transfers between devices: none -> 198 us  [exchange_sum(): lax.all_to_all(partial.reshape((n, chunk) + partial.shape[1:]), axis, 0,...]
    all_to_all x5 -> x1, blocking collectives: 154 us -> 20.2 us  [exchange_gather(): parts = lax.all_to_all(stacked, axis, 0, 0, tiled=False)]
    all_to_all x2 -> x13, waiting for transfers between devices: 53.9 us -> 148 us  [exchange_gather(): parts = lax.all_to_all(stacked, axis, 0, 0, tiled=False)]
    all_to_all x0 -> x10, starting transfers between devices: none -> 47 us  [exchange_sum(): lax.all_to_all(partial.reshape((n, chunk) + partial.shape[1:]), axis, 0,...]
    all_to_all x2 -> x13, starting transfers between devices: 8.94 us -> 53.5 us  [exchange_gather(): parts = lax.all_to_all(stacked, axis, 0, 0, tiled=False)]
    broadcast_in_dim x7 -> x22, local copies, waits for them, and re-layouts: 5.88 us -> 21.5 us  [exchange_gather(): stacked = jnp.broadcast_to(local[None], (n,) + local.shape)]
    dot_general x5 -> x10, matrix products: 32.3 us -> 42.4 us  [matmul(): jnp.einsum(spec, lhs, rhs, precision=PRECISE, preferred_element_type=jnp....]
  transfers between devices with their start and end apart: 2 -> 23, of which waited for: 2 -> 23; matrix products, arithmetic and copies ran while one was open for 0% -> 18% of each run, Pallas kernels for 0% -> 0%
where the time goes in v2:
time: 638 us; the launch traced here: 626 us
  waiting for transfers between devices  347 us (54%)
  starting transfers between devices  100 us (16%)
  local copies, waits for them, and re-layouts  87.6 us (14%)
  matrix products  42.4 us (7%)
  other arithmetic  27.4 us (4%)
  blocking collectives  20.2 us (3%)
    all_to_all x10, waiting for transfers between devices, exchange_sum(): lax.all_to_all(partial.reshape((n, chunk) + partial.shape[1:]), axis, 0,...  198 us
    all_to_all x13, waiting for transfers between devices, exchange_gather(): parts = lax.all_to_all(stacked, axis, 0, 0, tiled=False)  148 us
    all_to_all x13, starting transfers between devices, exchange_gather(): parts = lax.all_to_all(stacked, axis, 0, 0, tiled=False)  53.5 us
    all_to_all x10, starting transfers between devices, exchange_sum(): lax.all_to_all(partial.reshape((n, chunk) + partial.shape[1:]), axis, 0,...  47 us
    dot_general x10, matrix products, matmul(): jnp.einsum(spec, lhs, rhs, precision=PRECISE, preferred_element_type=jnp....  42.4 us
    broadcast_in_dim x22, local copies, waits for them, and re-layouts, exchange_gather(): stacked = jnp.broadcast_to(local[None], (n,) + local.shape)  21.5 us
    all_to_all x1, blocking collectives, exchange_gather(): parts = lax.all_to_all(stacked, axis, 0, 0, tiled=False)  20.2 us
    reduce_sum x10, other arithmetic, exchange_sum(): return parts.sum(0)  17.6 us
  transfers between devices with their start and end apart: 23, of which 23 were waited for; matrix products, arithmetic and copies ran while one was open for 18% of the time, Pallas kernels for 0%

profile of v2, /device:TPU:0, one launch (start us, length us, event | category | flops | bytes accessed | tf_op | source)
XLA Modules:
  0.0 626.3 jit_solution(19856233844621581)
XLA Ops:
  1.9 20.2 %all_to_all.120 = f32[8,32,1024]{2,1,0:T(8,128)} all-to-all(f32[8,32,1024]{2,1,0:T(8,128)S(1)} %broadcast_in_dim.59), channel_id=1, replica_groups=mesh['wide'=16,'col'=8] {'col'}, dimensions={0} | all-to-all | bytes 2097152 | tf_op jit(solution)/shard_map/all_to_all | solution.py:29
  26.8 10.9 %fusion.2 = f32[16,16,2048]{2,1,0:T(8,128)} fusion(f32[16,16,1024]{2,1,0:T(8,128)} %bitcast.100, f32[1024,2048]{1,0:T(8,128)} %param.17), kind=kOutput, calls=%fused_computation.6 | convolution fusion | flops 6442450944 | bytes 11534336 | tf_op jit(solution)/shard_map/si,ij->sj/dot_general | solution.py:35
  37.7 5.0 all-to-all-done.2
  42.7 8.2 %all-to-all-start.1 = ((f32[16,16,2048]{2,1,0:T(8,128)}), f32[16,16,2048]{2,1,0:T(8,128)}, u32[]{:S(2)}, u32[]{:S(2)}) async-start(f32[16,16,2048]{2,1,0:T(8,128)} %fusion.2), calls=%async_computation.1 | async-start | bytes 4194304 | tf_op jit(solution)/shard_map/all_to_all | solution.py:22
  51.0 10.6 %fusion = f32[16,16,2048]{2,1,0:T(8,128)} fusion(f32[16,16,1024]{2,1,0:T(8,128)S(1)} %bitcast.99, f32[1024,2048]{1,0:T(8,128)} %param.17), kind=kOutput, calls=%fused_computation.4 | convolution fusion | flops 6442450944 | bytes 11534336 | tf_op jit(solution)/shard_map/si,ij->sj/dot_general | solution.py:35
  61.5 20.6 %all-to-all-done.1 = f32[16,16,2048]{2,1,0:T(8,128)} async-done(((f32[16,16,2048]{2,1,0:T(8,128)}), f32[16,16,2048]{2,1,0:T(8,128)}, u32[]{:S(2)}, u32[]{:S(2)}) %all-to-all-start.1) | async-done | bytes 2097184 | tf_op jit(solution)/shard_map/all_to_all | solution.py:22
  82.1 4.4 all-to-all-start.3
  88.3 27.7 %all-to-all-done.3 = f32[16,16,2048]{2,1,0:T(8,128)} async-done(((f32[16,16,2048]{2,1,0:T(8,128)}), f32[16,16,2048]{2,1,0:T(8,128)}, u32[]{:S(2)}, u32[]{:S(2)}) %all-to-all-start.3) | async-done | bytes 2097184 | tf_op jit(solution)/shard_map/all_to_all | solution.py:22
  122.3 14.2 %all-to-all-done.4 = f32[8,16,2048]{2,1,0:T(8,128)S(1)} async-done(((f32[8,16,2048]{2,1,0:T(8,128)}), f32[8,16,2048]{2,1,0:T(8,128)S(1)}, u32[]{:S(2)}, u32[]{:S(2)}) %all-to-all-start.4) | async-done | bytes 1048608 | tf_op jit(solution)/shard_map/all_to_all | solution.py:29
  137.6 4.2 all-to-all-start.9
  146.5 11.3 %all-to-all-done.9 = f32[8,16,2048]{2,1,0:T(8,128)} async-done(((f32[8,16,2048]{2,1,0:T(8,128)}), f32[8,16,2048]{2,1,0:T(8,128)}, u32[]{:S(2)}, u32[]{:S(2)}) %all-to-all-start.9) | async-done | bytes 1048608 | tf_op jit(solution)/shard_map/all_to_all | solution.py:29
  166.9 4.5 all-to-all-start.5
  171.5 17.6 %all-to-all-done.5 = f32[16,16,2,512]{3,1,2,0:T(8,128)} async-done(((f32[16,16,2,512]{3,1,2,0:T(8,128)}), f32[16,16,2,512]{3,1,2,0:T(8,128)}, u32[]{:S(2)}, u32[]{:S(2)}) %all-to-all-start.5) | async-done | bytes 1048608 | tf_op jit(solution)/shard_map/all_to_all | solution.py:29
  190.2 4.3 all-to-all-start.10
  199.5 11.3 %all-to-all-done.10 = f32[16,16,2,512]{3,1,2,0:T(8,128)} async-done(((f32[16,16,2,512]{3,1,2,0:T(8,128)}), f32[16,16,2,512]{3,1,2,0:T(8,128)}, u32[]{:S(2)}, u32[]{:S(2)}) %all-to-all-start.10) | async-done | bytes 1048608 | tf_op jit(solution)/shard_map/all_to_all | solution.py:29
  210.9 4.2 all-to-all-start.6
  220.1 11.0 %all-to-all-done.6 = f32[8,32,2,512]{3,1,2,0:T(8,128)} async-done(((f32[8,32,2,512]{3,1,2,0:T(8,128)}), f32[8,32,2,512]{3,1,2,0:T(8,128)}, u32[]{:S(2)}, u32[]{:S(2)}) %all-to-all-start.6) | async-done | bytes 1048608 | tf_op jit(solution)/shard_map/all_to_all | solution.py:22
  231.1 4.2 all-to-all-start.11
  240.6 10.7 %all-to-all-done.11 = f32[8,32,2,512]{3,1,2,0:T(8,128)} async-done(((f32[8,32,2,512]{3,1,2,0:T(8,128)}), f32[8,32,2,512]{3,1,2,0:T(8,128)}, u32[]{:S(2)}, u32[]{:S(2)}) %all-to-all-start.11) | async-done | bytes 1048608 | tf_op jit(solution)/shard_map/all_to_all | solution.py:22
  252.4 4.4 all-to-all-start.7
  260.5 12.3 %all-to-all-done.7 = f32[8,32,2,512]{3,1,2,0:T(8,128)} async-done(((f32[8,32,2,512]{3,1,2,0:T(8,128)}), f32[8,32,2,512]{3,1,2,0:T(8,128)}, u32[]{:S(2)}, u32[]{:S(2)}) %all-to-all-start.7) | async-done | bytes 1048608 | tf_op jit(solution)/shard_map/all_to_all | solution.py:29
  273.9 4.3 all-to-all-start.12
  279.5 5.4 fusion.8
  286.4 7.7 %all-to-all-done.12 = f32[8,32,2,512]{3,1,2,0:T(8,128)} async-done(((f32[8,32,2,512]{3,1,2,0:T(8,128)}), f32[8,32,2,512]{3,1,2,0:T(8,128)}, u32[]{:S(2)}, u32[]{:S(2)}) %all-to-all-start.12) | async-done | bytes 1048608 | tf_op jit(solution)/shard_map/all_to_all | solution.py:29
  294.1 4.4 all-to-all-start.8
  299.9 5.4 fusion.10
  306.8 23.7 %all-to-all-done.8 = f32[16,16,2,1024]{3,1,2,0:T(8,128)} async-done(((f32[16,16,2,1024]{3,1,2,0:T(8,128)}), f32[16,16,2,1024]{3,1,2,0:T(8,128)}, u32[]{:S(2)}, u32[]{:S(2)}) %all-to-all-start.8) | async-done | bytes 2097184 | tf_op jit(solution)/shard_map/all_to_all | solution.py:22
  330.5 4.4 all-to-all-start.13
  337.4 27.5 %all-to-all-done.13 = f32[16,16,2,1024]{3,1,2,0:T(8,128)} async-done(((f32[16,16,2,1024]{3,1,2,0:T(8,128)}), f32[16,16,2,1024]{3,1,2,0:T(8,128)}, u32[]{:S(2)}, u32[]{:S(2)}) %all-to-all-start.13) | async-done | bytes 2097184 | tf_op jit(solution)/shard_map/all_to_all | solution.py:22
  367.1 4.2 all-to-all-start.14
  375.4 11.9 %all-to-all-done.14 = f32[8,16,2,1024]{3,2,1,0:T(2,128)} async-done(((f32[8,16,2,1024]{3,2,1,0:T(2,128)}), f32[8,16,2,1024]{3,2,1,0:T(2,128)}, u32[]{:S(2)}, u32[]{:S(2)}) %all-to-all-start.14) | async-done | bytes 1048608 | tf_op jit(solution)/shard_map/all_to_all | solution.py:29
  389.6 4.5 all-to-all-start.19
  402.9 7.1 %all-to-all-done.19 = f32[8,16,2,1024]{3,2,1,0:T(2,128)} async-done(((f32[8,16,2,1024]{3,2,1,0:T(2,128)}), f32[8,16,2,1024]{3,2,1,0:T(2,128)}, u32[]{:S(2)}, u32[]{:S(2)}) %all-to-all-start.19) | async-done | bytes 1048608 | tf_op jit(solution)/shard_map/all_to_all | solution.py:29
  424.7 3.7 all-to-all-start.15
  432.8 13.2 %all-to-all-done.15 = f32[16,16,4,256]{3,1,2,0:T(8,128)S(1)} async-done(((f32[16,16,4,256]{3,1,2,0:T(8,128)}), f32[16,16,4,256]{3,1,2,0:T(8,128)S(1)}, u32[]{:S(2)}, u32[]{:S(2)}) %all-to-all-start.15) | async-done | bytes 1048608 | tf_op jit(solution)/shard_map/all_to_all | solution.py:29
  449.0 4.5 all-to-all-start.20
  457.0 12.7 %all-to-all-done.20 = f32[16,16,4,256]{3,1,2,0:T(8,128)} async-done(((f32[16,16,4,256]{3,1,2,0:T(8,128)}), f32[16,16,4,256]{3,1,2,0:T(8,128)}, u32[]{:S(2)}, u32[]{:S(2)}) %all-to-all-start.20) | async-done | bytes 1048608 | tf_op jit(solution)/shard_map/all_to_all | solution.py:29
  469.7 4.2 all-to-all-start.16
  477.5 12.4 %all-to-all-done.16 = f32[8,32,4,256]{3,1,2,0:T(8,128)} async-done(((f32[8,32,4,256]{3,1,2,0:T(8,128)}), f32[8,32,4,256]{3,1,2,0:T(8,128)}, u32[]{:S(2)}, u32[]{:S(2)}) %all-to-all-start.16) | async-done | bytes 1048608 | tf_op jit(solution)/shard_map/all_to_all | solution.py:22
  489.9 3.6 all-to-all-start.21
  499.4 10.0 %all-to-all-done.21 = f32[8,32,4,256]{3,1,2,0:T(8,128)S(1)} async-done(((f32[8,32,4,256]{3,1,2,0:T(8,128)}), f32[8,32,4,256]{3,1,2,0:T(8,128)S(1)}, u32[]{:S(2)}, u32[]{:S(2)}) %all-to-all-start.21) | async-done | bytes 1048608 | tf_op jit(solution)/shard_map/all_to_all | solution.py:22
  511.4 4.2 all-to-all-start.17
  518.9 12.7 %all-to-all-done.17 = f32[8,32,4,256]{3,1,2,0:T(8,128)} async-done(((f32[8,32,4,256]{3,1,2,0:T(8,128)}), f32[8,32,4,256]{3,1,2,0:T(8,128)}, u32[]{:S(2)}, u32[]{:S(2)}) %all-to-all-start.17) | async-done | bytes 1048608 | tf_op jit(solution)/shard_map/all_to_all | solution.py:29
  541.2 11.0 %all-to-all-done.22 = f32[8,32,4,256]{3,1,2,0:T(8,128)S(1)} async-done(((f32[8,32,4,256]{3,1,2,0:T(8,128)}), f32[8,32,4,256]{3,1,2,0:T(8,128)S(1)}, u32[]{:S(2)}, u32[]{:S(2)}) %all-to-all-start.22) | async-done | bytes 1048608 | tf_op jit(solution)/shard_map/all_to_all | solution.py:29
  552.2 4.7 all-to-all-start.18
  560.5 28.3 %all-to-all-done.18 = f32[16,16,4,512]{3,1,2,0:T(8,128)} async-done(((f32[16,16,4,512]{3,1,2,0:T(8,128)}), f32[16,16,4,512]{3,1,2,0:T(8,128)}, u32[]{:S(2)}, u32[]{:S(2)}) %all-to-all-start.18) | async-done | bytes 2097184 | tf_op jit(solution)/shard_map/all_to_all | solution.py:22
  588.8 4.5 all-to-all-start.23
  596.7 26.6 %all-to-all-done.23 = f32[16,16,4,512]{3,1,2,0:T(8,128)} async-done(((f32[16,16,4,512]{3,1,2,0:T(8,128)}), f32[16,16,4,512]{3,1,2,0:T(8,128)}, u32[]{:S(2)}, u32[]{:S(2)}) %all-to-all-start.23) | async-done | bytes 2097184 | tf_op jit(solution)/shard_map/all_to_all | solution.py:22
  (130 shorter events, 135.7 us)
Async XLA Ops:
  0.6 536.9 %copy-start = (f32[4,256,512]{2,1,0:T(8,128)S(1)}, f32[4,256,512]{2,1,0:T(8,128)}, u32[]{:S(2)}) copy-start(f32[4,256,512]{2,1,0:T(8,128)} %param.19) | copy-start | bytes 6291460
  23.3 19.4 %all-to-all-start.2 = ((f32[8,32,1024]{2,1,0:T(8,128)}), f32[8,32,1024]{2,1,0:T(8,128)S(1)}, u32[]{:S(2)}, u32[]{:S(2)}) async-start(f32[8,32,1024]{2,1,0:T(8,128)} %broadcast_in_dim.61), calls=%async_computation.2 | async-start | bytes 2097152 | tf_op jit(solution)/shard_map/all_to_all | solution.py:29
  42.7 39.4 %all-to-all-start.1 = ((f32[16,16,2048]{2,1,0:T(8,128)}), f32[16,16,2048]{2,1,0:T(8,128)}, u32[]{:S(2)}, u32[]{:S(2)}) async-start(f32[16,16,2048]{2,1,0:T(8,128)} %fusion.2), calls=%async_computation.1 | async-start | bytes 4194304 | tf_op jit(solution)/shard_map/all_to_all | solution.py:22
  82.1 33.8 %all-to-all-start.3 = ((f32[16,16,2048]{2,1,0:T(8,128)}), f32[16,16,2048]{2,1,0:T(8,128)}, u32[]{:S(2)}, u32[]{:S(2)}) async-start(f32[16,16,2048]{2,1,0:T(8,128)} %fusion), calls=%async_computation.3 | async-start | bytes 4194304 | tf_op jit(solution)/shard_map/all_to_all | solution.py:22
  117.0 19.4 %all-to-all-start.4 = ((f32[8,16,2048]{2,1,0:T(8,128)}), f32[8,16,2048]{2,1,0:T(8,128)S(1)}, u32[]{:S(2)}, u32[]{:S(2)}) async-start(f32[8,16,2048]{2,1,0:T(8,128)} %broadcast_in_dim.112), calls=%async_computation.4 | async-start | bytes 2097152 | tf_op jit(solution)/shard_map/all_to_all | solution.py:29
  122.3 19.5 %copy-start.10 = (s32[2,4]{1,0:T(2,128)S(1)}, s32[2,4]{1,0:T(2,128)}, u32[]{:S(2)}) copy-start(s32[2,4]{1,0:T(2,128)} %param.22) | copy-start | bytes 100
  137.6 20.2 %all-to-all-start.9 = ((f32[8,16,2048]{2,1,0:T(8,128)}), f32[8,16,2048]{2,1,0:T(8,128)}, u32[]{:S(2)}, u32[]{:S(2)}) async-start(f32[8,16,2048]{2,1,0:T(8,128)} %broadcast_in_dim.116), calls=%async_computation.9 | async-start | bytes 2097152 | tf_op jit(solution)/shard_map/all_to_all | solution.py:29
  165.8 5.7 copy-start.8
  166.9 22.3 %all-to-all-start.5 = ((f32[16,16,2,512]{3,1,2,0:T(8,128)}), f32[16,16,2,512]{3,1,2,0:T(8,128)}, u32[]{:S(2)}, u32[]{:S(2)}) async-start(f32[16,16,2,512]{3,1,2,0:T(8,128)} %broadcast_in_dim.114), calls=%async_computation.5 | async-start | bytes 2097152 | tf_op jit(solution)/shard_map/all_to_all | solution.py:29
  190.2 20.6 %all-to-all-start.10 = ((f32[16,16,2,512]{3,1,2,0:T(8,128)}), f32[16,16,2,512]{3,1,2,0:T(8,128)}, u32[]{:S(2)}, u32[]{:S(2)}) async-start(f32[16,16,2,512]{3,1,2,0:T(8,128)} %broadcast_in_dim.118), calls=%async_computation.10 | async-start | bytes 2097152 | tf_op jit(solution)/shard_map/all_to_all | solution.py:29
  194.6 1.9 copy-start.1
  210.9 20.2 %all-to-all-start.6 = ((f32[8,32,2,512]{3,1,2,0:T(8,128)}), f32[8,32,2,512]{3,1,2,0:T(8,128)}, u32[]{:S(2)}, u32[]{:S(2)}) async-start(f32[8,32,2,512]{3,1,2,0:T(8,128)} %copy.60), calls=%async_computation.6 | async-start | bytes 2097152 | tf_op jit(solution)/shard_map/all_to_all | solution.py:22
  215.1 1.9 copy-start.2
  231.1 20.2 %all-to-all-start.11 = ((f32[8,32,2,512]{3,1,2,0:T(8,128)}), f32[8,32,2,512]{3,1,2,0:T(8,128)}, u32[]{:S(2)}, u32[]{:S(2)}) async-start(f32[8,32,2,512]{3,1,2,0:T(8,128)} %copy.70), calls=%async_computation.11 | async-start | bytes 2097152 | tf_op jit(solution)/shard_map/all_to_all | solution.py:22
  252.4 4.4 copy-start.7
  252.4 20.3 %all-to-all-start.7 = ((f32[8,32,2,512]{3,1,2,0:T(8,128)}), f32[8,32,2,512]{3,1,2,0:T(8,128)}, u32[]{:S(2)}, u32[]{:S(2)}) async-start(f32[8,32,2,512]{3,1,2,0:T(8,128)} %broadcast_in_dim.115), calls=%async_computation.7 | async-start | bytes 2097152 | tf_op jit(solution)/shard_map/all_to_all | solution.py:29
  273.9 20.2 %all-to-all-start.12 = ((f32[8,32,2,512]{3,1,2,0:T(8,128)}), f32[8,32,2,512]{3,1,2,0:T(8,128)}, u32[]{:S(2)}, u32[]{:S(2)}) async-start(f32[8,32,2,512]{3,1,2,0:T(8,128)} %broadcast_in_dim.119), calls=%async_computation.12 | async-start | bytes 2097152 | tf_op jit(solution)/shard_map/all_to_all | solution.py:29
  294.1 36.4 %all-to-all-start.8 = ((f32[16,16,2,1024]{3,1,2,0:T(8,128)}), f32[16,16,2,1024]{3,1,2,0:T(8,128)}, u32[]{:S(2)}, u32[]{:S(2)}) async-start(f32[16,16,2,1024]{3,1,2,0:T(8,128)} %copy.62), calls=%async_computation.8 | async-start | bytes 4194304 | tf_op jit(solution)/shard_map/all_to_all | solution.py:22
  330.5 34.4 %all-to-all-start.13 = ((f32[16,16,2,1024]{3,1,2,0:T(8,128)}), f32[16,16,2,1024]{3,1,2,0:T(8,128)}, u32[]{:S(2)}, u32[]{:S(2)}) async-start(f32[16,16,2,1024]{3,1,2,0:T(8,128)} %copy.72), calls=%async_computation.13 | async-start | bytes 4194304 | tf_op jit(solution)/shard_map/all_to_all | solution.py:22
  367.1 20.2 %all-to-all-start.14 = ((f32[8,16,2,1024]{3,2,1,0:T(2,128)}), f32[8,16,2,1024]{3,2,1,0:T(2,128)}, u32[]{:S(2)}, u32[]{:S(2)}) async-start(f32[8,16,2,1024]{3,2,1,0:T(2,128)} %broadcast_in_dim.120), calls=%async_computation.14 | async-start | bytes 2097152 | tf_op jit(solution)/shard_map/all_to_all | solution.py:29
  373.7 20.3 %copy-start.9 = (s32[4,2]{0,1:T(2,128)S(1)}, s32[4,2]{0,1:T(2,128)}, u32[]{:S(2)}) copy-start(s32[4,2]{0,1:T(2,128)} %param.23) | copy-start | bytes 100
  389.6 20.4 %all-to-all-start.19 = ((f32[8,16,2,1024]{3,2,1,0:T(2,128)}), f32[8,16,2,1024]{3,2,1,0:T(2,128)}, u32[]{:S(2)}, u32[]{:S(2)}) async-start(f32[8,16,2,1024]{3,2,1,0:T(2,128)} %broadcast_in_dim.124), calls=%async_computation.19 | async-start | bytes 2097152 | tf_op jit(solution)/shard_map/all_to_all | solution.py:29
  399.4 1.9 copy-start.3
  424.7 21.4 %all-to-all-start.15 = ((f32[16,16,4,256]{3,1,2,0:T(8,128)}), f32[16,16,4,256]{3,1,2,0:T(8,128)S(1)}, u32[]{:S(2)}, u32[]{:S(2)}) async-start(f32[16,16,4,256]{3,1,2,0:T(8,128)} %broadcast_in_dim.122), calls=%async_computation.15 | async-start | bytes 2097152 | tf_op jit(solution)/shard_map/all_to_all | solution.py:29
  446.0 1.0 copy-start.5
  449.0 5.8 copy-start.4
  449.0 20.8 %all-to-all-start.20 = ((f32[16,16,4,256]{3,1,2,0:T(8,128)}), f32[16,16,4,256]{3,1,2,0:T(8,128)}, u32[]{:S(2)}, u32[]{:S(2)}) async-start(f32[16,16,4,256]{3,1,2,0:T(8,128)} %broadcast_in_dim.126), calls=%async_computation.20 | async-start | bytes 2097152 | tf_op jit(solution)/shard_map/all_to_all | solution.py:29
  469.7 20.2 %all-to-all-start.16 = ((f32[8,32,4,256]{3,1,2,0:T(8,128)}), f32[8,32,4,256]{3,1,2,0:T(8,128)}, u32[]{:S(2)}, u32[]{:S(2)}) async-start(f32[8,32,4,256]{3,1,2,0:T(8,128)} %copy.83), calls=%async_computation.16 | async-start | bytes 2097152 | tf_op jit(solution)/shard_map/all_to_all | solution.py:22
  489.9 19.4 %all-to-all-start.21 = ((f32[8,32,4,256]{3,1,2,0:T(8,128)}), f32[8,32,4,256]{3,1,2,0:T(8,128)S(1)}, u32[]{:S(2)}, u32[]{:S(2)}) async-start(f32[8,32,4,256]{3,1,2,0:T(8,128)} %copy.95), calls=%async_computation.21 | async-start | bytes 2097152 | tf_op jit(solution)/shard_map/all_to_all | solution.py:22
  511.4 20.2 %all-to-all-start.17 = ((f32[8,32,4,256]{3,1,2,0:T(8,128)}), f32[8,32,4,256]{3,1,2,0:T(8,128)}, u32[]{:S(2)}, u32[]{:S(2)}) async-start(f32[8,32,4,256]{3,1,2,0:T(8,128)} %broadcast_in_dim.123), calls=%async_computation.17 | async-start | bytes 2097152 | tf_op jit(solution)/shard_map/all_to_all | solution.py:29
  532.7 19.4 %all-to-all-start.22 = ((f32[8,32,4,256]{3,1,2,0:T(8,128)}), f32[8,32,4,256]{3,1,2,0:T(8,128)S(1)}, u32[]{:S(2)}, u32[]{:S(2)}) async-start(f32[8,32,4,256]{3,1,2,0:T(8,128)} %broadcast_in_dim.127), calls=%async_computation.22 | async-start | bytes 2097152 | tf_op jit(solution)/shard_map/all_to_all | solution.py:29
  552.2 36.7 %all-to-all-start.18 = ((f32[16,16,4,512]{3,1,2,0:T(8,128)}), f32[16,16,4,512]{3,1,2,0:T(8,128)}, u32[]{:S(2)}, u32[]{:S(2)}) async-start(f32[16,16,4,512]{3,1,2,0:T(8,128)} %copy.85), calls=%async_computation.18 | async-start | bytes 4194304 | tf_op jit(solution)/shard_map/all_to_all | solution.py:22
  560.5 33.5 %copy-start.6 = (f32[16,2,1024]{2,0,1:T(8,128)S(1)}, f32[16,2,1024]{2,0,1:T(8,128)}, u32[]{:S(2)}) copy-start(f32[16,2,1024]{2,0,1:T(8,128)} %reduce_sum.95) | copy-start | bytes 393220
  588.8 34.4 %all-to-all-start.23 = ((f32[16,16,4,512]{3,1,2,0:T(8,128)}), f32[16,16,4,512]{3,1,2,0:T(8,128)}, u32[]{:S(2)}, u32[]{:S(2)}) async-start(f32[16,16,4,512]{3,1,2,0:T(8,128)} %copy.97), calls=%async_computation.23 | async-start | bytes 4194304 | tf_op jit(solution)/shard_map/all_to_all | solution.py:22

commit v3 on v1

--- a/solution.py
+++ b/solution.py
@@ -41,6 +41,25 @@
     return exchange_sum(matmul(right_side, inverse, "ski,kij->skj"), "wide")
 
 
+def send_blocks(tiles, owner, local):
+    here = lax.axis_index("col")
+    picked = jnp.take(tiles, local, axis=0)
+    outgoing = jnp.where((owner == here)[:, :, None, None], picked, 0.0)
+    return lax.all_to_all(outgoing, "col", 0, 0, tiled=False).sum(0)
+
+
+def slots_of(blocks, per_device):
+    rows = blocks.shape[0]
+    n_col = blocks.shape[1] // per_device
+    return blocks.reshape(rows, n_col, per_device).transpose(1, 0, 2).reshape(n_col, rows * per_device)
+
+
+def rows_of(received, rows, per_device):
+    samples = received.shape[1]
+    shaped = received.reshape(rows, per_device, samples, BLK).transpose(2, 0, 1, 3)
+    return shaped.reshape(samples, rows, per_device * BLK)
+
+
 def per_device(
     z_root,
     z_child,
@@ -53,14 +72,34 @@
     anc_child,
     anc_grand,
 ):
+    n_col = lax.axis_size("col")
     root_right = exchange_gather(z_root, "col", 0)
     x_root = exchange_sum(matmul(root_right, inv_root, "si,ij->sj"), "wide")
-    root_rows = exchange_gather(x_root, "col", 1)
-    near_rows = exchange_gather(pick_blocks(root_rows, anc_child), "wide", 0)
+    samples, width = x_root.shape
+    root_tiles = x_root.reshape(samples, width // BLK, BLK).transpose(1, 0, 2)
+    per_root = width // BLK
+
+    child_slots = slots_of(anc_child, anc_child.shape[1] // n_col)
+    near_local = send_blocks(root_tiles, child_slots // per_root, child_slots % per_root)
+    near_local = rows_of(near_local, anc_child.shape[0], anc_child.shape[1] // n_col)
+    near_rows = exchange_gather(near_local, "wide", 0)
     x_child = level(z_child, matmul(near_rows, panel_child, "ska,kaj->skj"), inv_child)
-    child_rows = exchange_gather(x_child, "col", 2)
-    solved_all = jnp.concatenate([root_rows, child_rows.reshape(child_rows.shape[0], -1)], axis=1)
-    far_rows = exchange_gather(pick_blocks(solved_all, anc_grand), "wide", 0)
+
+    kids, child_width = x_child.shape[1], x_child.shape[2]
+    per_child = child_width // BLK
+    child_tiles = x_child.reshape(samples, kids * per_child, BLK).transpose(1, 0, 2)
+    all_tiles = jnp.concatenate([root_tiles, child_tiles], axis=0)
+    grand_slots = slots_of(anc_grand, anc_grand.shape[1] // n_col)
+    root_blocks = per_root * n_col
+    is_root = grand_slots < root_blocks
+    in_child = grand_slots - root_blocks
+    child_block = in_child % (per_child * n_col)
+    child_kid = in_child // (per_child * n_col)
+    owner = jnp.where(is_root, grand_slots // per_root, child_block // per_child)
+    local = jnp.where(is_root, grand_slots % per_root, per_root + child_kid * per_child + child_block % per_child)
+    far_local = send_blocks(all_tiles, owner, local)
+    far_local = rows_of(far_local, anc_grand.shape[0], anc_grand.shape[1] // n_col)
+    far_rows = exchange_gather(far_local, "wide", 0)
     x_grand = level(z_grand, matmul(far_rows, panel_grand, "sga,gaj->sgj"), inv_grand)
     return (x_root, x_child, x_grand)
 
@@ -75,8 +114,8 @@
         P(None, "wide", "col"),
         P(None, "col", "wide"),
         P(None, "col", "wide"),
-        P(None, "col"),
-        P(None, "col"),
+        P(None, None),
+        P(None, None),
     )
     out_specs = (P("wide", "col"), P("wide", None, "col"), P("wide", None, "col"))
     return jax.shard_map(

time: 533 us -> 511 us (0.959)
  blocking collectives: 382 us -> 327 us
  waiting for transfers between devices: 53.9 us -> 106 us
  local copies, waits for them, and re-layouts: 40.3 us -> 16.3 us
    all_to_all x5 -> x3, blocking collectives: 228 us -> 116 us  [exchange_sum(): lax.all_to_all(partial.reshape((n, chunk) + partial.shape[1:]), axis, 0,...]
    all_to_all x2, waiting for transfers between devices: 53.9 us -> 106 us  [exchange_sum(): lax.all_to_all(partial.reshape((n, chunk) + partial.shape[1:]), axis, 0,...]
    all_to_all x0 -> x2, blocking collectives: none -> 37.3 us  [send_blocks(): return lax.all_to_all(outgoing, 'col', 0, 0, tiled=False).sum(0)]
    unnamed x0 -> x2, blocking collectives: none -> 17.6 us
    transpose x2 -> x3, local copies, waits for them, and re-layouts: 8.23 us -> 0.2 us  [the longest x2 0.18 us: slots_of(): blocks.reshape(rows, n_col, per_device).transpose(1, 0, 2)]
    another operation x2 -> x0, local copies, waits for them, and re-layouts: 6.86 us -> none  [pick_blocks(): tiled = source_rows.reshape(leading, source_rows.shape[1] // BLK, BLK)]
    concatenate x2 -> x0, local copies, waits for them, and re-layouts: 5.69 us -> none  [per_device(): jnp.concatenate([root_rows, child_rows.reshape(child_rows.shape[0], -1)],...]
where the time goes in v3:
time: 511 us; the launch traced here: 510 us
  blocking collectives  327 us (64%)
  waiting for transfers between devices  106 us (21%)
  matrix products  33.5 us (7%)
  local copies, waits for them, and re-layouts  16.3 us (3%)
  other arithmetic  13.2 us (3%)
  starting transfers between devices  12.9 us (3%)
    all_to_all x5, blocking collectives, exchange_gather(): parts = lax.all_to_all(stacked, axis, 0, 0, tiled=False)  157 us
    all_to_all x3, blocking collectives, exchange_sum(): lax.all_to_all(partial.reshape((n, chunk) + partial.shape[1:]), axis, 0,...  116 us
    all_to_all x2, waiting for transfers between devices, exchange_sum(): lax.all_to_all(partial.reshape((n, chunk) + partial.shape[1:]), axis, 0,...  106 us
    all_to_all x2, blocking collectives, send_blocks(): return lax.all_to_all(outgoing, 'col', 0, 0, tiled=False).sum(0)  37.3 us
    dot_general x5, matrix products, matmul(): jnp.einsum(spec, lhs, rhs, precision=PRECISE, preferred_element_type=jnp....  33.5 us
    unnamed x2, blocking collectives  17.6 us
    all_to_all x2, starting transfers between devices, exchange_sum(): lax.all_to_all(partial.reshape((n, chunk) + partial.shape[1:]), axis, 0,...  12.9 us
    reduce_sum x5, other arithmetic, exchange_sum(): return parts.sum(0)  11.2 us
  transfers between devices with their start and end apart: 2, of which 2 were waited for; matrix products, arithmetic and copies ran while one was open for 0% of the time, Pallas kernels for 0%

profile of v3, /device:TPU:0, one launch (start us, length us, event | category | flops | bytes accessed | tf_op | source)
XLA Modules:
  0.0 510.4 jit_solution(5573019050314918849)
XLA Ops:
  0.6 1.3 broadcast_in_dim.70
  2.0 31.5 %all_to_all.60 = f32[8,64,1024]{2,1,0:T(8,128)S(1)} all-to-all(f32[8,64,1024]{2,1,0:T(8,128)S(1)} %broadcast_in_dim.70), channel_id=1, replica_groups=mesh['wide'=16,'col'=8] {'col'}, dimensions={0} | all-to-all | bytes 4194304 | tf_op jit(solution)/shard_map/all_to_all | solution.py:29
  33.5 17.3 %fusion = f32[16,32,2048]{2,1,0:T(8,128)} fusion(f32[16,32,1024]{2,1,0:T(8,128)S(1)} %bitcast.82, f32[1024,2048]{1,0:T(8,128)} %param.13), kind=kOutput, calls=%fused_computation.2 | convolution fusion | flops 12884901888 | bytes 14680064 | tf_op jit(solution)/shard_map/si,ij->sj/dot_general | solution.py:35
  50.9 8.4 %all-to-all-start.1 = ((f32[16,32,2048]{2,1,0:T(8,128)}), f32[16,32,2048]{2,1,0:T(8,128)}, u32[]{:S(2)}, u32[]{:S(2)}) async-start(f32[16,32,2048]{2,1,0:T(8,128)} %fusion), calls=%async_computation.1 | async-start | bytes 8388608 | tf_op jit(solution)/shard_map/all_to_all | solution.py:22
  59.3 8.9 %all-gather.2 = s32[8,4,2]{1,2,0:T(2,128)S(1)} all-gather(s32[1,4,2]{1,2,0:T(2,128)S(1)} %bitcast.103), channel_id=2, replica_groups=mesh['wide'=16,'col'=8] {'col'}, dimensions={0}, use_global_device_ids=true | all-gather | bytes 288 | tf_op args[8]
  68.6 8.7 %all-gather.3 = s32[8,2,4]{2,1,0:T(2,128)S(1)} all-gather(s32[1,2,4]{2,1,0:T(2,128)S(1)} %bitcast.104), channel_id=3, replica_groups=mesh['wide'=16,'col'=8] {'col'}, dimensions={0}, use_global_device_ids=true | all-gather | bytes 288 | tf_op args[9]
  77.6 43.7 %all-to-all-done.1 = f32[16,32,2048]{2,1,0:T(8,128)} async-done(((f32[16,32,2048]{2,1,0:T(8,128)}), f32[16,32,2048]{2,1,0:T(8,128)}, u32[]{:S(2)}, u32[]{:S(2)}) %all-to-all-start.1) | async-done | bytes 4194336 | tf_op jit(solution)/shard_map/all_to_all | solution.py:22
  121.3 2.4 reduce_sum.63
  123.8 0.7 copy-done.4
  124.5 0.6 gather_fusion
  125.3 18.8 %all_to_all.61 = f32[8,8,32,128]{3,2,1,0:T(8,128)S(1)} all-to-all(f32[8,8,32,128]{3,2,1,0:T(8,128)S(1)} %select_select_fusion.1), channel_id=1, replica_groups=mesh['wide'=16,'col'=8] {'col'}, dimensions={0} | all-to-all | bytes 2097152 | tf_op jit(solution)/shard_map/all_to_all | solution.py:48
  144.2 0.3 broadcast_in_dim.76
  144.5 32.7 %all_to_all.62 = f32[16,32,2,512]{3,1,2,0:T(8,128)S(1)} all-to-all(f32[16,32,2,512]{3,1,2,0:T(8,128)S(1)} %broadcast_in_dim.76), channel_id=1, replica_groups=mesh['wide'=16,'col'=8] {'wide'}, dimensions={0} | all-to-all | bytes 4194304 | tf_op jit(solution)/shard_map/all_to_all | solution.py:29
  177.2 0.2 copy.64
  177.4 1.4 copy-done.2
  178.7 3.5 fusion.27
  182.3 0.2 copy.65
  182.5 30.8 %all_to_all.63 = f32[8,64,2,512]{3,1,2,0:T(8,128)} all-to-all(f32[8,64,2,512]{3,1,2,0:T(8,128)S(1)} %copy.65), channel_id=1, replica_groups=mesh['wide'=16,'col'=8] {'col'}, dimensions={0} | all-to-all | bytes 4194304 | tf_op jit(solution)/shard_map/all_to_all | solution.py:22
  213.3 1.9 reduce_sum.65
  215.3 0.3 broadcast_in_dim.77
  215.5 30.0 %all_to_all.64 = f32[8,64,2,512]{3,1,2,0:T(8,128)S(1)} all-to-all(f32[8,64,2,512]{3,1,2,0:T(8,128)S(1)} %broadcast_in_dim.77), channel_id=1, replica_groups=mesh['wide'=16,'col'=8] {'col'}, dimensions={0} | all-to-all | bytes 4194304 | tf_op jit(solution)/shard_map/all_to_all | solution.py:29
  245.5 0.2 copy.68
  245.7 2.0 copy-done.1
  247.7 7.0 %fusion.28 = f32[2,512,1024]{2,1,0:T(8,128)S(1)} fusion(f32[512,2,512]{2,0,1:T(8,128)S(1)} %bitcast.85, f32[2,512,1024]{2,1,0:T(8,128)S(1)} %copy-done.1), kind=kOutput, calls=%fused_computation.88 | convolution fusion | flops 6442450944 | bytes 10485760 | tf_op jit(solution)/shard_map/ski,kij->skj/dot_general | solution.py:35
  254.7 2.3 copy.69
  257.0 4.5 all-to-all-start.6
  261.9 62.5 %all-to-all-done.6 = f32[16,32,2,1024]{3,1,2,0:T(8,128)} async-done(((f32[16,32,2,1024]{3,1,2,0:T(8,128)}), f32[16,32,2,1024]{3,1,2,0:T(8,128)}, u32[]{:S(2)}, u32[]{:S(2)}) %all-to-all-start.6) | async-done | bytes 4194336 | tf_op jit(solution)/shard_map/all_to_all | solution.py:22
  324.4 2.5 reduce_sum.66
  326.9 0.2 copy.86
  327.2 0.2 reshape.432
  327.5 1.6 gather_fusion.1
  329.1 1.4 select_select_fusion
  330.6 18.5 %all_to_all.65 = f32[8,8,32,128]{3,2,1,0:T(8,128)S(1)} all-to-all(f32[8,8,32,128]{3,2,1,0:T(8,128)S(1)} %select_select_fusion), channel_id=1, replica_groups=mesh['wide'=16,'col'=8] {'col'}, dimensions={0} | all-to-all | bytes 2097152 | tf_op jit(solution)/shard_map/all_to_all | solution.py:48
  349.2 0.2 broadcast_in_dim.81
  349.4 32.5 %all_to_all.66 = f32[16,32,4,256]{3,1,2,0:T(8,128)S(1)} all-to-all(f32[16,32,4,256]{3,1,2,0:T(8,128)S(1)} %broadcast_in_dim.81), channel_id=1, replica_groups=mesh['wide'=16,'col'=8] {'wide'}, dimensions={0} | all-to-all | bytes 4194304 | tf_op jit(solution)/shard_map/all_to_all | solution.py:29
  381.9 0.2 copy.79
  382.2 1.0 copy-done.3
  383.2 2.0 fusion.29
  385.2 0.2 copy.80
  385.4 30.7 %all_to_all.67 = f32[8,64,4,256]{3,1,2,0:T(8,128)} all-to-all(f32[8,64,4,256]{3,1,2,0:T(8,128)S(1)} %copy.80), channel_id=1, replica_groups=mesh['wide'=16,'col'=8] {'col'}, dimensions={0} | all-to-all | bytes 4194304 | tf_op jit(solution)/shard_map/all_to_all | solution.py:22
  416.1 1.8 reduce_sum.68
  418.0 0.2 broadcast_in_dim.82
  418.2 30.0 %all_to_all.68 = f32[8,64,4,256]{3,1,2,0:T(8,128)S(1)} all-to-all(f32[8,64,4,256]{3,1,2,0:T(8,128)S(1)} %broadcast_in_dim.82), channel_id=1, replica_groups=mesh['wide'=16,'col'=8] {'col'}, dimensions={0} | all-to-all | bytes 4194304 | tf_op jit(solution)/shard_map/all_to_all | solution.py:29
  448.3 3.6 fusion.30
  451.9 0.8 copy.84
  452.8 54.1 %all_to_all.69 = f32[16,32,4,512]{3,1,2,0:T(8,128)} all-to-all(f32[16,32,4,512]{3,1,2,0:T(8,128)S(1)} %copy.84), channel_id=1, replica_groups=mesh['wide'=16,'col'=8] {'wide'}, dimensions={0} | all-to-all | bytes 8388608 | tf_op jit(solution)/shard_map/all_to_all | solution.py:22
  506.9 2.6 reduce_sum.69
  509.5 0.9 copy.87
  (45 shorter events, 1.9 us)
Async XLA Ops:
  0.6 447.7 %copy-start = (f32[4,256,512]{2,1,0:T(8,128)S(1)}, f32[4,256,512]{2,1,0:T(8,128)}, u32[]{:S(2)}) copy-start(f32[4,256,512]{2,1,0:T(8,128)} %param.15) | copy-start | bytes 6291460
  50.9 8.4 %copy-start.8 = (s32[2,4]{1,0:T(2,128)S(1)}, s32[2,4]{1,0:T(2,128)}, u32[]{:S(2)}) copy-start(s32[2,4]{1,0:T(2,128)} %param.18) | copy-start | bytes 100
  50.9 17.7 %copy-start.9 = (s32[4,2]{0,1:T(2,128)S(1)}, s32[4,2]{0,1:T(2,128)}, u32[]{:S(2)}) copy-start(s32[4,2]{0,1:T(2,128)} %param.19) | copy-start | bytes 100
  50.9 70.5 %all-to-all-start.1 = ((f32[16,32,2048]{2,1,0:T(8,128)}), f32[16,32,2048]{2,1,0:T(8,128)}, u32[]{:S(2)}, u32[]{:S(2)}) async-start(f32[16,32,2048]{2,1,0:T(8,128)} %fusion), calls=%async_computation.1 | async-start | bytes 8388608 | tf_op jit(solution)/shard_map/all_to_all | solution.py:22
  123.7 0.7 copy-start.4
  177.2 1.6 copy-start.2
  213.3 1.9 copy-start.6
  245.5 2.2 copy-start.1
  257.0 67.4 %all-to-all-start.6 = ((f32[16,32,2,1024]{3,1,2,0:T(8,128)}), f32[16,32,2,1024]{3,1,2,0:T(8,128)}, u32[]{:S(2)}, u32[]{:S(2)}) async-start(f32[16,32,2,1024]{3,1,2,0:T(8,128)} %copy.69), calls=%async_computation.6 | async-start | bytes 8388608 | tf_op jit(solution)/shard_map/all_to_all | solution.py:22
  327.1 2.0 copy-start.5
  381.9 1.2 copy-start.3
  416.1 1.8 copy-start.7

commit v4 on v3

--- a/solution.py
+++ b/solution.py
@@ -6,7 +6,7 @@
 BLK = 128
 
 
-PRECISE = lax.Precision.HIGHEST
+PRECISE = lax.Precision.HIGH
 
 
 def pick_blocks(source_rows, blocks):
@@ -73,7 +73,14 @@
     anc_grand,
 ):
     n_col = lax.axis_size("col")
-    root_right = exchange_gather(z_root, "col", 0)
+    lists = jnp.concatenate([anc_child.reshape(-1), anc_grand.reshape(-1)]).astype(jnp.float32)
+    extra = jnp.zeros((1, z_root.shape[1]), jnp.float32).at[0, : lists.shape[0]].set(lists)
+    stacked = exchange_gather(jnp.concatenate([z_root, extra], axis=0)[None], "col", 0)
+    root_right = stacked[:, :-1].reshape(-1, z_root.shape[1])
+    got = stacked[:, -1, : lists.shape[0]].astype(jnp.int32)
+    split = anc_child.size
+    anc_child = got[:, :split].reshape((n_col,) + anc_child.shape).transpose(1, 0, 2).reshape(anc_child.shape[0], -1)
+    anc_grand = got[:, split:].reshape((n_col,) + anc_grand.shape).transpose(1, 0, 2).reshape(anc_grand.shape[0], -1)
     x_root = exchange_sum(matmul(root_right, inv_root, "si,ij->sj"), "wide")
     samples, width = x_root.shape
     root_tiles = x_root.reshape(samples, width // BLK, BLK).transpose(1, 0, 2)
@@ -114,8 +121,8 @@
         P(None, "wide", "col"),
         P(None, "col", "wide"),
         P(None, "col", "wide"),
-        P(None, None),
-        P(None, None),
+        P(None, "col"),
+        P(None, "col"),
     )
     out_specs = (P("wide", "col"), P("wide", None, "col"), P("wide", None, "col"))
     return jax.shard_map(

time: 511 us -> 503 us (0.984)
  waiting for transfers between devices: 106 us -> 125 us
  blocking collectives: 327 us -> 310 us
  matrix products: 33.5 us -> 17.3 us
    all_to_all x2, waiting for transfers between devices: 106 us -> 125 us  [exchange_sum(): lax.all_to_all(partial.reshape((n, chunk) + partial.shape[1:]), axis, 0,...]
    unnamed x2 -> x0, blocking collectives: 17.6 us -> none
    dot_general x5, matrix products: 33.5 us -> 17.3 us  [matmul(): jnp.einsum(spec, lhs, rhs, precision=PRECISE, preferred_element_type=jnp....]
where the time goes in v4:
time: 503 us; the launch traced here: 502 us
  blocking collectives  310 us (62%)
  waiting for transfers between devices  125 us (25%)
  local copies, waits for them, and re-layouts  20.2 us (4%)
  matrix products  17.3 us (3%)
  other arithmetic  16.3 us (3%)
  starting transfers between devices  12.6 us (3%)
    all_to_all x5, blocking collectives, exchange_gather(): parts = lax.all_to_all(stacked, axis, 0, 0, tiled=False)  157 us
    all_to_all x2, waiting for transfers between devices, exchange_sum(): lax.all_to_all(partial.reshape((n, chunk) + partial.shape[1:]), axis, 0,...  125 us
    all_to_all x3, blocking collectives, exchange_sum(): lax.all_to_all(partial.reshape((n, chunk) + partial.shape[1:]), axis, 0,...  115 us
    all_to_all x2, blocking collectives, send_blocks(): return lax.all_to_all(outgoing, 'col', 0, 0, tiled=False).sum(0)  37 us
    dot_general x5, matrix products, matmul(): jnp.einsum(spec, lhs, rhs, precision=PRECISE, preferred_element_type=jnp....  17.3 us
    all_to_all x2, starting transfers between devices, exchange_sum(): lax.all_to_all(partial.reshape((n, chunk) + partial.shape[1:]), axis, 0,...  12.6 us
    reduce_sum x5, other arithmetic, exchange_sum(): return parts.sum(0)  11.2 us
  transfers between devices with their start and end apart: 2, of which 2 were waited for; matrix products, arithmetic and copies ran while one was open for 0% of the time, Pallas kernels for 0%

profile of v4, /device:TPU:0, one launch (start us, length us, event | category | flops | bytes accessed | tf_op | source)
XLA Modules:
  0.0 502.5 jit_solution(16168309087138312565)
XLA Ops:
  0.6 0.6 compare_reduce_fusion
  1.3 0.8 concatenate.20
  2.0 0.8 copy.53
  2.9 0.7 broadcast_select_fusion
  3.6 1.0 select_maximum_fusion
  4.6 1.1 broadcast_in_dim.74
  5.7 32.3 %all_to_all.60 = f32[8,1,65,1024]{3,1,2,0:T(1,128)S(1)} all-to-all(f32[8,1,65,1024]{3,1,2,0:T(1,128)S(1)} %broadcast_in_dim.74), channel_id=1, replica_groups=mesh['wide'=16,'col'=8] {'col'}, dimensions={0} | all-to-all | bytes 4259840 | tf_op jit(solution)/shard_map/all_to_all | solution.py:29
  38.0 0.5 copy.91
  38.5 0.2 slice.36
  38.8 1.1 copy-done.1
  39.9 1.2 copy.55
  41.1 8.7 %fusion = f32[16,32,2048]{2,1,0:T(8,128)} fusion(f32[16,32,1024]{2,1,0:T(8,128)S(1)} %bitcast.66, f32[1024,2048]{1,0:T(8,128)S(1)} %bitcast.65), kind=kOutput, calls=%fused_computation.2 | convolution fusion | flops 6442450944 | bytes 14680064 | tf_op jit(solution)/shard_map/si,ij->sj/dot_general | solution.py:35
  49.9 8.1 %all-to-all-start.1 = ((f32[16,32,2048]{2,1,0:T(8,128)}), f32[16,32,2048]{2,1,0:T(8,128)}, u32[]{:S(2)}, u32[]{:S(2)}) async-start(f32[16,32,2048]{2,1,0:T(8,128)} %fusion), calls=%async_computation.1 | async-start | bytes 8388608 | tf_op jit(solution)/shard_map/all_to_all | solution.py:22
  58.0 0.7 fusion.9
  59.0 62.4 %all-to-all-done.1 = f32[16,32,2048]{2,1,0:T(8,128)} async-done(((f32[16,32,2048]{2,1,0:T(8,128)}), f32[16,32,2048]{2,1,0:T(8,128)}, u32[]{:S(2)}, u32[]{:S(2)}) %all-to-all-start.1) | async-done | bytes 4194336 | tf_op jit(solution)/shard_map/all_to_all | solution.py:22
  121.3 2.4 reduce_sum.63
  123.8 0.7 copy-done.5
  124.5 0.6 gather_fusion
  125.4 18.5 %all_to_all.61 = f32[8,8,32,128]{3,2,1,0:T(8,128)S(1)} all-to-all(f32[8,8,32,128]{3,2,1,0:T(8,128)S(1)} %select_select_fusion.1), channel_id=1, replica_groups=mesh['wide'=16,'col'=8] {'col'}, dimensions={0} | all-to-all | bytes 2097152 | tf_op jit(solution)/shard_map/all_to_all | solution.py:48
  144.0 0.3 broadcast_in_dim.81
  144.2 32.7 %all_to_all.62 = f32[16,32,2,512]{3,1,2,0:T(8,128)S(1)} all-to-all(f32[16,32,2,512]{3,1,2,0:T(8,128)S(1)} %broadcast_in_dim.81), channel_id=1, replica_groups=mesh['wide'=16,'col'=8] {'wide'}, dimensions={0} | all-to-all | bytes 4194304 | tf_op jit(solution)/shard_map/all_to_all | solution.py:29
  177.2 1.4 copy-done.3
  178.5 2.0 fusion.17
  180.7 30.7 %all_to_all.63 = f32[8,64,2,512]{3,1,2,0:T(8,128)} all-to-all(f32[8,64,2,512]{3,1,2,0:T(8,128)S(1)} %copy.59), channel_id=1, replica_groups=mesh['wide'=16,'col'=8] {'col'}, dimensions={0} | all-to-all | bytes 4194304 | tf_op jit(solution)/shard_map/all_to_all | solution.py:22
  211.4 1.9 reduce_sum.65
  213.3 0.3 broadcast_in_dim.82
  213.6 30.0 %all_to_all.64 = f32[8,64,2,512]{3,1,2,0:T(8,128)S(1)} all-to-all(f32[8,64,2,512]{3,1,2,0:T(8,128)S(1)} %broadcast_in_dim.82), channel_id=1, replica_groups=mesh['wide'=16,'col'=8] {'col'}, dimensions={0} | all-to-all | bytes 4194304 | tf_op jit(solution)/shard_map/all_to_all | solution.py:29
  243.8 2.0 copy-done.2
  245.7 3.6 fusion.18
  249.3 2.6 copy.63
  251.9 4.5 all-to-all-start.6
  256.5 62.8 %all-to-all-done.6 = f32[16,32,2,1024]{3,1,2,0:T(8,128)} async-done(((f32[16,32,2,1024]{3,1,2,0:T(8,128)}), f32[16,32,2,1024]{3,1,2,0:T(8,128)}, u32[]{:S(2)}, u32[]{:S(2)}) %all-to-all-start.6) | async-done | bytes 4194336 | tf_op jit(solution)/shard_map/all_to_all | solution.py:22
  319.3 2.5 reduce_sum.66
  322.4 1.6 gather_fusion.1
  324.0 1.4 select_select_fusion
  325.5 18.5 %all_to_all.65 = f32[8,8,32,128]{3,2,1,0:T(8,128)S(1)} all-to-all(f32[8,8,32,128]{3,2,1,0:T(8,128)S(1)} %select_select_fusion), channel_id=1, replica_groups=mesh['wide'=16,'col'=8] {'col'}, dimensions={0} | all-to-all | bytes 2097152 | tf_op jit(solution)/shard_map/all_to_all | solution.py:48
  344.1 0.2 broadcast_in_dim.87
  344.3 32.4 %all_to_all.66 = f32[16,32,4,256]{3,1,2,0:T(8,128)S(1)} all-to-all(f32[16,32,4,256]{3,1,2,0:T(8,128)S(1)} %broadcast_in_dim.87), channel_id=1, replica_groups=mesh['wide'=16,'col'=8] {'wide'}, dimensions={0} | all-to-all | bytes 4194304 | tf_op jit(solution)/shard_map/all_to_all | solution.py:29
  376.9 1.0 copy-done.4
  377.9 1.1 fusion.19
  379.2 30.7 %all_to_all.67 = f32[8,64,4,256]{3,1,2,0:T(8,128)} all-to-all(f32[8,64,4,256]{3,1,2,0:T(8,128)S(1)} %copy.69), channel_id=1, replica_groups=mesh['wide'=16,'col'=8] {'col'}, dimensions={0} | all-to-all | bytes 4194304 | tf_op jit(solution)/shard_map/all_to_all | solution.py:22
  409.9 1.8 reduce_sum.68
  412.0 30.0 %all_to_all.68 = f32[8,64,4,256]{3,1,2,0:T(8,128)S(1)} all-to-all(f32[8,64,4,256]{3,1,2,0:T(8,128)S(1)} %broadcast_in_dim.88), channel_id=1, replica_groups=mesh['wide'=16,'col'=8] {'col'}, dimensions={0} | all-to-all | bytes 4194304 | tf_op jit(solution)/shard_map/all_to_all | solution.py:29
  442.1 1.9 fusion.20
  444.0 0.8 copy.73
  444.8 54.1 %all_to_all.69 = f32[16,32,4,512]{3,1,2,0:T(8,128)} all-to-all(f32[16,32,4,512]{3,1,2,0:T(8,128)S(1)} %copy.73), channel_id=1, replica_groups=mesh['wide'=16,'col'=8] {'wide'}, dimensions={0} | all-to-all | bytes 8388608 | tf_op jit(solution)/shard_map/all_to_all | solution.py:22
  499.0 2.6 reduce_sum.69
  501.6 0.9 copy.76
  (44 shorter events, 3.0 us)
Async XLA Ops:
  0.6 441.5 %copy-start = (f32[4,256,512]{2,1,0:T(8,128)S(1)}, f32[4,256,512]{2,1,0:T(8,128)}, u32[]{:S(2)}) copy-start(f32[4,256,512]{2,1,0:T(8,128)} %param.17) | copy-start | bytes 6291460
  5.7 35.4 %slice-start = ((s8[8388608]{0:T(1024)(128)(4,1)}), s8[4194304]{0:T(1024)(128)(4,1)S(1)}, s32[]{:S(2)}) async-start(s8[8388608]{0:T(1024)(128)(4,1)} %bitcast.64), calls=%async_computation.12 | async-start | bytes 8388608
  38.0 3.1 slice-start.1
  38.5 1.4 copy-start.1
  49.9 71.5 %all-to-all-start.1 = ((f32[16,32,2048]{2,1,0:T(8,128)}), f32[16,32,2048]{2,1,0:T(8,128)}, u32[]{:S(2)}, u32[]{:S(2)}) async-start(f32[16,32,2048]{2,1,0:T(8,128)} %fusion), calls=%async_computation.1 | async-start | bytes 8388608 | tf_op jit(solution)/shard_map/all_to_all | solution.py:22
  123.8 0.7 copy-start.5
  176.9 1.6 copy-start.3
  211.4 1.9 copy-start.7
  243.5 2.2 copy-start.2
  251.9 67.4 %all-to-all-start.6 = ((f32[16,32,2,1024]{3,1,2,0:T(8,128)}), f32[16,32,2,1024]{3,1,2,0:T(8,128)}, u32[]{:S(2)}, u32[]{:S(2)}) async-start(f32[16,32,2,1024]{3,1,2,0:T(8,128)} %copy.63), calls=%async_computation.6 | async-start | bytes 8388608 | tf_op jit(solution)/shard_map/all_to_all | solution.py:22
  322.0 2.0 copy-start.6
  376.7 1.2 copy-start.4
  409.9 1.8 copy-start.8

commit v5 on v4

--- a/solution.py
+++ b/solution.py
@@ -41,10 +41,9 @@
     return exchange_sum(matmul(right_side, inverse, "ski,kij->skj"), "wide")
 
 
-def send_blocks(tiles, owner, local):
-    here = lax.axis_index("col")
+def send_blocks(tiles, mine, local):
     picked = jnp.take(tiles, local, axis=0)
-    outgoing = jnp.where((owner == here)[:, :, None, None], picked, 0.0)
+    outgoing = jnp.where(mine[:, :, None, None], picked, 0.0)
     return lax.all_to_all(outgoing, "col", 0, 0, tiled=False).sum(0)
 
 
@@ -75,27 +74,21 @@
     n_col = lax.axis_size("col")
     lists = jnp.concatenate([anc_child.reshape(-1), anc_grand.reshape(-1)]).astype(jnp.float32)
     extra = jnp.zeros((1, z_root.shape[1]), jnp.float32).at[0, : lists.shape[0]].set(lists)
-    stacked = exchange_gather(jnp.concatenate([z_root, extra], axis=0)[None], "col", 0)
+    here = lax.axis_index("col")
+    with_lists, here = lax.optimization_barrier((jnp.concatenate([z_root, extra], axis=0)[None], here))
+    stacked = exchange_gather(with_lists, "col", 0)
     root_right = stacked[:, :-1].reshape(-1, z_root.shape[1])
     got = stacked[:, -1, : lists.shape[0]].astype(jnp.int32)
     split = anc_child.size
     anc_child = got[:, :split].reshape((n_col,) + anc_child.shape).transpose(1, 0, 2).reshape(anc_child.shape[0], -1)
     anc_grand = got[:, split:].reshape((n_col,) + anc_grand.shape).transpose(1, 0, 2).reshape(anc_grand.shape[0], -1)
-    x_root = exchange_sum(matmul(root_right, inv_root, "si,ij->sj"), "wide")
-    samples, width = x_root.shape
-    root_tiles = x_root.reshape(samples, width // BLK, BLK).transpose(1, 0, 2)
+    width = inv_root.shape[1]
     per_root = width // BLK
+    kids, child_width = inv_child.shape[0], inv_child.shape[2]
+    per_child = child_width // BLK
 
     child_slots = slots_of(anc_child, anc_child.shape[1] // n_col)
-    near_local = send_blocks(root_tiles, child_slots // per_root, child_slots % per_root)
-    near_local = rows_of(near_local, anc_child.shape[0], anc_child.shape[1] // n_col)
-    near_rows = exchange_gather(near_local, "wide", 0)
-    x_child = level(z_child, matmul(near_rows, panel_child, "ska,kaj->skj"), inv_child)
-
-    kids, child_width = x_child.shape[1], x_child.shape[2]
-    per_child = child_width // BLK
-    child_tiles = x_child.reshape(samples, kids * per_child, BLK).transpose(1, 0, 2)
-    all_tiles = jnp.concatenate([root_tiles, child_tiles], axis=0)
+    child_owner, child_local = child_slots // per_root, child_slots % per_root
     grand_slots = slots_of(anc_grand, anc_grand.shape[1] // n_col)
     root_blocks = per_root * n_col
     is_root = grand_slots < root_blocks
@@ -104,6 +97,23 @@
     child_kid = in_child // (per_child * n_col)
     owner = jnp.where(is_root, grand_slots // per_root, child_block // per_child)
     local = jnp.where(is_root, grand_slots % per_root, per_root + child_kid * per_child + child_block % per_child)
+    child_owner, owner = child_owner == here, owner == here
+    root_right, child_owner, child_local, owner, local = lax.optimization_barrier(
+        (root_right, child_owner, child_local, owner, local)
+    )
+    x_root = exchange_sum(matmul(root_right, inv_root, "si,ij->sj"), "wide")
+    x_root, child_owner, child_local, owner, local = lax.optimization_barrier(
+        (x_root, child_owner, child_local, owner, local)
+    )
+    root_tiles = x_root.reshape(x_root.shape[0], per_root, BLK).transpose(1, 0, 2)
+    near_local = send_blocks(root_tiles, child_owner, child_local)
+    near_local = rows_of(near_local, anc_child.shape[0], anc_child.shape[1] // n_col)
+    near_rows = exchange_gather(near_local, "wide", 0)
+    x_child = level(z_child, matmul(near_rows, panel_child, "ska,kaj->skj"), inv_child)
+
+    x_child, owner, local = lax.optimization_barrier((x_child, owner, local))
+    child_tiles = x_child.reshape(x_child.shape[0], kids * per_child, BLK).transpose(1, 0, 2)
+    all_tiles = jnp.concatenate([root_tiles, child_tiles], axis=0)
     far_local = send_blocks(all_tiles, owner, local)
     far_local = rows_of(far_local, anc_grand.shape[0], anc_grand.shape[1] // n_col)
     far_rows = exchange_gather(far_local, "wide", 0)

time: 503 us -> 470 us (0.934)
  waiting for transfers between devices: 125 us -> 0 us
  blocking collectives: 310 us -> 420 us
  starting transfers between devices: 12.6 us -> 0 us
    all_to_all x2 -> x0, waiting for transfers between devices: 125 us -> none  [exchange_sum(): lax.all_to_all(partial.reshape((n, chunk) + partial.shape[1:]), axis, 0,...]
    all_to_all x3 -> x5, blocking collectives: 115 us -> 229 us  [exchange_sum(): lax.all_to_all(partial.reshape((n, chunk) + partial.shape[1:]), axis, 0,...]
    all_to_all x2 -> x0, starting transfers between devices: 12.6 us -> none  [exchange_sum(): lax.all_to_all(partial.reshape((n, chunk) + partial.shape[1:]), axis, 0,...]
  transfers between devices with their start and end apart: 2 -> 0, of which waited for: 2 -> 0; matrix products, arithmetic and copies ran while one was open for 0% -> 0% of each run, Pallas kernels for 0% -> 0%
where the time goes in v5:
time: 470 us; the launch traced here: 469 us
  blocking collectives  420 us (89%)
  local copies, waits for them, and re-layouts  17 us (4%)
  matrix products  16 us (3%)
  other arithmetic  15.7 us (3%)
    all_to_all x5, blocking collectives, exchange_sum(): lax.all_to_all(partial.reshape((n, chunk) + partial.shape[1:]), axis, 0,...  229 us
    all_to_all x5, blocking collectives, exchange_gather(): parts = lax.all_to_all(stacked, axis, 0, 0, tiled=False)  154 us
    all_to_all x2, blocking collectives, send_blocks(): return lax.all_to_all(outgoing, 'col', 0, 0, tiled=False).sum(0)  37 us
    dot_general x5, matrix products, matmul(): jnp.einsum(spec, lhs, rhs, precision=PRECISE, preferred_element_type=jnp....  16 us
    reduce_sum x5, other arithmetic, exchange_sum(): return parts.sum(0)  11.2 us

profile of v5, /device:TPU:0, one launch (start us, length us, event | category | flops | bytes accessed | tf_op | source)
XLA Modules:
  0.0 469.4 jit_solution(12318408043167588125)
XLA Ops:
  0.6 0.6 compare_reduce_fusion
  1.3 0.8 concatenate.20
  2.0 0.8 copy.48
  2.9 0.7 broadcast_select_fusion
  3.6 1.0 fusion
  4.6 1.1 broadcast_in_dim.82
  5.7 32.3 %all_to_all.60 = f32[8,1,65,1024]{3,1,2,0:T(1,128)S(1)} all-to-all(f32[8,1,65,1024]{3,1,2,0:T(1,128)S(1)} %broadcast_in_dim.82), channel_id=1, replica_groups=mesh['wide'=16,'col'=8] {'col'}, dimensions={0} | all-to-all | bytes 4259840 | tf_op jit(solution)/shard_map/all_to_all | solution.py:29
  38.0 0.5 copy.86
  38.5 0.2 slice.36
  38.8 1.2 copy.50
  40.2 7.4 %fusion.16 = f32[512,2048]{1,0:T(8,128)S(1)} fusion(f32[512,1024]{1,0:T(8,128)S(1)} %bitcast.69, f32[1024,2048]{1,0:T(8,128)S(1)} %bitcast.68), kind=kOutput, calls=%fused_computation.68 | convolution fusion | flops 6442450944 | bytes 14680064 | tf_op jit(solution)/shard_map/si,ij->sj/dot_general | solution.py:35
  47.6 58.9 %all_to_all.61 = f32[16,32,2048]{2,1,0:T(8,128)} all-to-all(f32[16,32,2048]{2,1,0:T(8,128)S(1)} %bitcast.62), channel_id=1, replica_groups=mesh['wide'=16,'col'=8] {'wide'}, dimensions={0} | all-to-all | bytes 8388608 | tf_op jit(solution)/shard_map/all_to_all | solution.py:22
  106.6 2.4 reduce_sum.63
  109.1 0.6 copy-done.4
  109.7 0.6 gather_fusion
  110.6 18.5 %all_to_all.62 = f32[8,8,32,128]{3,2,1,0:T(8,128)S(1)} all-to-all(f32[8,8,32,128]{3,2,1,0:T(8,128)S(1)} %select_select_fusion.1), channel_id=1, replica_groups=mesh['wide'=16,'col'=8] {'col'}, dimensions={0} | all-to-all | bytes 2097152 | tf_op jit(solution)/shard_map/all_to_all | solution.py:47
  129.2 0.3 broadcast_in_dim.89
  129.4 31.0 %all_to_all.63 = f32[16,32,2,512]{3,1,2,0:T(8,128)S(1)} all-to-all(f32[16,32,2,512]{3,1,2,0:T(8,128)S(1)} %broadcast_in_dim.89), channel_id=1, replica_groups=mesh['wide'=16,'col'=8] {'wide'}, dimensions={0} | all-to-all | bytes 4194304 | tf_op jit(solution)/shard_map/all_to_all | solution.py:29
  160.4 0.2 copy.53
  160.7 1.4 copy-done.2
  162.0 2.0 fusion.17
  164.2 30.7 %all_to_all.64 = f32[8,64,2,512]{3,1,2,0:T(8,128)} all-to-all(f32[8,64,2,512]{3,1,2,0:T(8,128)S(1)} %copy.54), channel_id=1, replica_groups=mesh['wide'=16,'col'=8] {'col'}, dimensions={0} | all-to-all | bytes 4194304 | tf_op jit(solution)/shard_map/all_to_all | solution.py:22
  194.9 1.9 reduce_sum.65
  196.8 0.3 broadcast_in_dim.90
  197.1 30.0 %all_to_all.65 = f32[8,64,2,512]{3,1,2,0:T(8,128)S(1)} all-to-all(f32[8,64,2,512]{3,1,2,0:T(8,128)S(1)} %broadcast_in_dim.90), channel_id=1, replica_groups=mesh['wide'=16,'col'=8] {'col'}, dimensions={0} | all-to-all | bytes 4194304 | tf_op jit(solution)/shard_map/all_to_all | solution.py:29
  227.0 0.2 copy.57
  227.3 2.0 copy-done.1
  229.2 3.6 fusion.18
  232.8 0.6 copy.58
  233.4 54.1 %all_to_all.66 = f32[16,32,2,1024]{3,1,2,0:T(8,128)} all-to-all(f32[16,32,2,1024]{3,1,2,0:T(8,128)S(1)} %copy.58), channel_id=1, replica_groups=mesh['wide'=16,'col'=8] {'wide'}, dimensions={0} | all-to-all | bytes 8388608 | tf_op jit(solution)/shard_map/all_to_all | solution.py:22
  287.5 2.5 reduce_sum.66
  290.7 1.6 gather_fusion.1
  292.3 1.4 select_select_fusion
  293.8 18.5 %all_to_all.67 = f32[8,8,32,128]{3,2,1,0:T(8,128)S(1)} all-to-all(f32[8,8,32,128]{3,2,1,0:T(8,128)S(1)} %select_select_fusion), channel_id=1, replica_groups=mesh['wide'=16,'col'=8] {'col'}, dimensions={0} | all-to-all | bytes 2097152 | tf_op jit(solution)/shard_map/all_to_all | solution.py:47
  312.4 0.2 broadcast_in_dim.95
  312.6 31.0 %all_to_all.68 = f32[16,32,4,256]{3,1,2,0:T(8,128)S(1)} all-to-all(f32[16,32,4,256]{3,1,2,0:T(8,128)S(1)} %broadcast_in_dim.95), channel_id=1, replica_groups=mesh['wide'=16,'col'=8] {'wide'}, dimensions={0} | all-to-all | bytes 4194304 | tf_op jit(solution)/shard_map/all_to_all | solution.py:29
  343.6 0.2 copy.63
  343.9 1.0 copy-done.3
  344.8 1.1 fusion.19
  346.2 30.7 %all_to_all.69 = f32[8,64,4,256]{3,1,2,0:T(8,128)} all-to-all(f32[8,64,4,256]{3,1,2,0:T(8,128)S(1)} %copy.64), channel_id=1, replica_groups=mesh['wide'=16,'col'=8] {'col'}, dimensions={0} | all-to-all | bytes 4194304 | tf_op jit(solution)/shard_map/all_to_all | solution.py:22
  376.8 1.8 reduce_sum.68
  378.7 0.2 broadcast_in_dim.96
  378.9 30.0 %all_to_all.70 = f32[8,64,4,256]{3,1,2,0:T(8,128)S(1)} all-to-all(f32[8,64,4,256]{3,1,2,0:T(8,128)S(1)} %broadcast_in_dim.96), channel_id=1, replica_groups=mesh['wide'=16,'col'=8] {'col'}, dimensions={0} | all-to-all | bytes 4194304 | tf_op jit(solution)/shard_map/all_to_all | solution.py:29
  409.1 1.9 fusion.20
  411.0 0.8 copy.68
  411.8 54.1 %all_to_all.71 = f32[16,32,4,512]{3,1,2,0:T(8,128)} all-to-all(f32[16,32,4,512]{3,1,2,0:T(8,128)S(1)} %copy.68), channel_id=1, replica_groups=mesh['wide'=16,'col'=8] {'wide'}, dimensions={0} | all-to-all | bytes 8388608 | tf_op jit(solution)/shard_map/all_to_all | solution.py:22
  465.9 2.6 reduce_sum.69
  468.5 0.9 copy.71
  (44 shorter events, 2.1 us)
Async XLA Ops:
  0.6 408.4 %copy-start = (f32[4,256,512]{2,1,0:T(8,128)S(1)}, f32[4,256,512]{2,1,0:T(8,128)}, u32[]{:S(2)}) copy-start(f32[4,256,512]{2,1,0:T(8,128)} %param.17) | copy-start | bytes 6291460
  5.7 34.5 %slice-start = ((s8[8388608]{0:T(1024)(128)(4,1)}), s8[4194304]{0:T(1024)(128)(4,1)S(1)}, s32[]{:S(2)}) async-start(s8[8388608]{0:T(1024)(128)(4,1)} %bitcast.67), calls=%async_computation.12 | async-start | bytes 8388608
  38.0 2.2 slice-start.1
  109.0 0.7 copy-start.4
  160.4 1.6 copy-start.2
  194.9 1.9 copy-start.6
  227.0 2.2 copy-start.1
  290.3 2.1 copy-start.5
  343.6 1.2 copy-start.3
  376.8 1.8 copy-start.7

commit v6 on v4

v6 whole, which is shorter than its diff:
```python
import jax
import jax.numpy as jnp
from jax import lax
from jax.sharding import PartitionSpec as P

BLK = 128
STREAMS = 2


PRECISE = lax.Precision.HIGH


def exchange_sum(partial, axis):
    n = lax.axis_size(axis)
    chunk = partial.shape[0] // n
    parts = lax.all_to_all(partial.reshape((n, chunk) + partial.shape[1:]), axis, 0, 0, tiled=False)
    return parts.sum(0)


def exchange_gather(local, axis, dim):
    n = lax.axis_size(axis)
    stacked = jnp.broadcast_to(local[None], (n,) + local.shape)
    parts = lax.all_to_all(stacked, axis, 0, 0, tiled=False)
    parts = jnp.moveaxis(parts, 0, dim)
    return parts.reshape(local.shape[:dim] + (n * local.shape[dim],) + local.shape[dim + 1 :])


def shifted(value, axis, step):
    n = lax.axis_size(axis)
    return lax.ppermute(value, axis, [(i, (i + step) % n) for i in range(n)])


def permute_gather(local, axis):
    n = lax.axis_size(axis)
    here = lax.axis_index(axis)
    parts = jnp.stack([local] + [shifted(local, axis, step) for step in range(1, n)])
    ordered = jnp.take(parts, (here - jnp.arange(n)) % n, axis=0)
    return ordered.reshape((n * local.shape[0],) + local.shape[1:])


def permute_sum(chunks, axis):
    n = lax.axis_size(axis)
    here = lax.axis_index(axis)
    total = jnp.take(chunks, here, axis=0)
    for step in range(1, n):
        total = total + shifted(jnp.take(chunks, (here + step) % n, axis=0), axis, step)
    return total


def matmul(lhs, rhs, spec):
    return jnp.einsum(spec, lhs, rhs, precision=PRECISE, preferred_element_type=jnp.float32)


def level(z_local, update_partial, inverse):
    n = lax.axis_size("col")
    update = permute_sum(update_partial.reshape((n, -1) + update_partial.shape[1:]), "col")
    right_side = permute_gather(z_local - update, "col")
    return exchange_sum(matmul(right_side, inverse, "ski,kij->skj"), "wide")


def send_blocks(tiles, mine, local):
    picked = jnp.take(tiles, local, axis=0)
    outgoing = jnp.where(mine[:, :, None, None], picked, 0.0)
    return permute_sum(outgoing, "col")


def slots_of(blocks, per_device):
    rows = blocks.shape[0]
    n_col = blocks.shape[1] // per_device
    return blocks.reshape(rows, n_col, per_device).transpose(1, 0, 2).reshape(n_col, rows * per_device)


def rows_of(received, rows, per_device):
    samples = received.shape[1]
    shaped = received.reshape(rows, per_device, samples, BLK).transpose(2, 0, 1, 3)
    return shaped.reshape(samples, rows, per_device * BLK)


def stream_rows(z_local, stream):
    rows = z_local.reshape((2, STREAMS, z_local.shape[0] // (2 * STREAMS)) + z_local.shape[1:])[:, stream]
    return rows.reshape((-1,) + z_local.shape[1:])


def one_stream(z_root, z_child, z_grand, inv_root, inv_child, inv_grand, panel_child, panel_grand, tables):
    child_mine, child_local, grand_mine, grand_local, child_rows, child_per, grand_rows, grand_per = tables
    root_right = permute_gather(z_root, "col")
    x_root = exchange_sum(matmul(root_right, inv_root, "si,ij->sj"), "wide")
    per_root = x_root.shape[1] // BLK
    root_tiles = x_root.reshape(x_root.shape[0], per_root, BLK).transpose(1, 0, 2)
    near_local = rows_of(send_blocks(root_tiles, child_mine, child_local), child_rows, child_per)
    near_rows = exchange_gather(near_local, "wide", 0)
    x_child = level(z_child, matmul(near_rows, panel_child, "ska,kaj->skj"), inv_child)

    kids, per_child = x_child.shape[1], x_child.shape[2] // BLK
    child_tiles = x_child.reshape(x_child.shape[0], kids * per_child, BLK).transpose(1, 0, 2)
    all_tiles = jnp.concatenate([root_tiles, child_tiles], axis=0)
    far_local = rows_of(send_blocks(all_tiles, grand_mine, grand_local), grand_rows, grand_per)
    far_rows = exchange_gather(far_local, "wide", 0)
    x_grand = level(z_grand, matmul(far_rows, panel_grand, "sga,gaj->sgj"), inv_grand)
    return (x_root, x_child, x_grand)


def per_device(
    z_root,
    z_child,
    z_grand,
    inv_root,
    inv_child,
    inv_grand,
    panel_child,
    panel_grand,
    anc_child,
    anc_grand,
):
    n_col = lax.axis_size("col")
    here = lax.axis_index("col")
    lists = jnp.concatenate([anc_child.reshape(-1), anc_grand.reshape(-1)])
    got = permute_gather(lists[None], "col")
    split = anc_child.size
    anc_child = got[:, :split].reshape((n_col,) + anc_child.shape).transpose(1, 0, 2).reshape(anc_child.shape[0], -1)
    anc_grand = got[:, split:].reshape((n_col,) + anc_grand.shape).transpose(1, 0, 2).reshape(anc_grand.shape[0], -1)

    per_root = inv_root.shape[1] // BLK
    per_child = inv_child.shape[2] // BLK
    child_slots = slots_of(anc_child, anc_child.shape[1] // n_col)
    grand_slots = slots_of(anc_grand, anc_grand.shape[1] // n_col)
    root_blocks = per_root * n_col
    is_root = grand_slots < root_blocks
    in_child = grand_slots - root_blocks
    child_block = in_child % (per_child * n_col)
    child_kid = in_child // (per_child * n_col)
    owner = jnp.where(is_root, grand_slots // per_root, child_block // per_child)
    local = jnp.where(is_root, grand_slots % per_root, per_root + child_kid * per_child + child_block % per_child)
    tables = (
        child_slots // per_root == here,
        child_slots % per_root,
        owner == here,
        local,
        anc_child.shape[0],
        anc_child.shape[1] // n_col,
        anc_grand.shape[0],
        anc_grand.shape[1] // n_col,
    )
    outs = [
        one_stream(
            stream_rows(z_root, h),
            stream_rows(z_child, h),
            stream_rows(z_grand, h),
            inv_root,
            inv_child,
            inv_grand,
            panel_child,
            panel_grand,
            tables,
        )
        for h in range(STREAMS)
    ]
    return tuple(jnp.concatenate(parts, axis=0) for parts in zip(*outs))


def solution(mesh):
    in_specs = (
        P("col", "wide"),
        P("col", None, "wide"),
        P("col", None, "wide"),
        P("wide", "col"),
        P(None, "wide", "col"),
        P(None, "wide", "col"),
        P(None, "col", "wide"),
        P(None, "col", "wide"),
        P(None, "col"),
        P(None, "col"),
    )
    out_specs = (P("wide", "col"), P("wide", None, "col"), P("wide", None, "col"))
    return jax.shard_map(
        per_device, mesh=mesh, in_specs=in_specs, out_specs=out_specs, check_vma=False
    )
```

time: 503 us -> 566 us (1.13); the launches traced: 502 us -> 556 us
  blocking collectives: 310 us -> 0 us
  starting transfers between devices: 12.6 us -> 191 us
  waiting for transfers between devices: 125 us -> 214 us
  local copies, waits for them, and re-layouts: 20.2 us -> 82.5 us
  other arithmetic: 16.3 us -> 38.4 us
  matrix products: 17.3 us -> 27.8 us
    all_to_all x10 -> x0, blocking collectives: 310 us -> none  [the longest x5 157 us: exchange_gather(): parts = lax.all_to_all(stacked, axis, 0, 0, tiled=False)]
    ppermute x0 -> x105, starting transfers between devices: none -> 144 us  [shifted(): return lax.ppermute(value, axis, [(i, (i + step) % n) for i in range(n)])]
    all_to_all x2 -> x6, waiting for transfers between devices: 125 us -> 167 us  [exchange_sum(): lax.all_to_all(partial.reshape((n, chunk) + partial.shape[1:]), axis, 0,...]
    unnamed x25 -> x95, local copies, waits for them, and re-layouts: 8 us -> 41.8 us
    ppermute x0 -> x105, waiting for transfers between devices: none -> 24.6 us  [shifted(): return lax.ppermute(value, axis, [(i, (i + step) % n) for i in range(n)])]
    all_to_all x0 -> x4, waiting for transfers between devices: none -> 22.6 us  [exchange_gather(): parts = lax.all_to_all(stacked, axis, 0, 0, tiled=False)]
    all_to_all x2 -> x6, starting transfers between devices: 12.6 us -> 30.9 us  [exchange_sum(): lax.all_to_all(partial.reshape((n, chunk) + partial.shape[1:]), axis, 0,...]
    all_to_all x0 -> x4, starting transfers between devices: none -> 16.1 us  [exchange_gather(): parts = lax.all_to_all(stacked, axis, 0, 0, tiled=False)]
  transfers between devices with their start and end apart: 2 -> 115, of which waited for: 2 -> 32; matrix products, arithmetic and copies ran while one was open for 0% -> 16% of each run, Pallas kernels for 0% -> 0%
where the time goes in v6:
time: 566 us; the launch traced here: 556 us
  waiting for transfers between devices  214 us (38%)
  starting transfers between devices  191 us (34%)
  local copies, waits for them, and re-layouts  82.5 us (15%)
  other arithmetic  38.4 us (7%)
  matrix products  27.8 us (5%)
    all_to_all x6, waiting for transfers between devices, exchange_sum(): lax.all_to_all(partial.reshape((n, chunk) + partial.shape[1:]), axis, 0,...  167 us
    ppermute x105, starting transfers between devices, shifted(): return lax.ppermute(value, axis, [(i, (i + step) % n) for i in range(n)])  144 us
    unnamed x95, local copies, waits for them, and re-layouts  41.8 us
    all_to_all x6, starting transfers between devices, exchange_sum(): lax.all_to_all(partial.reshape((n, chunk) + partial.shape[1:]), axis, 0,...  30.9 us
    dot_general x10, matrix products, matmul(): jnp.einsum(spec, lhs, rhs, precision=PRECISE, preferred_element_type=jnp....  27.8 us
    ppermute x105, waiting for transfers between devices, shifted(): return lax.ppermute(value, axis, [(i, (i + step) % n) for i in range(n)])  24.6 us
    all_to_all x4, waiting for transfers between devices, exchange_gather(): parts = lax.all_to_all(stacked, axis, 0, 0, tiled=False)  22.6 us
    all_to_all x4, starting transfers between devices, exchange_gather(): parts = lax.all_to_all(stacked, axis, 0, 0, tiled=False)  16.1 us
  transfers between devices with their start and end apart: 115, of which 32 were waited for; matrix products, arithmetic and copies ran while one was open for 16% of the time, Pallas kernels for 0%

profile of v6, /device:TPU:0, one launch (start us, length us, event | category | flops | bytes accessed | tf_op | source)
XLA Modules:
  0.0 556.0 jit_solution(9482577119676225239)
XLA Ops:
  18.8 3.9 collective-permute-start.3
  35.6 2.8 gather_fusion.1
  38.5 2.5 broadcast_select_fusion.5
  41.0 7.7 %fusion.2 = f32[16,16,2048]{2,1,0:T(8,128)} fusion(f32[16,16,1024]{2,1,0:T(8,128)S(1)} %bitcast.682, f32[1024,2048]{1,0:T(8,128)} %param.29), kind=kOutput, calls=%fused_computation.13 | convolution fusion | flops 3221225472 | bytes 11534336 | tf_op jit(solution)/shard_map/si,ij->sj/dot_general | solution.py:51
  48.6 8.4 %all-to-all-start = ((f32[16,16,2048]{2,1,0:T(8,128)}), f32[16,16,2048]{2,1,0:T(8,128)}, u32[]{:S(2)}, u32[]{:S(2)}) async-start(f32[16,16,2048]{2,1,0:T(8,128)} %fusion.2), calls=%async_computation | async-start | bytes 4194304 | tf_op jit(solution)/shard_map/all_to_all | solution.py:16
  60.0 3.5 collective-permute-start.17
  65.6 7.6 %fusion = f32[16,16,2048]{2,1,0:T(8,128)} fusion(f32[16,16,1024]{2,1,0:T(8,128)S(1)} %bitcast.681, f32[1024,2048]{1,0:T(8,128)} %param.29), kind=kOutput, calls=%fused_computation.11 | convolution fusion | flops 3221225472 | bytes 11534336 | tf_op jit(solution)/shard_map/si,ij->sj/dot_general | solution.py:51
  73.2 18.9 %all-to-all-done = f32[16,16,2048]{2,1,0:T(8,128)} async-done(((f32[16,16,2048]{2,1,0:T(8,128)}), f32[16,16,2048]{2,1,0:T(8,128)}, u32[]{:S(2)}, u32[]{:S(2)}) %all-to-all-start) | async-done | bytes 2097184 | tf_op jit(solution)/shard_map/all_to_all | solution.py:16
  92.0 4.4 all-to-all-start.1
  100.4 28.9 %all-to-all-done.1 = f32[16,16,2048]{2,1,0:T(8,128)} async-done(((f32[16,16,2048]{2,1,0:T(8,128)}), f32[16,16,2048]{2,1,0:T(8,128)}, u32[]{:S(2)}, u32[]{:S(2)}) %all-to-all-start.1) | async-done | bytes 2097184 | tf_op jit(solution)/shard_map/all_to_all | solution.py:16
  136.3 4.4 collective-permute-start.45
  149.0 3.7 all-to-all-start.4
  159.2 2.6 collective-permute-start.25
  167.6 5.1 all-to-all-done.4
  174.7 4.4 all-to-all-start.2
  183.9 3.2 collective-permute-start.51
  188.0 2.7 collective-permute-start.53
  191.4 5.5 all-to-all-done.2
  200.0 3.7 collective-permute-start.54
  212.6 4.6 collective-permute-start.34
  221.6 4.1 collective-permute-start.59
  225.6 8.6 %collective-permute-start.60 = (f32[32,2,512]{2,0,1:T(8,128)S(1)}, f32[32,2,512]{2,0,1:T(8,128)S(1)}, u32[]{:S(2)}, u32[]{:S(2)}) collective-permute-start(f32[32,2,512]{2,0,1:T(8,128)S(1)} %get-tuple-element.58), channel_id=1, source_target_pairs={{0,5},{1,6},{2,7},{3,0},{4,1},{5,2},{6,3},{7,4},{8,13},{9,14},{10,... | collective-permute-start | bytes 393224 | tf_op jit(solution)/shard_map/ppermute | solution.py:30
  240.3 2.4 collective-permute-start.37
  260.3 2.8 gather_fusion.4
  263.1 2.6 broadcast_select_fusion.3
  269.7 4.6 all-to-all-start.5
  274.4 4.3 fusion.114
  280.2 28.8 %all-to-all-done.5 = f32[16,16,2,1024]{3,1,2,0:T(8,128)} async-done(((f32[16,16,2,1024]{3,1,2,0:T(8,128)}), f32[16,16,2,1024]{3,1,2,0:T(8,128)}, u32[]{:S(2)}, u32[]{:S(2)}) %all-to-all-start.5) | async-done | bytes 2097184 | tf_op jit(solution)/shard_map/all_to_all | solution.py:16
  309.0 4.4 all-to-all-start.3
  315.9 29.8 %all-to-all-done.3 = f32[16,16,2,1024]{3,1,2,0:T(8,128)} async-done(((f32[16,16,2,1024]{3,1,2,0:T(8,128)}), f32[16,16,2,1024]{3,1,2,0:T(8,128)}, u32[]{:S(2)}, u32[]{:S(2)}) %all-to-all-start.3) | async-done | bytes 2097184 | tf_op jit(solution)/shard_map/all_to_all | solution.py:16
  352.1 4.1 collective-permute-start.87
  363.1 3.7 all-to-all-start.8
  381.0 5.7 %all-to-all-done.8 = f32[16,16,4,256]{3,1,2,0:T(8,128)S(1)} async-done(((f32[16,16,4,256]{3,1,2,0:T(8,128)}), f32[16,16,4,256]{3,1,2,0:T(8,128)S(1)}, u32[]{:S(2)}, u32[]{:S(2)}) %all-to-all-start.8) | async-done | bytes 1048608 | tf_op jit(solution)/shard_map/all_to_all | solution.py:23
  388.8 4.5 all-to-all-start.6
  397.7 2.9 collective-permute-start.93
  401.8 2.4 collective-permute-start.95
  404.8 6.3 %all-to-all-done.6 = f32[16,16,4,256]{3,1,2,0:T(8,128)} async-done(((f32[16,16,4,256]{3,1,2,0:T(8,128)}), f32[16,16,4,256]{3,1,2,0:T(8,128)}, u32[]{:S(2)}, u32[]{:S(2)}) %all-to-all-start.6) | async-done | bytes 1048608 | tf_op jit(solution)/shard_map/all_to_all | solution.py:23
  413.3 3.4 collective-permute-start.96
  425.7 4.6 collective-permute-start.76
  434.6 4.1 collective-permute-start.101
  442.0 4.0 collective-permute-start.104
  451.0 4.1 collective-permute-start.80
  468.7 2.8 gather_fusion.8
  471.5 2.5 broadcast_select_fusion.1
  477.0 4.6 all-to-all-start.7
  484.4 31.9 %all-to-all-done.7 = f32[16,16,4,512]{3,1,2,0:T(8,128)} async-done(((f32[16,16,4,512]{3,1,2,0:T(8,128)}), f32[16,16,4,512]{3,1,2,0:T(8,128)}, u32[]{:S(2)}, u32[]{:S(2)}) %all-to-all-start.7) | async-done | bytes 2097184 | tf_op jit(solution)/shard_map/all_to_all | solution.py:16
  516.3 4.4 all-to-all-start.9
  524.2 28.8 %all-to-all-done.9 = f32[16,16,4,512]{3,1,2,0:T(8,128)} async-done(((f32[16,16,4,512]{3,1,2,0:T(8,128)}), f32[16,16,4,512]{3,1,2,0:T(8,128)}, u32[]{:S(2)}, u32[]{:S(2)}) %all-to-all-start.9) | async-done | bytes 2097184 | tf_op jit(solution)/shard_map/all_to_all | solution.py:16
  (391 shorter events, 208.6 us)
Async XLA Ops:
  15.9 12.5 %collective-permute-start.1 = (f32[32,1024]{1,0:T(8,128)S(1)}, f32[32,1024]{1,0:T(8,128)S(1)}, u32[]{:S(2)}, u32[]{:S(2)}) collective-permute-start(f32[32,1024]{1,0:T(8,128)S(1)} %bitcast.693), channel_id=1, source_target_pairs={{0,2},{1,3},{2,4},{3,5},{4,6},{5,7},{6,0},{7,1},{8,10},{9,11},{10,... | collective-permute-start | bytes 393224 | tf_op jit(solution)/shard_map/ppermute | solution.py:30
  16.6 13.0 %collective-permute-start.2 = (f32[32,1024]{1,0:T(8,128)S(1)}, f32[32,1024]{1,0:T(8,128)}, u32[]{:S(2)}, u32[]{:S(2)}) collective-permute-start(f32[32,1024]{1,0:T(8,128)S(1)} %bitcast.694), channel_id=1, source_target_pairs={{0,3},{1,4},{2,5},{3,6},{4,7},{5,0},{6,1},{7,2},{8,11},{9,12},{10,... | collective-permute-start | bytes 393224 | tf_op jit(solution)/shard_map/ppermute | solution.py:30
  48.6 43.4 %all-to-all-start = ((f32[16,16,2048]{2,1,0:T(8,128)}), f32[16,16,2048]{2,1,0:T(8,128)}, u32[]{:S(2)}, u32[]{:S(2)}) async-start(f32[16,16,2048]{2,1,0:T(8,128)} %fusion.2), calls=%async_computation | async-start | bytes 4194304 | tf_op jit(solution)/shard_map/all_to_all | solution.py:16
  59.4 37.1 %collective-permute-start.16 = (s32[1,16]{1,0:T(1,128)S(1)}, s32[1,16]{1,0:T(1,128)S(1)}, u32[]{:S(2)}, u32[]{:S(2)}) collective-permute-start(s32[1,16]{1,0:T(1,128)S(1)} %fusion.105), channel_id=1, source_target_pairs={{0,3},{1,4},{2,5},{3,6},{4,7},{5,0},{6,1},{7,2},{8,11},{9,12},{10,... | collective-permute-start | bytes 200 | tf_op jit(solution)/shard_map/ppermute | solution.py:30
  60.0 36.5 %collective-permute-start.17 = (s32[1,16]{1,0:T(1,128)S(1)}, s32[1,16]{1,0:T(1,128)S(1)}, u32[]{:S(2)}, u32[]{:S(2)}) collective-permute-start(s32[1,16]{1,0:T(1,128)S(1)} %fusion.105), channel_id=1, source_target_pairs={{0,4},{1,5},{2,6},{3,7},{4,0},{5,1},{6,2},{7,3},{8,12},{9,13},{10,... | collective-permute-start | bytes 200 | tf_op jit(solution)/shard_map/ppermute | solution.py:30
  63.5 33.0 %collective-permute-start.18 = (s32[1,16]{1,0:T(1,128)S(1)}, s32[1,16]{1,0:T(1,128)S(1)}, u32[]{:S(2)}, u32[]{:S(2)}) collective-permute-start(s32[1,16]{1,0:T(1,128)S(1)} %fusion.105), channel_id=1, source_target_pairs={{0,5},{1,6},{2,7},{3,0},{4,1},{5,2},{6,3},{7,4},{8,13},{9,14},{10,... | collective-permute-start | bytes 200 | tf_op jit(solution)/shard_map/ppermute | solution.py:30
  63.8 32.8 %collective-permute-start.19 = (s32[1,16]{1,0:T(1,128)S(1)}, s32[1,16]{1,0:T(1,128)S(1)}, u32[]{:S(2)}, u32[]{:S(2)}) collective-permute-start(s32[1,16]{1,0:T(1,128)S(1)} %fusion.105), channel_id=1, source_target_pairs={{0,6},{1,7},{2,0},{3,1},{4,2},{5,3},{6,4},{7,5},{8,14},{9,15},{10,... | collective-permute-start | bytes 200 | tf_op jit(solution)/shard_map/ppermute | solution.py:30
  65.5 31.1 %collective-permute-start.20 = (s32[1,16]{1,0:T(1,128)S(1)}, s32[1,16]{1,0:T(1,128)S(1)}, u32[]{:S(2)}, u32[]{:S(2)}) collective-permute-start(s32[1,16]{1,0:T(1,128)S(1)} %fusion.105), channel_id=1, source_target_pairs={{0,7},{1,0},{2,1},{3,2},{4,3},{5,4},{6,5},{7,6},{8,15},{9,8},{10,9... | collective-permute-start | bytes 200 | tf_op jit(solution)/shard_map/ppermute | solution.py:30
  92.0 37.3 %all-to-all-start.1 = ((f32[16,16,2048]{2,1,0:T(8,128)}), f32[16,16,2048]{2,1,0:T(8,128)}, u32[]{:S(2)}, u32[]{:S(2)}) async-start(f32[16,16,2048]{2,1,0:T(8,128)} %fusion), calls=%async_computation.1 | async-start | bytes 4194304 | tf_op jit(solution)/shard_map/all_to_all | solution.py:16
  149.0 23.7 %all-to-all-start.4 = ((f32[16,16,2,512]{3,1,2,0:T(8,128)}), f32[16,16,2,512]{3,1,2,0:T(8,128)S(1)}, u32[]{:S(2)}, u32[]{:S(2)}) async-start(f32[16,16,2,512]{3,1,2,0:T(8,128)} %broadcast_in_dim.151), calls=%async_computation.4 | async-start | bytes 2097152 | tf_op jit(solution)/shard_map/all_to_all | solution.py:23
  174.7 22.2 %all-to-all-start.2 = ((f32[16,16,2,512]{3,1,2,0:T(8,128)}), f32[16,16,2,512]{3,1,2,0:T(8,128)}, u32[]{:S(2)}, u32[]{:S(2)}) async-start(f32[16,16,2,512]{3,1,2,0:T(8,128)} %broadcast_in_dim.149), calls=%async_computation.2 | async-start | bytes 2097152 | tf_op jit(solution)/shard_map/all_to_all | solution.py:23
  182.7 17.3 %collective-permute-start.49 = (f32[32,2,512]{2,0,1:T(8,128)}, f32[32,2,512]{2,0,1:T(8,128)}, u32[]{:S(2)}, u32[]{:S(2)}) collective-permute-start(f32[32,2,512]{2,0,1:T(8,128)} %get-tuple-element.81), channel_id=1, source_target_pairs={{0,1},{1,2},{2,3},{3,4},{4,5},{5,6},{6,7},{7,0},{8,9},{9,10},{10,1... | collective-permute-start | bytes 393224 | tf_op jit(solution)/shard_map/ppermute | solution.py:30
  182.7 21.0 %collective-permute-start.50 = (f32[32,2,512]{2,0,1:T(8,128)}, f32[32,2,512]{2,0,1:T(8,128)}, u32[]{:S(2)}, u32[]{:S(2)}) collective-permute-start(f32[32,2,512]{2,0,1:T(8,128)} %get-tuple-element.85), channel_id=1, source_target_pairs={{0,2},{1,3},{2,4},{3,5},{4,6},{5,7},{6,0},{7,1},{8,10},{9,11},{10,... | collective-permute-start | bytes 393224 | tf_op jit(solution)/shard_map/ppermute | solution.py:30
  183.9 19.8 %collective-permute-start.51 = (f32[32,2,512]{2,0,1:T(8,128)}, f32[32,2,512]{2,0,1:T(8,128)}, u32[]{:S(2)}, u32[]{:S(2)}) collective-permute-start(f32[32,2,512]{2,0,1:T(8,128)} %get-tuple-element.84), channel_id=1, source_target_pairs={{0,3},{1,4},{2,5},{3,6},{4,7},{5,0},{6,1},{7,2},{8,11},{9,12},{10,... | collective-permute-start | bytes 393224 | tf_op jit(solution)/shard_map/ppermute | solution.py:30
  187.1 17.1 %collective-permute-start.52 = (f32[32,2,512]{2,0,1:T(8,128)}, f32[32,2,512]{2,0,1:T(8,128)}, u32[]{:S(2)}, u32[]{:S(2)}) collective-permute-start(f32[32,2,512]{2,0,1:T(8,128)} %get-tuple-element.83), channel_id=1, source_target_pairs={{0,4},{1,5},{2,6},{3,7},{4,0},{5,1},{6,2},{7,3},{8,12},{9,13},{10,... | collective-permute-start | bytes 393224 | tf_op jit(solution)/shard_map/ppermute | solution.py:30
  188.0 16.4 %collective-permute-start.53 = (f32[32,2,512]{2,0,1:T(8,128)}, f32[32,2,512]{2,0,1:T(8,128)}, u32[]{:S(2)}, u32[]{:S(2)}) collective-permute-start(f32[32,2,512]{2,0,1:T(8,128)} %get-tuple-element.82), channel_id=1, source_target_pairs={{0,5},{1,6},{2,7},{3,0},{4,1},{5,2},{6,3},{7,4},{8,13},{9,14},{10,... | collective-permute-start | bytes 393224 | tf_op jit(solution)/shard_map/ppermute | solution.py:30
  204.4 14.8 %collective-permute-start.30 = (f32[32,2,512]{2,0,1:T(8,128)S(1)}, f32[32,2,512]{2,0,1:T(8,128)S(1)}, u32[]{:S(2)}, u32[]{:S(2)}) collective-permute-start(f32[32,2,512]{2,0,1:T(8,128)S(1)} %get-tuple-element.78), channel_id=1, source_target_pairs={{0,3},{1,4},{2,5},{3,6},{4,7},{5,0},{6,1},{7,2},{8,11},{9,12},{10,... | collective-permute-start | bytes 393224 | tf_op jit(solution)/shard_map/ppermute | solution.py:30
  206.2 13.6 %collective-permute-start.31 = (f32[32,2,512]{2,0,1:T(8,128)S(1)}, f32[32,2,512]{2,0,1:T(8,128)S(1)}, u32[]{:S(2)}, u32[]{:S(2)}) collective-permute-start(f32[32,2,512]{2,0,1:T(8,128)S(1)} %get-tuple-element.77), channel_id=1, source_target_pairs={{0,4},{1,5},{2,6},{3,7},{4,0},{5,1},{6,2},{7,3},{8,12},{9,13},{10,... | collective-permute-start | bytes 393224 | tf_op jit(solution)/shard_map/ppermute | solution.py:30
  208.5 13.0 %collective-permute-start.32 = (f32[32,2,512]{2,0,1:T(8,128)S(1)}, f32[32,2,512]{2,0,1:T(8,128)S(1)}, u32[]{:S(2)}, u32[]{:S(2)}) collective-permute-start(f32[32,2,512]{2,0,1:T(8,128)S(1)} %get-tuple-element.76), channel_id=1, source_target_pairs={{0,5},{1,6},{2,7},{3,0},{4,1},{5,2},{6,3},{7,4},{8,13},{9,14},{10,... | collective-permute-start | bytes 393224 | tf_op jit(solution)/shard_map/ppermute | solution.py:30
  212.6 13.0 %collective-permute-start.34 = (f32[32,2,512]{2,0,1:T(8,128)S(1)}, f32[32,2,512]{2,0,1:T(8,128)S(1)}, u32[]{:S(2)}, u32[]{:S(2)}) collective-permute-start(f32[32,2,512]{2,0,1:T(8,128)S(1)} %select_bitcast_fusion.3), channel_id=1, source_target_pairs={{0,7},{1,0},{2,1},{3,2},{4,3},{5,4},{6,5},{7,6},{8,15},{9,8},{10,9... | collective-permute-start | bytes 393224 | tf_op jit(solution)/shard_map/ppermute | solution.py:30
  219.2 15.9 %collective-permute-start.56 = (f32[32,2,512]{2,0,1:T(8,128)S(1)}, f32[32,2,512]{2,0,1:T(8,128)S(1)}, u32[]{:S(2)}, u32[]{:S(2)}) collective-permute-start(f32[32,2,512]{2,0,1:T(8,128)S(1)} %get-tuple-element.58), channel_id=1, source_target_pairs={{0,1},{1,2},{2,3},{3,4},{4,5},{5,6},{6,7},{7,0},{8,9},{9,10},{10,1... | collective-permute-start | bytes 393224 | tf_op jit(solution)/shard_map/ppermute | solution.py:30
  219.9 17.7 %collective-permute-start.57 = (f32[32,2,512]{2,0,1:T(8,128)S(1)}, f32[32,2,512]{2,0,1:T(8,128)S(1)}, u32[]{:S(2)}, u32[]{:S(2)}) collective-permute-start(f32[32,2,512]{2,0,1:T(8,128)S(1)} %get-tuple-element.58), channel_id=1, source_target_pairs={{0,2},{1,3},{2,4},{3,5},{4,6},{5,7},{6,0},{7,1},{8,10},{9,11},{10,... | collective-permute-start | bytes 393224 | tf_op jit(solution)/shard_map/ppermute | solution.py:30
  221.6 16.7 %collective-permute-start.58 = (f32[32,2,512]{2,0,1:T(8,128)S(1)}, f32[32,2,512]{2,0,1:T(8,128)S(1)}, u32[]{:S(2)}, u32[]{:S(2)}) collective-permute-start(f32[32,2,512]{2,0,1:T(8,128)S(1)} %get-tuple-element.58), channel_id=1, source_target_pairs={{0,3},{1,4},{2,5},{3,6},{4,7},{5,0},{6,1},{7,2},{8,11},{9,12},{10,... | collective-permute-start | bytes 393224 | tf_op jit(solution)/shard_map/ppermute | solution.py:30
  221.6 17.8 %collective-permute-start.59 = (f32[32,2,512]{2,0,1:T(8,128)S(1)}, f32[32,2,512]{2,0,1:T(8,128)S(1)}, u32[]{:S(2)}, u32[]{:S(2)}) collective-permute-start(f32[32,2,512]{2,0,1:T(8,128)S(1)} %get-tuple-element.58), channel_id=1, source_target_pairs={{0,4},{1,5},{2,6},{3,7},{4,0},{5,1},{6,2},{7,3},{8,12},{9,13},{10,... | collective-permute-start | bytes 393224 | tf_op jit(solution)/shard_map/ppermute | solution.py:30
  225.6 14.6 %collective-permute-start.60 = (f32[32,2,512]{2,0,1:T(8,128)S(1)}, f32[32,2,512]{2,0,1:T(8,128)S(1)}, u32[]{:S(2)}, u32[]{:S(2)}) collective-permute-start(f32[32,2,512]{2,0,1:T(8,128)S(1)} %get-tuple-element.58), channel_id=1, source_target_pairs={{0,5},{1,6},{2,7},{3,0},{4,1},{5,2},{6,3},{7,4},{8,13},{9,14},{10,... | collective-permute-start | bytes 393224 | tf_op jit(solution)/shard_map/ppermute | solution.py:30
  239.4 13.3 %collective-permute-start.36 = (f32[32,2,512]{2,0,1:T(8,128)}, f32[32,2,512]{2,0,1:T(8,128)}, u32[]{:S(2)}, u32[]{:S(2)}) collective-permute-start(f32[32,2,512]{2,0,1:T(8,128)} %get-tuple-element.56), channel_id=1, source_target_pairs={{0,2},{1,3},{2,4},{3,5},{4,6},{5,7},{6,0},{7,1},{8,10},{9,11},{10,... | collective-permute-start | bytes 393224 | tf_op jit(solution)/shard_map/ppermute | solution.py:30
  240.3 14.0 %collective-permute-start.37 = (f32[32,2,512]{2,0,1:T(8,128)}, f32[32,2,512]{2,0,1:T(8,128)}, u32[]{:S(2)}, u32[]{:S(2)}) collective-permute-start(f32[32,2,512]{2,0,1:T(8,128)} %get-tuple-element.56), channel_id=1, source_target_pairs={{0,3},{1,4},{2,5},{3,6},{4,7},{5,0},{6,1},{7,2},{8,11},{9,12},{10,... | collective-permute-start | bytes 393224 | tf_op jit(solution)/shard_map/ppermute | solution.py:30
  243.3 12.5 %collective-permute-start.38 = (f32[32,2,512]{2,0,1:T(8,128)}, f32[32,2,512]{2,0,1:T(8,128)}, u32[]{:S(2)}, u32[]{:S(2)}) collective-permute-start(f32[32,2,512]{2,0,1:T(8,128)} %get-tuple-element.56), channel_id=1, source_target_pairs={{0,4},{1,5},{2,6},{3,7},{4,0},{5,1},{6,2},{7,3},{8,12},{9,13},{10,... | collective-permute-start | bytes 393224 | tf_op jit(solution)/shard_map/ppermute | solution.py:30
  269.7 39.3 %all-to-all-start.5 = ((f32[16,16,2,1024]{3,1,2,0:T(8,128)}), f32[16,16,2,1024]{3,1,2,0:T(8,128)}, u32[]{:S(2)}, u32[]{:S(2)}) async-start(f32[16,16,2,1024]{3,1,2,0:T(8,128)} %copy.195), calls=%async_computation.5 | async-start | bytes 4194304 | tf_op jit(solution)/shard_map/all_to_all | solution.py:16
  309.0 36.6 %all-to-all-start.3 = ((f32[16,16,2,1024]{3,1,2,0:T(8,128)}), f32[16,16,2,1024]{3,1,2,0:T(8,128)}, u32[]{:S(2)}, u32[]{:S(2)}) async-start(f32[16,16,2,1024]{3,1,2,0:T(8,128)} %copy.181), calls=%async_computation.3 | async-start | bytes 4194304 | tf_op jit(solution)/shard_map/all_to_all | solution.py:16
  363.1 23.6 %all-to-all-start.8 = ((f32[16,16,4,256]{3,1,2,0:T(8,128)}), f32[16,16,4,256]{3,1,2,0:T(8,128)S(1)}, u32[]{:S(2)}, u32[]{:S(2)}) async-start(f32[16,16,4,256]{3,1,2,0:T(8,128)} %broadcast_in_dim.156), calls=%async_computation.8 | async-start | bytes 2097152 | tf_op jit(solution)/shard_map/all_to_all | solution.py:23
  388.8 22.3 %all-to-all-start.6 = ((f32[16,16,4,256]{3,1,2,0:T(8,128)}), f32[16,16,4,256]{3,1,2,0:T(8,128)}, u32[]{:S(2)}, u32[]{:S(2)}) async-start(f32[16,16,4,256]{3,1,2,0:T(8,128)} %broadcast_in_dim.154), calls=%async_computation.6 | async-start | bytes 2097152 | tf_op jit(solution)/shard_map/all_to_all | solution.py:23
  396.3 16.9 %collective-permute-start.91 = (f32[32,4,256]{2,0,1:T(8,128)}, f32[32,4,256]{2,0,1:T(8,128)}, u32[]{:S(2)}, u32[]{:S(2)}) collective-permute-start(f32[32,4,256]{2,0,1:T(8,128)} %get-tuple-element.69), channel_id=1, source_target_pairs={{0,1},{1,2},{2,3},{3,4},{4,5},{5,6},{6,7},{7,0},{8,9},{9,10},{10,1... | collective-permute-start | bytes 393224 | tf_op jit(solution)/shard_map/ppermute | solution.py:30
  396.3 20.5 %collective-permute-start.92 = (f32[32,4,256]{2,0,1:T(8,128)}, f32[32,4,256]{2,0,1:T(8,128)}, u32[]{:S(2)}, u32[]{:S(2)}) collective-permute-start(f32[32,4,256]{2,0,1:T(8,128)} %get-tuple-element.73), channel_id=1, source_target_pairs={{0,2},{1,3},{2,4},{3,5},{4,6},{5,7},{6,0},{7,1},{8,10},{9,11},{10,... | collective-permute-start | bytes 393224 | tf_op jit(solution)/shard_map/ppermute | solution.py:30
  397.7 19.1 %collective-permute-start.93 = (f32[32,4,256]{2,0,1:T(8,128)}, f32[32,4,256]{2,0,1:T(8,128)}, u32[]{:S(2)}, u32[]{:S(2)}) collective-permute-start(f32[32,4,256]{2,0,1:T(8,128)} %get-tuple-element.72), channel_id=1, source_target_pairs={{0,3},{1,4},{2,5},{3,6},{4,7},{5,0},{6,1},{7,2},{8,11},{9,12},{10,... | collective-permute-start | bytes 393224 | tf_op jit(solution)/shard_map/ppermute | solution.py:30
  400.5 16.7 %collective-permute-start.94 = (f32[32,4,256]{2,0,1:T(8,128)}, f32[32,4,256]{2,0,1:T(8,128)}, u32[]{:S(2)}, u32[]{:S(2)}) collective-permute-start(f32[32,4,256]{2,0,1:T(8,128)} %get-tuple-element.71), channel_id=1, source_target_pairs={{0,4},{1,5},{2,6},{3,7},{4,0},{5,1},{6,2},{7,3},{8,12},{9,13},{10,... | collective-permute-start | bytes 393224 | tf_op jit(solution)/shard_map/ppermute | solution.py:30
  401.8 15.6 %collective-permute-start.95 = (f32[32,4,256]{2,0,1:T(8,128)}, f32[32,4,256]{2,0,1:T(8,128)}, u32[]{:S(2)}, u32[]{:S(2)}) collective-permute-start(f32[32,4,256]{2,0,1:T(8,128)} %get-tuple-element.70), channel_id=1, source_target_pairs={{0,5},{1,6},{2,7},{3,0},{4,1},{5,2},{6,3},{7,4},{8,13},{9,14},{10,... | collective-permute-start | bytes 393224 | tf_op jit(solution)/shard_map/ppermute | solution.py:30
  417.4 14.8 %collective-permute-start.72 = (f32[32,4,256]{2,0,1:T(8,128)S(1)}, f32[32,4,256]{2,0,1:T(8,128)S(1)}, u32[]{:S(2)}, u32[]{:S(2)}) collective-permute-start(f32[32,4,256]{2,0,1:T(8,128)S(1)} %get-tuple-element.66), channel_id=1, source_target_pairs={{0,3},{1,4},{2,5},{3,6},{4,7},{5,0},{6,1},{7,2},{8,11},{9,12},{10,... | collective-permute-start | bytes 393224 | tf_op jit(solution)/shard_map/ppermute | solution.py:30
  419.3 13.6 %collective-permute-start.73 = (f32[32,4,256]{2,0,1:T(8,128)S(1)}, f32[32,4,256]{2,0,1:T(8,128)S(1)}, u32[]{:S(2)}, u32[]{:S(2)}) collective-permute-start(f32[32,4,256]{2,0,1:T(8,128)S(1)} %get-tuple-element.65), channel_id=1, source_target_pairs={{0,4},{1,5},{2,6},{3,7},{4,0},{5,1},{6,2},{7,3},{8,12},{9,13},{10,... | collective-permute-start | bytes 393224 | tf_op jit(solution)/shard_map/ppermute | solution.py:30
  421.6 13.0 %collective-permute-start.74 = (f32[32,4,256]{2,0,1:T(8,128)S(1)}, f32[32,4,256]{2,0,1:T(8,128)S(1)}, u32[]{:S(2)}, u32[]{:S(2)}) collective-permute-start(f32[32,4,256]{2,0,1:T(8,128)S(1)} %get-tuple-element.64), channel_id=1, source_target_pairs={{0,5},{1,6},{2,7},{3,0},{4,1},{5,2},{6,3},{7,4},{8,13},{9,14},{10,... | collective-permute-start | bytes 393224 | tf_op jit(solution)/shard_map/ppermute | solution.py:30
  425.7 13.0 %collective-permute-start.76 = (f32[32,4,256]{2,0,1:T(8,128)S(1)}, f32[32,4,256]{2,0,1:T(8,128)S(1)}, u32[]{:S(2)}, u32[]{:S(2)}) collective-permute-start(f32[32,4,256]{2,0,1:T(8,128)S(1)} %select_bitcast_fusion.1), channel_id=1, source_target_pairs={{0,7},{1,0},{2,1},{3,2},{4,3},{5,4},{6,5},{7,6},{8,15},{9,8},{10,9... | collective-permute-start | bytes 393224 | tf_op jit(solution)/shard_map/ppermute | solution.py:30
  434.6 13.5 %collective-permute-start.101 = (f32[32,4,256]{2,0,1:T(8,128)S(1)}, f32[32,4,256]{2,0,1:T(8,128)S(1)}, u32[]{:S(2)}, u32[]{:S(2)}) collective-permute-start(f32[32,4,256]{2,0,1:T(8,128)S(1)} %get-tuple-element.50), channel_id=1, source_target_pairs={{0,4},{1,5},{2,6},{3,7},{4,0},{5,1},{6,2},{7,3},{8,12},{9,13},{10,... | collective-permute-start | bytes 393224 | tf_op jit(solution)/shard_map/ppermute | solution.py:30
  442.0 13.8 %collective-permute-start.104 = (f32[32,4,256]{2,0,1:T(8,128)S(1)}, f32[32,4,256]{2,0,1:T(8,128)S(1)}, u32[]{:S(2)}, u32[]{:S(2)}) collective-permute-start(f32[32,4,256]{2,0,1:T(8,128)S(1)} %get-tuple-element.50), channel_id=1, source_target_pairs={{0,7},{1,0},{2,1},{3,2},{4,3},{5,4},{6,5},{7,6},{8,15},{9,8},{10,9... | collective-permute-start | bytes 393224 | tf_op jit(solution)/shard_map/ppermute | solution.py:30
  448.1 13.8 %collective-permute-start.78 = (f32[32,4,256]{2,0,1:T(8,128)S(1)}, f32[32,4,256]{2,0,1:T(8,128)}, u32[]{:S(2)}, u32[]{:S(2)}) collective-permute-start(f32[32,4,256]{2,0,1:T(8,128)S(1)} %get-tuple-element.48), channel_id=1, source_target_pairs={{0,2},{1,3},{2,4},{3,5},{4,6},{5,7},{6,0},{7,1},{8,10},{9,11},{10,... | collective-permute-start | bytes 393224 | tf_op jit(solution)/shard_map/ppermute | solution.py:30
  450.3 13.2 %collective-permute-start.79 = (f32[32,4,256]{2,0,1:T(8,128)S(1)}, f32[32,4,256]{2,0,1:T(8,128)}, u32[]{:S(2)}, u32[]{:S(2)}) collective-permute-start(f32[32,4,256]{2,0,1:T(8,128)S(1)} %get-tuple-element.48), channel_id=1, source_target_pairs={{0,3},{1,4},{2,5},{3,6},{4,7},{5,0},{6,1},{7,2},{8,11},{9,12},{10,... | collective-permute-start | bytes 393224 | tf_op jit(solution)/shard_map/ppermute | solution.py:30
  451.0 14.1 %collective-permute-start.80 = (f32[32,4,256]{2,0,1:T(8,128)S(1)}, f32[32,4,256]{2,0,1:T(8,128)}, u32[]{:S(2)}, u32[]{:S(2)}) collective-permute-start(f32[32,4,256]{2,0,1:T(8,128)S(1)} %get-tuple-element.48), channel_id=1, source_target_pairs={{0,4},{1,5},{2,6},{3,7},{4,0},{5,1},{6,2},{7,3},{8,12},{9,13},{10,... | collective-permute-start | bytes 393224 | tf_op jit(solution)/shard_map/ppermute | solution.py:30
  477.0 39.3 %all-to-all-start.7 = ((f32[16,16,4,512]{3,1,2,0:T(8,128)}), f32[16,16,4,512]{3,1,2,0:T(8,128)}, u32[]{:S(2)}, u32[]{:S(2)}) async-start(f32[16,16,4,512]{3,1,2,0:T(8,128)} %copy.210), calls=%async_computation.7 | async-start | bytes 4194304 | tf_op jit(solution)/shard_map/all_to_all | solution.py:16
  516.3 36.6 %all-to-all-start.9 = ((f32[16,16,4,512]{3,1,2,0:T(8,128)}), f32[16,16,4,512]{3,1,2,0:T(8,128)}, u32[]{:S(2)}, u32[]{:S(2)}) async-start(f32[16,16,4,512]{3,1,2,0:T(8,128)} %copy.225), calls=%async_computation.9 | async-start | bytes 4194304 | tf_op jit(solution)/shard_map/all_to_all | solution.py:16
  (91 other events, 1188.9 us)

commit v7 on v5

--- a/solution.py
+++ b/solution.py
@@ -31,20 +31,45 @@
     return parts.reshape(local.shape[:dim] + (n * local.shape[dim],) + local.shape[dim + 1 :])
 
 
+def chip_groups(n):
+    return [[2 * x + core for x in range(n // 2)] for core in range(2)]
+
+
+def col_sum(chunks, cores):
+    n = lax.axis_size("col")
+    paired = chunks.reshape((n // 2, 2) + chunks.shape[1:])
+    mine = lax.dynamic_index_in_dim(paired, cores[0], axis=1, keepdims=False)
+    other = lax.dynamic_index_in_dim(paired, cores[1], axis=1, keepdims=False)
+    chip = mine + lax.ppermute(other, "col", [(d, d ^ 1) for d in range(n)])
+    parts = lax.all_to_all(chip, "col", 0, 0, tiled=False, axis_index_groups=chip_groups(n))
+    return parts.sum(0)
+
+
+def col_gather(local, cores):
+    n = lax.axis_size("col")
+    stacked = jnp.broadcast_to(local[None], (n // 2,) + local.shape)
+    same = lax.all_to_all(stacked, "col", 0, 0, tiled=False, axis_index_groups=chip_groups(n))
+    other = lax.ppermute(same, "col", [(d, d ^ 1) for d in range(n)])
+    both = jnp.where(cores[2], jnp.stack([same, other], 1), jnp.stack([other, same], 1))
+    return both.reshape((n,) + local.shape)
+
+
 def matmul(lhs, rhs, spec):
     return jnp.einsum(spec, lhs, rhs, precision=PRECISE, preferred_element_type=jnp.float32)
 
 
-def level(z_local, update_partial, inverse):
-    update = exchange_sum(update_partial, "col")
-    right_side = exchange_gather(z_local - update, "col", 0)
+def level(z_local, update_partial, inverse, cores):
+    n = lax.axis_size("col")
+    update = col_sum(update_partial.reshape((n, -1) + update_partial.shape[1:]), cores)
+    right_side = col_gather(z_local - update, cores)
+    right_side = right_side.reshape((-1,) + right_side.shape[2:])
     return exchange_sum(matmul(right_side, inverse, "ski,kij->skj"), "wide")
 
 
-def send_blocks(tiles, mine, local):
+def send_blocks(tiles, mine, local, cores):
     picked = jnp.take(tiles, local, axis=0)
     outgoing = jnp.where(mine[:, :, None, None], picked, 0.0)
-    return lax.all_to_all(outgoing, "col", 0, 0, tiled=False).sum(0)
+    return col_sum(outgoing, cores)
 
 
 def slots_of(blocks, per_device):
@@ -75,8 +100,9 @@
     lists = jnp.concatenate([anc_child.reshape(-1), anc_grand.reshape(-1)]).astype(jnp.float32)
     extra = jnp.zeros((1, z_root.shape[1]), jnp.float32).at[0, : lists.shape[0]].set(lists)
     here = lax.axis_index("col")
-    with_lists, here = lax.optimization_barrier((jnp.concatenate([z_root, extra], axis=0)[None], here))
-    stacked = exchange_gather(with_lists, "col", 0)
+    cores = (here % 2, 1 - here % 2, here % 2 == 0)
+    with_lists, here, cores = lax.optimization_barrier((jnp.concatenate([z_root, extra], axis=0)[None], here, cores))
+    stacked = col_gather(with_lists[0], cores)
     root_right = stacked[:, :-1].reshape(-1, z_root.shape[1])
     got = stacked[:, -1, : lists.shape[0]].astype(jnp.int32)
     split = anc_child.size
@@ -98,26 +124,26 @@
     owner = jnp.where(is_root, grand_slots // per_root, child_block // per_child)
     local = jnp.where(is_root, grand_slots % per_root, per_root + child_kid * per_child + child_block % per_child)
     child_owner, owner = child_owner == here, owner == here
-    root_right, child_owner, child_local, owner, local = lax.optimization_barrier(
-        (root_right, child_owner, child_local, owner, local)
+    root_right, child_owner, child_local, owner, local, cores = lax.optimization_barrier(
+        (root_right, child_owner, child_local, owner, local, cores)
     )
     x_root = exchange_sum(matmul(root_right, inv_root, "si,ij->sj"), "wide")
-    x_root, child_owner, child_local, owner, local = lax.optimization_barrier(
-        (x_root, child_owner, child_local, owner, local)
+    x_root, child_owner, child_local, owner, local, cores = lax.optimization_barrier(
+        (x_root, child_owner, child_local, owner, local, cores)
     )
     root_tiles = x_root.reshape(x_root.shape[0], per_root, BLK).transpose(1, 0, 2)
-    near_local = send_blocks(root_tiles, child_owner, child_local)
+    near_local = send_blocks(root_tiles, child_owner, child_local, cores)
     near_local = rows_of(near_local, anc_child.shape[0], anc_child.shape[1] // n_col)
     near_rows = exchange_gather(near_local, "wide", 0)
-    x_child = level(z_child, matmul(near_rows, panel_child, "ska,kaj->skj"), inv_child)
+    x_child = level(z_child, matmul(near_rows, panel_child, "ska,kaj->skj"), inv_child, cores)
 
-    x_child, owner, local = lax.optimization_barrier((x_child, owner, local))
+    x_child, owner, local, cores = lax.optimization_barrier((x_child, owner, local, cores))
     child_tiles = x_child.reshape(x_child.shape[0], kids * per_child, BLK).transpose(1, 0, 2)
     all_tiles = jnp.concatenate([root_tiles, child_tiles], axis=0)
-    far_local = send_blocks(all_tiles, owner, local)
+    far_local = send_blocks(all_tiles, owner, local, cores)
     far_local = rows_of(far_local, anc_grand.shape[0], anc_grand.shape[1] // n_col)
     far_rows = exchange_gather(far_local, "wide", 0)
-    x_grand = level(z_grand, matmul(far_rows, panel_grand, "sga,gaj->sgj"), inv_grand)
+    x_grand = level(z_grand, matmul(far_rows, panel_grand, "sga,gaj->sgj"), inv_grand, cores)
     return (x_root, x_child, x_grand)
 
 

time: 470 us -> 423 us (0.900)
  blocking collectives: 420 us -> 347 us
  waiting for transfers between devices: 0 us -> 17.8 us
    all_to_all x5 -> x2, blocking collectives: 154 us -> 61.7 us  [exchange_gather(): parts = lax.all_to_all(stacked, axis, 0, 0, tiled=False)]
    all_to_all x2 -> x7, blocking collectives: 37 us -> 116 us  [the longest x4 61.1 us: col_sum(): lax.all_to_all(chip, 'col', 0, 0, tiled=False, axis_index_groups=chip_gro...]
    all_to_all x5 -> x3, blocking collectives: 229 us -> 169 us  [exchange_sum(): lax.all_to_all(partial.reshape((n, chunk) + partial.shape[1:]), axis, 0,...]
    ppermute x0 -> x7, waiting for transfers between devices: none -> 17.8 us  [the longest x4 9.79 us: col_sum(): chip = mine + lax.ppermute(other, 'col', [(d, d ^ 1) for d in range(n)])]
    reduce_sum x5 -> x3, other arithmetic: 11.2 us -> 7.53 us  [exchange_sum(): return parts.sum(0)]
  transfers between devices with their start and end apart: 0 -> 7, of which waited for: 0 -> 7; matrix products, arithmetic and copies ran while one was open for 0% -> 0% of each run, Pallas kernels for 0% -> 0%
where the time goes in v7:
time: 423 us; the launch traced here: 422 us
  blocking collectives  347 us (82%)
  local copies, waits for them, and re-layouts  19.8 us (5%)
  other arithmetic  19.5 us (5%)
  waiting for transfers between devices  17.8 us (4%)
  matrix products  16 us (4%)
    all_to_all x3, blocking collectives, exchange_sum(): lax.all_to_all(partial.reshape((n, chunk) + partial.shape[1:]), axis, 0,...  169 us
    all_to_all x2, blocking collectives, exchange_gather(): parts = lax.all_to_all(stacked, axis, 0, 0, tiled=False)  61.7 us
    all_to_all x4, blocking collectives, col_sum(): lax.all_to_all(chip, 'col', 0, 0, tiled=False, axis_index_groups=chip_gro...  61.1 us
    all_to_all x3, blocking collectives, col_gather(): lax.all_to_all(stacked, 'col', 0, 0, tiled=False, axis_index_groups=chip_...  55.2 us
    dot_general x5, matrix products, matmul(): jnp.einsum(spec, lhs, rhs, precision=PRECISE, preferred_element_type=jnp....  16 us
    ppermute x4, waiting for transfers between devices, col_sum(): chip = mine + lax.ppermute(other, 'col', [(d, d ^ 1) for d in range(n)])  9.79 us
    unnamed x19, local copies, waits for them, and re-layouts  8.67 us
  transfers between devices with their start and end apart: 7, of which 7 were waited for; matrix products, arithmetic and copies ran while one was open for 0% of the time, Pallas kernels for 0%

profile of v7, /device:TPU:0, one launch (start us, length us, event | category | flops | bytes accessed | tf_op | source)
XLA Modules:
  0.0 422.1 jit_solution(17391040242949149163)
XLA Ops:
  1.3 0.8 concatenate.20
  2.0 0.8 copy.76
  2.9 0.7 broadcast_select_fusion
  3.6 1.0 fusion
  4.7 20.7 %all_to_all.60 = f32[4,65,1024]{2,1,0:T(8,128)S(1)} all-to-all(f32[4,65,1024]{2,1,0:T(8,128)S(1)} %broadcast_in_dim.89), channel_id=1, replica_groups={{0,2,4,6},{1,3,5,7},{8,10,12,14},{9,11,13,15},{16,18,20,22},{17,19,21,2..., dimensions={0} | all-to-all | bytes 2129920 | tf_op jit(solution)/shard_map/all_to_all | solution.py:51
  26.2 2.7 collective-permute-done
  31.0 1.5 slice-done.1
  32.6 7.4 %fusion.15 = f32[512,2048]{1,0:T(8,128)S(1)} fusion(f32[512,1024]{1,0:T(8,128)S(1)} %bitcast.98, f32[1024,2048]{1,0:T(8,128)S(1)} %bitcast.97), kind=kOutput, calls=%fused_computation.84 | convolution fusion | flops 6442450944 | bytes 14680064 | tf_op jit(solution)/shard_map/si,ij->sj/dot_general | solution.py:58
  40.0 59.1 %all_to_all.61 = f32[16,32,2048]{2,1,0:T(8,128)} all-to-all(f32[16,32,2048]{2,1,0:T(8,128)S(1)} %bitcast.89), channel_id=1, replica_groups=mesh['wide'=16,'col'=8] {'wide'}, dimensions={0} | all-to-all | bytes 8388608 | tf_op jit(solution)/shard_map/all_to_all | solution.py:22
  99.1 2.4 reduce_sum.63
  101.7 1.6 gather_fusion
  103.3 1.4 select_select_fusion.1
  104.8 0.8 dynamic-slice_bitcast_fusion.1
  105.6 2.2 collective-permute-done.1
  107.9 1.1 bitcast_add_fusion.3
  109.0 12.5 %all_to_all.62 = f32[4,8,32,128]{3,2,1,0:T(8,128)S(1)} all-to-all(f32[4,8,32,128]{3,2,1,0:T(8,128)S(1)} %bitcast_add_fusion.3), channel_id=1, replica_groups={{0,2,4,6},{1,3,5,7},{8,10,12,14},{9,11,13,15},{16,18,20,22},{17,19,21,2..., dimensions={0} | all-to-all | bytes 1048576 | tf_op jit(solution)/shard_map/all_to_all | solution.py:44
  121.8 30.9 %all_to_all.63 = f32[16,32,2,512]{3,1,2,0:T(8,128)S(1)} all-to-all(f32[16,32,2,512]{3,1,2,0:T(8,128)S(1)} %broadcast_in_dim.98), channel_id=1, replica_groups=mesh['wide'=16,'col'=8] {'wide'}, dimensions={0} | all-to-all | bytes 4194304 | tf_op jit(solution)/shard_map/all_to_all | solution.py:29
  152.9 1.4 copy-done.2
  154.2 2.0 fusion.16
  156.6 2.6 collective-permute-done.2
  159.5 18.1 %all_to_all.64 = f32[4,64,2,512]{3,1,2,0:T(8,128)S(1)} all-to-all(f32[4,64,2,512]{3,1,2,0:T(8,128)S(1)} %bitcast_add_fusion.1), channel_id=1, replica_groups={{0,2,4,6},{1,3,5,7},{8,10,12,14},{9,11,13,15},{16,18,20,22},{17,19,21,2..., dimensions={0} | all-to-all | bytes 2097152 | tf_op jit(solution)/shard_map/all_to_all | solution.py:44
  177.6 0.8 reduce_sum.65
  178.4 1.1 copy_subtract_fusion.1
  179.6 17.3 %all_to_all.65 = f32[4,64,2,512]{3,1,2,0:T(8,128)S(1)} all-to-all(f32[4,64,2,512]{3,1,2,0:T(8,128)S(1)} %broadcast_in_dim.99), channel_id=1, replica_groups={{0,2,4,6},{1,3,5,7},{8,10,12,14},{9,11,13,15},{16,18,20,22},{17,19,21,2..., dimensions={0} | all-to-all | bytes 2097152 | tf_op jit(solution)/shard_map/all_to_all | solution.py:51
  197.0 2.6 collective-permute-done.3
  199.9 2.0 copy-done.1
  201.9 3.6 fusion.17
  206.1 55.1 %all_to_all.66 = f32[16,32,2,1024]{3,1,2,0:T(8,128)} all-to-all(f32[16,32,2,1024]{3,1,2,0:T(8,128)S(1)} %copy.89), channel_id=1, replica_groups=mesh['wide'=16,'col'=8] {'wide'}, dimensions={0} | all-to-all | bytes 8388608 | tf_op jit(solution)/shard_map/all_to_all | solution.py:22
  261.2 2.5 reduce_sum.66
  264.6 1.6 gather_fusion.1
  266.3 1.4 select_select_fusion
  267.7 0.8 dynamic-slice_bitcast_fusion
  268.5 2.2 collective-permute-done.4
  270.8 1.1 bitcast_add_fusion.2
  271.9 12.5 %all_to_all.67 = f32[4,8,32,128]{3,2,1,0:T(8,128)S(1)} all-to-all(f32[4,8,32,128]{3,2,1,0:T(8,128)S(1)} %bitcast_add_fusion.2), channel_id=1, replica_groups={{0,2,4,6},{1,3,5,7},{8,10,12,14},{9,11,13,15},{16,18,20,22},{17,19,21,2..., dimensions={0} | all-to-all | bytes 1048576 | tf_op jit(solution)/shard_map/all_to_all | solution.py:44
  284.7 30.8 %all_to_all.68 = f32[16,32,4,256]{3,1,2,0:T(8,128)S(1)} all-to-all(f32[16,32,4,256]{3,1,2,0:T(8,128)S(1)} %broadcast_in_dim.106), channel_id=1, replica_groups=mesh['wide'=16,'col'=8] {'wide'}, dimensions={0} | all-to-all | bytes 4194304 | tf_op jit(solution)/shard_map/all_to_all | solution.py:29
  315.6 1.1 copy-done.3
  316.7 1.1 fusion.18
  318.3 2.6 collective-permute-done.5
  321.1 18.1 %all_to_all.69 = f32[4,64,4,256]{3,1,2,0:T(8,128)S(1)} all-to-all(f32[4,64,4,256]{3,1,2,0:T(8,128)S(1)} %bitcast_add_fusion), channel_id=1, replica_groups={{0,2,4,6},{1,3,5,7},{8,10,12,14},{9,11,13,15},{16,18,20,22},{17,19,21,2..., dimensions={0} | all-to-all | bytes 2097152 | tf_op jit(solution)/shard_map/all_to_all | solution.py:44
  339.3 1.0 copy_subtract_fusion
  340.4 17.3 %all_to_all.70 = f32[4,64,4,256]{3,1,2,0:T(8,128)S(1)} all-to-all(f32[4,64,4,256]{3,1,2,0:T(8,128)S(1)} %broadcast_in_dim.107), channel_id=1, replica_groups={{0,2,4,6},{1,3,5,7},{8,10,12,14},{9,11,13,15},{16,18,20,22},{17,19,21,2..., dimensions={0} | all-to-all | bytes 2097152 | tf_op jit(solution)/shard_map/all_to_all | solution.py:51
  357.9 2.6 collective-permute-done.6
  360.8 1.9 fusion.19
  362.7 0.8 copy.101
  363.5 55.1 %all_to_all.71 = f32[16,32,4,512]{3,1,2,0:T(8,128)} all-to-all(f32[16,32,4,512]{3,1,2,0:T(8,128)S(1)} %copy.101), channel_id=1, replica_groups=mesh['wide'=16,'col'=8] {'wide'}, dimensions={0} | all-to-all | bytes 8388608 | tf_op jit(solution)/shard_map/all_to_all | solution.py:22
  418.6 2.6 reduce_sum.69
  421.3 0.9 copy.104
  (70 shorter events, 8.8 us)
Async XLA Ops:
  0.6 360.2 %copy-start = (f32[4,256,512]{2,1,0:T(8,128)S(1)}, f32[4,256,512]{2,1,0:T(8,128)}, u32[]{:S(2)}) copy-start(f32[4,256,512]{2,1,0:T(8,128)} %param.17) | copy-start | bytes 6291460
  26.1 2.8 collective-permute-start
  28.9 2.2 slice-start
  29.9 2.7 slice-start.1
  101.5 1.8 copy-start.4
  105.6 2.3 collective-permute-start.1
  152.7 1.6 copy-start.2
  156.5 2.7 collective-permute-start.2
  196.9 2.7 collective-permute-start.3
  199.7 2.2 copy-start.1
  263.9 0.7 copy-start.5
  268.5 2.3 collective-permute-start.4
  315.4 1.2 copy-start.3
  318.0 3.0 collective-permute-start.5
  357.8 2.7 collective-permute-start.6

commit v8 on v7

--- a/solution.py
+++ b/solution.py
@@ -58,9 +58,16 @@
     return jnp.einsum(spec, lhs, rhs, precision=PRECISE, preferred_element_type=jnp.float32)
 
 
-def level(z_local, update_partial, inverse, cores):
+def level(z_local, near_rows, panel, spec, inverse, cores):
     n = lax.axis_size("col")
-    update = col_sum(update_partial.reshape((n, -1) + update_partial.shape[1:]), cores)
+    paired = near_rows.reshape((n // 2, 2, -1) + near_rows.shape[1:])
+    other = lax.dynamic_index_in_dim(paired, cores[1], axis=1, keepdims=False)
+    other = matmul(other.reshape((-1,) + other.shape[2:]), panel, spec)
+    sent = lax.ppermute(other.reshape((n // 2, -1) + other.shape[1:]), "col", [(d, d ^ 1) for d in range(n)])
+    mine = lax.dynamic_index_in_dim(paired, cores[0], axis=1, keepdims=False)
+    mine = matmul(mine.reshape((-1,) + mine.shape[2:]), panel, spec)
+    chip = mine.reshape(sent.shape) + sent
+    update = lax.all_to_all(chip, "col", 0, 0, tiled=False, axis_index_groups=chip_groups(n)).sum(0)
     right_side = col_gather(z_local - update, cores)
     right_side = right_side.reshape((-1,) + right_side.shape[2:])
     return exchange_sum(matmul(right_side, inverse, "ski,kij->skj"), "wide")
@@ -135,7 +142,7 @@
     near_local = send_blocks(root_tiles, child_owner, child_local, cores)
     near_local = rows_of(near_local, anc_child.shape[0], anc_child.shape[1] // n_col)
     near_rows = exchange_gather(near_local, "wide", 0)
-    x_child = level(z_child, matmul(near_rows, panel_child, "ska,kaj->skj"), inv_child, cores)
+    x_child = level(z_child, near_rows, panel_child, "ska,kaj->skj", inv_child, cores)
 
     x_child, owner, local, cores = lax.optimization_barrier((x_child, owner, local, cores))
     child_tiles = x_child.reshape(x_child.shape[0], kids * per_child, BLK).transpose(1, 0, 2)
@@ -143,7 +150,7 @@
     far_local = send_blocks(all_tiles, owner, local, cores)
     far_local = rows_of(far_local, anc_grand.shape[0], anc_grand.shape[1] // n_col)
     far_rows = exchange_gather(far_local, "wide", 0)
-    x_grand = level(z_grand, matmul(far_rows, panel_grand, "sga,gaj->sgj"), inv_grand, cores)
+    x_grand = level(z_grand, far_rows, panel_grand, "sga,gaj->sgj", inv_grand, cores)
     return (x_root, x_child, x_grand)
 
 

time: 423 us -> 422 us (level)
    all_to_all x4 -> x2, blocking collectives: 61.1 us -> 24.9 us  [col_sum(): lax.all_to_all(chip, 'col', 0, 0, tiled=False, axis_index_groups=chip_gro...]
    all_to_all x0 -> x2, blocking collectives: none -> 36.2 us  [level(): lax.all_to_all(chip, 'col', 0, 0, tiled=False, axis_index_groups=chip_gro...]
    ppermute x4 -> x2, waiting for transfers between devices: 9.79 us -> 4.5 us  [col_sum(): chip = mine + lax.ppermute(other, 'col', [(d, d ^ 1) for d in range(n)])]
    dot_general x5 -> x7, matrix products: 16 us -> 16.6 us  [matmul(): jnp.einsum(spec, lhs, rhs, precision=PRECISE, preferred_element_type=jnp....]
where the time goes in v8:
time: 422 us; the launch traced here: 421 us
  blocking collectives  347 us (82%)
  local copies, waits for them, and re-layouts  20 us (5%)
  other arithmetic  19.5 us (5%)
  matrix products  16.6 us (4%)
  waiting for transfers between devices  15.9 us (4%)
    all_to_all x3, blocking collectives, exchange_sum(): lax.all_to_all(partial.reshape((n, chunk) + partial.shape[1:]), axis, 0,...  169 us
    all_to_all x2, blocking collectives, exchange_gather(): parts = lax.all_to_all(stacked, axis, 0, 0, tiled=False)  61.7 us
    all_to_all x3, blocking collectives, col_gather(): lax.all_to_all(stacked, 'col', 0, 0, tiled=False, axis_index_groups=chip_...  55.2 us
    all_to_all x2, blocking collectives, level(): lax.all_to_all(chip, 'col', 0, 0, tiled=False, axis_index_groups=chip_gro...  36.2 us
    all_to_all x2, blocking collectives, col_sum(): lax.all_to_all(chip, 'col', 0, 0, tiled=False, axis_index_groups=chip_gro...  24.9 us
    dot_general x7, matrix products, matmul(): jnp.einsum(spec, lhs, rhs, precision=PRECISE, preferred_element_type=jnp....  16.6 us
    unnamed x19, local copies, waits for them, and re-layouts  8.57 us
  transfers between devices with their start and end apart: 7, of which 7 were waited for; matrix products, arithmetic and copies ran while one was open for 0% of the time, Pallas kernels for 0%

profile of v8, /device:TPU:0, one launch (start us, length us, event | category | flops | bytes accessed | tf_op | source)
XLA Modules:
  0.0 421.1 jit_solution(7184202809869395683)
XLA Ops:
  1.3 0.8 concatenate.20
  2.0 0.8 copy.76
  2.9 0.7 broadcast_select_fusion
  3.6 1.0 fusion
  4.7 20.7 %all_to_all.60 = f32[4,65,1024]{2,1,0:T(8,128)S(1)} all-to-all(f32[4,65,1024]{2,1,0:T(8,128)S(1)} %broadcast_in_dim.89), channel_id=1, replica_groups={{0,2,4,6},{1,3,5,7},{8,10,12,14},{9,11,13,15},{16,18,20,22},{17,19,21,2..., dimensions={0} | all-to-all | bytes 2129920 | tf_op jit(solution)/shard_map/all_to_all | solution.py:51
  26.2 2.7 collective-permute-done
  31.0 1.5 slice-done.1
  32.6 7.4 %fusion.15 = f32[512,2048]{1,0:T(8,128)S(1)} fusion(f32[512,1024]{1,0:T(8,128)S(1)} %bitcast.101, f32[1024,2048]{1,0:T(8,128)S(1)} %bitcast.100), kind=kOutput, calls=%fused_computation.82 | convolution fusion | flops 6442450944 | bytes 14680064 | tf_op jit(solution)/shard_map/si,ij->sj/dot_general | solution.py:58
  40.0 59.1 %all_to_all.61 = f32[16,32,2048]{2,1,0:T(8,128)} all-to-all(f32[16,32,2048]{2,1,0:T(8,128)S(1)} %bitcast.93), channel_id=1, replica_groups=mesh['wide'=16,'col'=8] {'wide'}, dimensions={0} | all-to-all | bytes 8388608 | tf_op jit(solution)/shard_map/all_to_all | solution.py:22
  99.1 2.4 reduce_sum.63
  101.7 1.6 gather_fusion
  103.3 1.4 select_select_fusion.1
  104.8 0.8 dynamic-slice_bitcast_fusion.1
  105.6 2.2 collective-permute-done.1
  107.9 1.1 bitcast_add_fusion.1
  109.0 12.5 %all_to_all.62 = f32[4,8,32,128]{3,2,1,0:T(8,128)S(1)} all-to-all(f32[4,8,32,128]{3,2,1,0:T(8,128)S(1)} %bitcast_add_fusion.1), channel_id=1, replica_groups={{0,2,4,6},{1,3,5,7},{8,10,12,14},{9,11,13,15},{16,18,20,22},{17,19,21,2..., dimensions={0} | all-to-all | bytes 1048576 | tf_op jit(solution)/shard_map/all_to_all | solution.py:44
  121.8 30.9 %all_to_all.63 = f32[16,32,2,512]{3,1,2,0:T(8,128)S(1)} all-to-all(f32[16,32,2,512]{3,1,2,0:T(8,128)S(1)} %broadcast_in_dim.98), channel_id=1, replica_groups=mesh['wide'=16,'col'=8] {'wide'}, dimensions={0} | all-to-all | bytes 4194304 | tf_op jit(solution)/shard_map/all_to_all | solution.py:29
  153.2 1.3 copy-done.1
  154.5 1.2 fusion.17
  155.9 1.2 fusion.16
  157.1 1.5 collective-permute-done.2
  158.8 18.1 %all_to_all.64 = f32[4,64,2,512]{3,1,2,0:T(8,128)S(1)} all-to-all(f32[4,64,2,512]{3,1,2,0:T(8,128)S(1)} %copy_add_fusion.1), channel_id=1, replica_groups={{0,2,4,6},{1,3,5,7},{8,10,12,14},{9,11,13,15},{16,18,20,22},{17,19,21,2..., dimensions={0} | all-to-all | bytes 2097152 | tf_op jit(solution)/shard_map/all_to_all | solution.py:70
  176.8 0.8 reduce_sum.65
  177.6 1.1 copy_subtract_fusion.1
  178.9 17.3 %all_to_all.65 = f32[4,64,2,512]{3,1,2,0:T(8,128)S(1)} all-to-all(f32[4,64,2,512]{3,1,2,0:T(8,128)S(1)} %broadcast_in_dim.99), channel_id=1, replica_groups={{0,2,4,6},{1,3,5,7},{8,10,12,14},{9,11,13,15},{16,18,20,22},{17,19,21,2..., dimensions={0} | all-to-all | bytes 2097152 | tf_op jit(solution)/shard_map/all_to_all | solution.py:51
  196.3 2.6 collective-permute-done.3
  199.2 2.0 copy-done.3
  201.1 3.6 fusion.18
  205.3 55.1 %all_to_all.66 = f32[16,32,2,1024]{3,1,2,0:T(8,128)} all-to-all(f32[16,32,2,1024]{3,1,2,0:T(8,128)S(1)} %copy.89), channel_id=1, replica_groups=mesh['wide'=16,'col'=8] {'wide'}, dimensions={0} | all-to-all | bytes 8388608 | tf_op jit(solution)/shard_map/all_to_all | solution.py:22
  260.4 2.5 reduce_sum.66
  263.9 1.6 gather_fusion.1
  265.5 1.4 select_select_fusion
  267.0 0.8 dynamic-slice_bitcast_fusion
  267.8 2.2 collective-permute-done.4
  270.1 1.1 bitcast_add_fusion
  271.2 12.5 %all_to_all.67 = f32[4,8,32,128]{3,2,1,0:T(8,128)S(1)} all-to-all(f32[4,8,32,128]{3,2,1,0:T(8,128)S(1)} %bitcast_add_fusion), channel_id=1, replica_groups={{0,2,4,6},{1,3,5,7},{8,10,12,14},{9,11,13,15},{16,18,20,22},{17,19,21,2..., dimensions={0} | all-to-all | bytes 1048576 | tf_op jit(solution)/shard_map/all_to_all | solution.py:44
  283.9 30.8 %all_to_all.68 = f32[16,32,4,256]{3,1,2,0:T(8,128)S(1)} all-to-all(f32[16,32,4,256]{3,1,2,0:T(8,128)S(1)} %broadcast_in_dim.106), channel_id=1, replica_groups=mesh['wide'=16,'col'=8] {'wide'}, dimensions={0} | all-to-all | bytes 4194304 | tf_op jit(solution)/shard_map/all_to_all | solution.py:29
  315.2 1.0 copy-done.2
  318.0 2.0 collective-permute-done.5
  320.1 18.1 %all_to_all.69 = f32[4,64,4,256]{3,1,2,0:T(8,128)S(1)} all-to-all(f32[4,64,4,256]{3,1,2,0:T(8,128)S(1)} %copy_add_fusion), channel_id=1, replica_groups={{0,2,4,6},{1,3,5,7},{8,10,12,14},{9,11,13,15},{16,18,20,22},{17,19,21,2..., dimensions={0} | all-to-all | bytes 2097152 | tf_op jit(solution)/shard_map/all_to_all | solution.py:70
  338.3 1.0 copy_subtract_fusion
  339.4 17.3 %all_to_all.70 = f32[4,64,4,256]{3,1,2,0:T(8,128)S(1)} all-to-all(f32[4,64,4,256]{3,1,2,0:T(8,128)S(1)} %broadcast_in_dim.107), channel_id=1, replica_groups={{0,2,4,6},{1,3,5,7},{8,10,12,14},{9,11,13,15},{16,18,20,22},{17,19,21,2..., dimensions={0} | all-to-all | bytes 2097152 | tf_op jit(solution)/shard_map/all_to_all | solution.py:51
  356.9 2.6 collective-permute-done.6
  359.8 1.9 fusion.21
  361.7 0.8 copy.101
  362.5 55.1 %all_to_all.71 = f32[16,32,4,512]{3,1,2,0:T(8,128)} all-to-all(f32[16,32,4,512]{3,1,2,0:T(8,128)S(1)} %copy.101), channel_id=1, replica_groups=mesh['wide'=16,'col'=8] {'wide'}, dimensions={0} | all-to-all | bytes 8388608 | tf_op jit(solution)/shard_map/all_to_all | solution.py:22
  417.6 2.6 reduce_sum.69
  420.2 0.9 copy.104
  (72 shorter events, 10.4 us)
Async XLA Ops:
  0.6 359.1 %copy-start = (f32[4,256,512]{2,1,0:T(8,128)S(1)}, f32[4,256,512]{2,1,0:T(8,128)}, u32[]{:S(2)}) copy-start(f32[4,256,512]{2,1,0:T(8,128)} %param.17) | copy-start | bytes 6291460
  26.1 2.8 collective-permute-start
  28.9 2.2 slice-start
  29.9 2.7 slice-start.1
  101.5 1.8 copy-start.4
  105.6 2.3 collective-permute-start.1
  152.9 1.6 copy-start.1
  155.8 2.7 collective-permute-start.2
  196.2 2.7 collective-permute-start.3
  198.9 2.2 copy-start.3
  263.2 0.7 copy-start.5
  267.8 2.3 collective-permute-start.4
  315.0 1.2 copy-start.2
  317.0 3.0 collective-permute-start.5
  356.8 2.7 collective-permute-start.6

commit v9 on v7

--- a/solution.py
+++ b/solution.py
@@ -35,11 +35,16 @@
     return [[2 * x + core for x in range(n // 2)] for core in range(2)]
 
 
+def pick_core(paired, index):
+    taken = lax.dynamic_slice_in_dim(paired, index, 1, axis=1, allow_negative_indices=False)
+    return taken.reshape(paired.shape[:1] + paired.shape[2:])
+
+
 def col_sum(chunks, cores):
     n = lax.axis_size("col")
     paired = chunks.reshape((n // 2, 2) + chunks.shape[1:])
-    mine = lax.dynamic_index_in_dim(paired, cores[0], axis=1, keepdims=False)
-    other = lax.dynamic_index_in_dim(paired, cores[1], axis=1, keepdims=False)
+    mine = pick_core(paired, cores[0])
+    other = pick_core(paired, cores[1])
     chip = mine + lax.ppermute(other, "col", [(d, d ^ 1) for d in range(n)])
     parts = lax.all_to_all(chip, "col", 0, 0, tiled=False, axis_index_groups=chip_groups(n))
     return parts.sum(0)
@@ -66,10 +71,22 @@
     return exchange_sum(matmul(right_side, inverse, "ski,kij->skj"), "wide")
 
 
-def send_blocks(tiles, mine, local, cores):
-    picked = jnp.take(tiles, local, axis=0)
-    outgoing = jnp.where(mine[:, :, None, None], picked, 0.0)
-    return col_sum(outgoing, cores)
+def send_blocks(tiles, tables):
+    other_mine, other_local, own_mine, own_local = tables
+    n = 2 * other_mine.shape[0]
+    other = jnp.where(other_mine[:, :, None, None], jnp.take(tiles, other_local, axis=0), 0.0)
+    sent = lax.ppermute(other, "col", [(d, d ^ 1) for d in range(n)])
+    own = jnp.where(own_mine[:, :, None, None], jnp.take(tiles, own_local, axis=0), 0.0)
+    parts = lax.all_to_all(own + sent, "col", 0, 0, tiled=False, axis_index_groups=chip_groups(n))
+    return parts.sum(0)
+
+
+def by_core(table, cores):
+    paired = table.reshape((table.shape[0] // 2, 2) + table.shape[1:])
+    return (
+        pick_core(paired, cores[1]),
+        pick_core(paired, cores[0]),
+    )
 
 
 def slots_of(blocks, per_device):
@@ -124,23 +141,27 @@
     owner = jnp.where(is_root, grand_slots // per_root, child_block // per_child)
     local = jnp.where(is_root, grand_slots % per_root, per_root + child_kid * per_child + child_block % per_child)
     child_owner, owner = child_owner == here, owner == here
-    root_right, child_owner, child_local, owner, local, cores = lax.optimization_barrier(
-        (root_right, child_owner, child_local, owner, local, cores)
+    child_tables = by_core(child_owner, cores) + by_core(child_local, cores)
+    child_tables = (child_tables[0], child_tables[2], child_tables[1], child_tables[3])
+    grand_tables = by_core(owner, cores) + by_core(local, cores)
+    grand_tables = (grand_tables[0], grand_tables[2], grand_tables[1], grand_tables[3])
+    root_right, child_tables, grand_tables, cores = lax.optimization_barrier(
+        (root_right, child_tables, grand_tables, cores)
     )
     x_root = exchange_sum(matmul(root_right, inv_root, "si,ij->sj"), "wide")
-    x_root, child_owner, child_local, owner, local, cores = lax.optimization_barrier(
-        (x_root, child_owner, child_local, owner, local, cores)
+    x_root, child_tables, grand_tables, cores = lax.optimization_barrier(
+        (x_root, child_tables, grand_tables, cores)
     )
     root_tiles = x_root.reshape(x_root.shape[0], per_root, BLK).transpose(1, 0, 2)
-    near_local = send_blocks(root_tiles, child_owner, child_local, cores)
+    near_local = send_blocks(root_tiles, child_tables)
     near_local = rows_of(near_local, anc_child.shape[0], anc_child.shape[1] // n_col)
     near_rows = exchange_gather(near_local, "wide", 0)
     x_child = level(z_child, matmul(near_rows, panel_child, "ska,kaj->skj"), inv_child, cores)
 
-    x_child, owner, local, cores = lax.optimization_barrier((x_child, owner, local, cores))
+    x_child, grand_tables, cores = lax.optimization_barrier((x_child, grand_tables, cores))
     child_tiles = x_child.reshape(x_child.shape[0], kids * per_child, BLK).transpose(1, 0, 2)
     all_tiles = jnp.concatenate([root_tiles, child_tiles], axis=0)
-    far_local = send_blocks(all_tiles, owner, local, cores)
+    far_local = send_blocks(all_tiles, grand_tables)
     far_local = rows_of(far_local, anc_grand.shape[0], anc_grand.shape[1] // n_col)
     far_rows = exchange_gather(far_local, "wide", 0)
     x_grand = level(z_grand, matmul(far_rows, panel_grand, "sga,gaj->sgj"), inv_grand, cores)

time: 423 us -> 420 us (level)
    all_to_all x0 -> x2, blocking collectives: none -> 24.9 us  [send_blocks(): lax.all_to_all(own + sent, 'col', 0, 0, tiled=False, axis_index_groups=ch...]
    all_to_all x4 -> x2, blocking collectives: 61.1 us -> 36.2 us  [col_sum(): lax.all_to_all(chip, 'col', 0, 0, tiled=False, axis_index_groups=chip_gro...]
    ppermute x4 -> x2, waiting for transfers between devices: 9.79 us -> 5.29 us  [col_sum(): chip = mine + lax.ppermute(other, 'col', [(d, d ^ 1) for d in range(n)])]
where the time goes in v9:
time: 420 us; the launch traced here: 419 us
  blocking collectives  347 us (83%)
  matrix products  18.6 us (4%)
  other arithmetic  17.9 us (4%)
  local copies, waits for them, and re-layouts  17.3 us (4%)
  waiting for transfers between devices  16.1 us (4%)
    all_to_all x3, blocking collectives, exchange_sum(): lax.all_to_all(partial.reshape((n, chunk) + partial.shape[1:]), axis, 0,...  169 us
    all_to_all x2, blocking collectives, exchange_gather(): parts = lax.all_to_all(stacked, axis, 0, 0, tiled=False)  61.7 us
    all_to_all x3, blocking collectives, col_gather(): lax.all_to_all(stacked, 'col', 0, 0, tiled=False, axis_index_groups=chip_...  55.2 us
    all_to_all x2, blocking collectives, col_sum(): lax.all_to_all(chip, 'col', 0, 0, tiled=False, axis_index_groups=chip_gro...  36.2 us
    all_to_all x2, blocking collectives, send_blocks(): lax.all_to_all(own + sent, 'col', 0, 0, tiled=False, axis_index_groups=ch...  24.9 us
    dot_general x5, matrix products, matmul(): jnp.einsum(spec, lhs, rhs, precision=PRECISE, preferred_element_type=jnp....  18.6 us
  transfers between devices with their start and end apart: 7, of which 7 were waited for; matrix products, arithmetic and copies ran while one was open for 0% of the time, Pallas kernels for 0%

profile of v9, /device:TPU:0, one launch (start us, length us, event | category | flops | bytes accessed | tf_op | source)
XLA Modules:
  0.0 419.0 jit_solution(9706508091219563511)
XLA Ops:
  0.6 0.6 compare_reduce_fusion
  1.3 0.8 concatenate.20
  2.0 0.8 copy.76
  2.9 0.7 broadcast_select_fusion
  3.6 1.0 fusion.2
  4.7 20.7 %all_to_all.60 = f32[4,65,1024]{2,1,0:T(8,128)S(1)} all-to-all(f32[4,65,1024]{2,1,0:T(8,128)S(1)} %broadcast_in_dim.91), channel_id=1, replica_groups={{0,2,4,6},{1,3,5,7},{8,10,12,14},{9,11,13,15},{16,18,20,22},{17,19,21,2..., dimensions={0} | all-to-all | bytes 2129920 | tf_op jit(solution)/shard_map/all_to_all | solution.py:56
  25.4 0.7 copy.77
  26.2 2.7 collective-permute-done
  28.9 0.6 copy.135
  30.1 1.5 slice.40
  31.9 10.0 %fusion.17 = f32[512,2048]{1,0:T(8,128)S(1)} fusion(f32[512,1024]{1,0:T(8,128)} %bitcast.108, f32[1024,2048]{1,0:T(8,128)} %param.19), kind=kOutput, calls=%fused_computation.104 | convolution fusion | flops 6442450944 | bytes 14680064 | tf_op jit(solution)/shard_map/si,ij->sj/dot_general | solution.py:63
  41.9 59.1 %all_to_all.61 = f32[16,32,2048]{2,1,0:T(8,128)} all-to-all(f32[16,32,2048]{2,1,0:T(8,128)S(1)} %bitcast.101), channel_id=1, replica_groups=mesh['wide'=16,'col'=8] {'wide'}, dimensions={0} | all-to-all | bytes 8388608 | tf_op jit(solution)/shard_map/all_to_all | solution.py:22
  101.0 2.4 reduce_sum.63
  104.2 0.6 gather_fusion.1
  105.7 1.3 collective-permute-done.1
  107.0 1.2 fusion.1
  108.2 12.5 %all_to_all.62 = f32[4,8,32,128]{3,2,1,0:T(8,128)S(1)} all-to-all(f32[4,8,32,128]{3,2,1,0:T(8,128)S(1)} %fusion.1), channel_id=1, replica_groups={{0,2,4,6},{1,3,5,7},{8,10,12,14},{9,11,13,15},{16,18,20,22},{17,19,21,2..., dimensions={0} | all-to-all | bytes 1048576 | tf_op jit(solution)/shard_map/all_to_all | solution.py:80
  121.0 30.9 %all_to_all.63 = f32[16,32,2,512]{3,1,2,0:T(8,128)S(1)} all-to-all(f32[16,32,2,512]{3,1,2,0:T(8,128)S(1)} %broadcast_in_dim.96), channel_id=1, replica_groups=mesh['wide'=16,'col'=8] {'wide'}, dimensions={0} | all-to-all | bytes 4194304 | tf_op jit(solution)/shard_map/all_to_all | solution.py:29
  152.1 1.4 copy-done.2
  153.5 2.0 fusion.18
  155.8 2.6 collective-permute-done.2
  158.7 18.1 %all_to_all.64 = f32[4,64,2,512]{3,1,2,0:T(8,128)S(1)} all-to-all(f32[4,64,2,512]{3,1,2,0:T(8,128)S(1)} %bitcast_add_fusion.1), channel_id=1, replica_groups={{0,2,4,6},{1,3,5,7},{8,10,12,14},{9,11,13,15},{16,18,20,22},{17,19,21,2..., dimensions={0} | all-to-all | bytes 2097152 | tf_op jit(solution)/shard_map/all_to_all | solution.py:49
  176.8 0.8 reduce_sum.65
  177.6 1.1 copy_subtract_fusion.1
  178.8 17.3 %all_to_all.65 = f32[4,64,2,512]{3,1,2,0:T(8,128)S(1)} all-to-all(f32[4,64,2,512]{3,1,2,0:T(8,128)S(1)} %broadcast_in_dim.97), channel_id=1, replica_groups={{0,2,4,6},{1,3,5,7},{8,10,12,14},{9,11,13,15},{16,18,20,22},{17,19,21,2..., dimensions={0} | all-to-all | bytes 2097152 | tf_op jit(solution)/shard_map/all_to_all | solution.py:56
  196.4 2.6 collective-permute-done.3
  199.3 2.0 copy-done.1
  201.3 3.6 fusion.19
  205.5 55.1 %all_to_all.66 = f32[16,32,2,1024]{3,1,2,0:T(8,128)} all-to-all(f32[16,32,2,1024]{3,1,2,0:T(8,128)S(1)} %copy.89), channel_id=1, replica_groups=mesh['wide'=16,'col'=8] {'wide'}, dimensions={0} | all-to-all | bytes 8388608 | tf_op jit(solution)/shard_map/all_to_all | solution.py:22
  260.6 2.5 reduce_sum.66
  264.6 0.9 select_select_fusion
  265.7 0.6 gather_fusion.2
  266.3 1.5 collective-permute-done.4
  267.8 1.2 fusion
  269.0 12.5 %all_to_all.67 = f32[4,8,32,128]{3,2,1,0:T(8,128)S(1)} all-to-all(f32[4,8,32,128]{3,2,1,0:T(8,128)S(1)} %fusion), channel_id=1, replica_groups={{0,2,4,6},{1,3,5,7},{8,10,12,14},{9,11,13,15},{16,18,20,22},{17,19,21,2..., dimensions={0} | all-to-all | bytes 1048576 | tf_op jit(solution)/shard_map/all_to_all | solution.py:80
  281.8 30.8 %all_to_all.68 = f32[16,32,4,256]{3,1,2,0:T(8,128)S(1)} all-to-all(f32[16,32,4,256]{3,1,2,0:T(8,128)S(1)} %broadcast_in_dim.101), channel_id=1, replica_groups=mesh['wide'=16,'col'=8] {'wide'}, dimensions={0} | all-to-all | bytes 4194304 | tf_op jit(solution)/shard_map/all_to_all | solution.py:29
  312.7 1.1 copy-done.3
  313.8 1.1 fusion.20
  315.2 2.6 collective-permute-done.5
  318.0 18.1 %all_to_all.69 = f32[4,64,4,256]{3,1,2,0:T(8,128)S(1)} all-to-all(f32[4,64,4,256]{3,1,2,0:T(8,128)S(1)} %bitcast_add_fusion), channel_id=1, replica_groups={{0,2,4,6},{1,3,5,7},{8,10,12,14},{9,11,13,15},{16,18,20,22},{17,19,21,2..., dimensions={0} | all-to-all | bytes 2097152 | tf_op jit(solution)/shard_map/all_to_all | solution.py:49
  336.2 1.0 copy_subtract_fusion
  337.3 17.3 %all_to_all.70 = f32[4,64,4,256]{3,1,2,0:T(8,128)S(1)} all-to-all(f32[4,64,4,256]{3,1,2,0:T(8,128)S(1)} %broadcast_in_dim.102), channel_id=1, replica_groups={{0,2,4,6},{1,3,5,7},{8,10,12,14},{9,11,13,15},{16,18,20,22},{17,19,21,2..., dimensions={0} | all-to-all | bytes 2097152 | tf_op jit(solution)/shard_map/all_to_all | solution.py:56
  354.8 2.6 collective-permute-done.6
  357.7 1.9 fusion.21
  359.6 0.8 copy.101
  360.4 55.1 %all_to_all.71 = f32[16,32,4,512]{3,1,2,0:T(8,128)} all-to-all(f32[16,32,4,512]{3,1,2,0:T(8,128)S(1)} %copy.101), channel_id=1, replica_groups=mesh['wide'=16,'col'=8] {'wide'}, dimensions={0} | all-to-all | bytes 8388608 | tf_op jit(solution)/shard_map/all_to_all | solution.py:22
  415.5 2.6 reduce_sum.69
  418.1 0.9 copy.104
  (77 shorter events, 8.2 us)
Async XLA Ops:
  0.6 357.1 %copy-start = (f32[4,256,512]{2,1,0:T(8,128)S(1)}, f32[4,256,512]{2,1,0:T(8,128)}, u32[]{:S(2)}) copy-start(f32[4,256,512]{2,1,0:T(8,128)} %param.21) | copy-start | bytes 6291460
  26.1 2.8 collective-permute-start
  103.4 0.7 copy-start.4
  104.9 2.1 collective-permute-start.1
  151.9 1.6 copy-start.2
  155.8 2.7 collective-permute-start.2
  196.2 2.9 collective-permute-start.3
  199.1 2.2 copy-start.1
  263.3 0.7 copy-start.5
  265.6 2.3 collective-permute-start.4
  312.5 1.2 copy-start.3
  315.1 2.7 collective-permute-start.5
  354.7 2.7 collective-permute-start.6

commit v10 on v9

--- a/solution.py
+++ b/solution.py
@@ -50,13 +50,21 @@
     return parts.sum(0)
 
 
-def col_gather(local, cores):
+def col_halves(local):
     n = lax.axis_size("col")
     stacked = jnp.broadcast_to(local[None], (n // 2,) + local.shape)
     same = lax.all_to_all(stacked, "col", 0, 0, tiled=False, axis_index_groups=chip_groups(n))
     other = lax.ppermute(same, "col", [(d, d ^ 1) for d in range(n)])
+    return same, other
+
+
+def col_join(same, other, cores):
     both = jnp.where(cores[2], jnp.stack([same, other], 1), jnp.stack([other, same], 1))
-    return both.reshape((n,) + local.shape)
+    return both.reshape((-1,) + same.shape[1:])
+
+
+def col_gather(local, cores):
+    return col_join(*col_halves(local), cores)
 
 
 def matmul(lhs, rhs, spec):
@@ -115,13 +123,14 @@
 ):
     n_col = lax.axis_size("col")
     lists = jnp.concatenate([anc_child.reshape(-1), anc_grand.reshape(-1)]).astype(jnp.float32)
-    extra = jnp.zeros((1, z_root.shape[1]), jnp.float32).at[0, : lists.shape[0]].set(lists)
+    extra = jnp.zeros((8, z_root.shape[1]), jnp.float32).at[0, : lists.shape[0]].set(lists)
     here = lax.axis_index("col")
     cores = (here % 2, 1 - here % 2, here % 2 == 0)
     with_lists, here, cores = lax.optimization_barrier((jnp.concatenate([z_root, extra], axis=0)[None], here, cores))
-    stacked = col_gather(with_lists[0], cores)
-    root_right = stacked[:, :-1].reshape(-1, z_root.shape[1])
-    got = stacked[:, -1, : lists.shape[0]].astype(jnp.int32)
+    same, other = col_halves(with_lists[0])
+    rows = z_root.shape[0]
+    root_right = col_join(same[:, :rows], other[:, :rows], cores).reshape(-1, z_root.shape[1])
+    got = col_join(same[:, rows : rows + 1], other[:, rows : rows + 1], cores)[:, 0, : lists.shape[0]].astype(jnp.int32)
     split = anc_child.size
     anc_child = got[:, :split].reshape((n_col,) + anc_child.shape).transpose(1, 0, 2).reshape(anc_child.shape[0], -1)
     anc_grand = got[:, split:].reshape((n_col,) + anc_grand.shape).transpose(1, 0, 2).reshape(anc_grand.shape[0], -1)

time: 420 us -> 418 us (level)
  no operation moved by 1% of the time
where the time goes in v10:
time: 418 us; the launch traced here: 417 us
  blocking collectives  347 us (83%)
  matrix products  17.9 us (4%)
  local copies, waits for them, and re-layouts  16.9 us (4%)
  other arithmetic  16.4 us (4%)
  waiting for transfers between devices  16.2 us (4%)
    all_to_all x3, blocking collectives, exchange_sum(): lax.all_to_all(partial.reshape((n, chunk) + partial.shape[1:]), axis, 0,...  169 us
    all_to_all x2, blocking collectives, exchange_gather(): parts = lax.all_to_all(stacked, axis, 0, 0, tiled=False)  61.7 us
    all_to_all x3, blocking collectives, col_halves(): lax.all_to_all(stacked, 'col', 0, 0, tiled=False, axis_index_groups=chip_...  55.1 us
    all_to_all x2, blocking collectives, col_sum(): lax.all_to_all(chip, 'col', 0, 0, tiled=False, axis_index_groups=chip_gro...  36.2 us
    all_to_all x2, blocking collectives, send_blocks(): lax.all_to_all(own + sent, 'col', 0, 0, tiled=False, axis_index_groups=ch...  24.9 us
    dot_general x5, matrix products, matmul(): jnp.einsum(spec, lhs, rhs, precision=PRECISE, preferred_element_type=jnp....  17.9 us
  transfers between devices with their start and end apart: 7, of which 7 were waited for; matrix products, arithmetic and copies ran while one was open for 0% of the time, Pallas kernels for 0%

profile of v10, /device:TPU:0, one launch (start us, length us, event | category | flops | bytes accessed | tf_op | source)
XLA Modules:
  0.0 416.5 jit_solution(13172442121012557023)
XLA Ops:
  0.7 0.9 concatenate.24
  1.6 0.8 copy.48
  2.5 1.0 fusion.2
  3.6 20.5 %all_to_all.60 = f32[4,72,1024]{2,1,0:T(8,128)S(1)} all-to-all(f32[4,72,1024]{2,1,0:T(8,128)S(1)} %broadcast_in_dim.91), channel_id=1, replica_groups={{0,2,4,6},{1,3,5,7},{8,10,12,14},{9,11,13,15},{16,18,20,22},{17,19,21,2..., dimensions={0} | all-to-all | bytes 2359296 | tf_op jit(solution)/shard_map/all_to_all | solution.py:56
  24.2 2.8 collective-permute-done
  27.0 1.0 copy-done.6
  28.4 1.3 slice_bitcast_fusion
  29.9 9.4 %fusion.18 = f32[512,2048]{1,0:T(8,128)S(1)} fusion(f32[512,1024]{1,0:T(8,128)S(1)} %bitcast.111, f32[1024,2048]{1,0:T(8,128)} %param.19), kind=kOutput, calls=%fused_computation.107 | convolution fusion | flops 6442450944 | bytes 14680064 | tf_op jit(solution)/shard_map/si,ij->sj/dot_general | solution.py:71
  39.3 59.3 %all_to_all.61 = f32[16,32,2048]{2,1,0:T(8,128)} all-to-all(f32[16,32,2048]{2,1,0:T(8,128)S(1)} %bitcast.107), channel_id=1, replica_groups=mesh['wide'=16,'col'=8] {'wide'}, dimensions={0} | all-to-all | bytes 8388608 | tf_op jit(solution)/shard_map/all_to_all | solution.py:22
  98.5 2.4 reduce_sum.63
  101.1 0.6 copy-done.4
  101.7 0.6 gather_fusion.1
  102.6 0.6 gather_fusion
  103.2 1.3 collective-permute-done.1
  104.6 1.2 fusion.1
  105.7 12.5 %all_to_all.62 = f32[4,8,32,128]{3,2,1,0:T(8,128)S(1)} all-to-all(f32[4,8,32,128]{3,2,1,0:T(8,128)S(1)} %fusion.1), channel_id=1, replica_groups={{0,2,4,6},{1,3,5,7},{8,10,12,14},{9,11,13,15},{16,18,20,22},{17,19,21,2..., dimensions={0} | all-to-all | bytes 1048576 | tf_op jit(solution)/shard_map/all_to_all | solution.py:88
  118.5 30.9 %all_to_all.63 = f32[16,32,2,512]{3,1,2,0:T(8,128)S(1)} all-to-all(f32[16,32,2,512]{3,1,2,0:T(8,128)S(1)} %broadcast_in_dim.96), channel_id=1, replica_groups=mesh['wide'=16,'col'=8] {'wide'}, dimensions={0} | all-to-all | bytes 4194304 | tf_op jit(solution)/shard_map/all_to_all | solution.py:29
  149.6 1.4 copy-done.2
  151.0 2.0 fusion.19
  153.4 2.6 collective-permute-done.2
  156.2 18.1 %all_to_all.64 = f32[4,64,2,512]{3,1,2,0:T(8,128)S(1)} all-to-all(f32[4,64,2,512]{3,1,2,0:T(8,128)S(1)} %bitcast_add_fusion.1), channel_id=1, replica_groups={{0,2,4,6},{1,3,5,7},{8,10,12,14},{9,11,13,15},{16,18,20,22},{17,19,21,2..., dimensions={0} | all-to-all | bytes 2097152 | tf_op jit(solution)/shard_map/all_to_all | solution.py:49
  174.3 0.8 reduce_sum.65
  175.1 1.1 copy_subtract_fusion.1
  176.3 17.3 %all_to_all.65 = f32[4,64,2,512]{3,1,2,0:T(8,128)S(1)} all-to-all(f32[4,64,2,512]{3,1,2,0:T(8,128)S(1)} %broadcast_in_dim.97), channel_id=1, replica_groups={{0,2,4,6},{1,3,5,7},{8,10,12,14},{9,11,13,15},{16,18,20,22},{17,19,21,2..., dimensions={0} | all-to-all | bytes 2097152 | tf_op jit(solution)/shard_map/all_to_all | solution.py:56
  194.0 2.6 collective-permute-done.3
  196.8 2.0 copy-done.1
  198.8 3.6 fusion.20
  203.0 55.1 %all_to_all.66 = f32[16,32,2,1024]{3,1,2,0:T(8,128)} all-to-all(f32[16,32,2,1024]{3,1,2,0:T(8,128)S(1)} %copy.58), channel_id=1, replica_groups=mesh['wide'=16,'col'=8] {'wide'}, dimensions={0} | all-to-all | bytes 8388608 | tf_op jit(solution)/shard_map/all_to_all | solution.py:22
  258.1 2.5 reduce_sum.66
  261.6 0.6 gather_fusion.3
  262.2 0.9 select_select_fusion
  263.2 0.6 gather_fusion.2
  263.8 1.5 collective-permute-done.4
  265.3 1.2 fusion
  266.5 12.5 %all_to_all.67 = f32[4,8,32,128]{3,2,1,0:T(8,128)S(1)} all-to-all(f32[4,8,32,128]{3,2,1,0:T(8,128)S(1)} %fusion), channel_id=1, replica_groups={{0,2,4,6},{1,3,5,7},{8,10,12,14},{9,11,13,15},{16,18,20,22},{17,19,21,2..., dimensions={0} | all-to-all | bytes 1048576 | tf_op jit(solution)/shard_map/all_to_all | solution.py:88
  279.3 30.8 %all_to_all.68 = f32[16,32,4,256]{3,1,2,0:T(8,128)S(1)} all-to-all(f32[16,32,4,256]{3,1,2,0:T(8,128)S(1)} %broadcast_in_dim.101), channel_id=1, replica_groups=mesh['wide'=16,'col'=8] {'wide'}, dimensions={0} | all-to-all | bytes 4194304 | tf_op jit(solution)/shard_map/all_to_all | solution.py:29
  310.2 1.1 copy-done.3
  311.3 1.1 fusion.21
  312.7 2.6 collective-permute-done.5
  315.5 18.1 %all_to_all.69 = f32[4,64,4,256]{3,1,2,0:T(8,128)S(1)} all-to-all(f32[4,64,4,256]{3,1,2,0:T(8,128)S(1)} %bitcast_add_fusion), channel_id=1, replica_groups={{0,2,4,6},{1,3,5,7},{8,10,12,14},{9,11,13,15},{16,18,20,22},{17,19,21,2..., dimensions={0} | all-to-all | bytes 2097152 | tf_op jit(solution)/shard_map/all_to_all | solution.py:49
  333.7 1.0 copy_subtract_fusion
  334.8 17.3 %all_to_all.70 = f32[4,64,4,256]{3,1,2,0:T(8,128)S(1)} all-to-all(f32[4,64,4,256]{3,1,2,0:T(8,128)S(1)} %broadcast_in_dim.102), channel_id=1, replica_groups={{0,2,4,6},{1,3,5,7},{8,10,12,14},{9,11,13,15},{16,18,20,22},{17,19,21,2..., dimensions={0} | all-to-all | bytes 2097152 | tf_op jit(solution)/shard_map/all_to_all | solution.py:56
  352.3 2.6 collective-permute-done.6
  355.2 1.9 fusion.22
  357.1 0.8 copy.70
  357.9 55.1 %all_to_all.71 = f32[16,32,4,512]{3,1,2,0:T(8,128)} all-to-all(f32[16,32,4,512]{3,1,2,0:T(8,128)S(1)} %copy.70), channel_id=1, replica_groups=mesh['wide'=16,'col'=8] {'wide'}, dimensions={0} | all-to-all | bytes 8388608 | tf_op jit(solution)/shard_map/all_to_all | solution.py:22
  413.0 2.6 reduce_sum.69
  415.7 0.9 copy.73
  (80 shorter events, 6.3 us)
Async XLA Ops:
  0.6 354.6 %copy-start = (f32[4,256,512]{2,1,0:T(8,128)S(1)}, f32[4,256,512]{2,1,0:T(8,128)}, u32[]{:S(2)}) copy-start(f32[4,256,512]{2,1,0:T(8,128)} %param.21) | copy-start | bytes 6291460
  24.1 2.8 collective-permute-start
  27.0 1.0 copy-start.6
  101.0 0.7 copy-start.4
  102.4 2.1 collective-permute-start.1
  149.4 1.6 copy-start.2
  153.3 2.7 collective-permute-start.2
  193.7 2.9 collective-permute-start.3
  196.6 2.2 copy-start.1
  260.8 0.7 copy-start.5
  263.1 2.3 collective-permute-start.4
  310.1 1.2 copy-start.3
  312.7 2.7 collective-permute-start.5
  352.2 2.7 collective-permute-start.6

commit v11 on v10

--- a/solution.py
+++ b/solution.py
@@ -122,18 +122,22 @@
     anc_grand,
 ):
     n_col = lax.axis_size("col")
-    lists = jnp.concatenate([anc_child.reshape(-1), anc_grand.reshape(-1)]).astype(jnp.float32)
-    extra = jnp.zeros((8, z_root.shape[1]), jnp.float32).at[0, : lists.shape[0]].set(lists)
+    child_list = anc_child.reshape(-1).astype(jnp.float32)
+    grand_list = anc_grand.reshape(-1).astype(jnp.float32)
+    width = z_root.shape[1]
+    extra = jnp.stack(
+        [jnp.pad(child_list, (0, width - child_list.shape[0])), jnp.pad(grand_list, (0, width - grand_list.shape[0]))]
+        + [jnp.zeros((width,), jnp.float32)] * 6
+    )
     here = lax.axis_index("col")
     cores = (here % 2, 1 - here % 2, here % 2 == 0)
     with_lists, here, cores = lax.optimization_barrier((jnp.concatenate([z_root, extra], axis=0)[None], here, cores))
     same, other = col_halves(with_lists[0])
     rows = z_root.shape[0]
     root_right = col_join(same[:, :rows], other[:, :rows], cores).reshape(-1, z_root.shape[1])
-    got = col_join(same[:, rows : rows + 1], other[:, rows : rows + 1], cores)[:, 0, : lists.shape[0]].astype(jnp.int32)
-    split = anc_child.size
-    anc_child = got[:, :split].reshape((n_col,) + anc_child.shape).transpose(1, 0, 2).reshape(anc_child.shape[0], -1)
-    anc_grand = got[:, split:].reshape((n_col,) + anc_grand.shape).transpose(1, 0, 2).reshape(anc_grand.shape[0], -1)
+    got = col_join(same[:, rows : rows + 2], other[:, rows : rows + 2], cores).astype(jnp.int32)
+    anc_child = got[:, 0, : anc_child.size].reshape((n_col,) + anc_child.shape).transpose(1, 0, 2).reshape(anc_child.shape[0], -1)
+    anc_grand = got[:, 1, : anc_grand.size].reshape((n_col,) + anc_grand.shape).transpose(1, 0, 2).reshape(anc_grand.shape[0], -1)
     width = inv_root.shape[1]
     per_root = width // BLK
     kids, child_width = inv_child.shape[0], inv_child.shape[2]

time: 418 us -> 416 us (level)
  no operation moved by 1% of the time
where the time goes in v11:
time: 416 us; the launch traced here: 415 us
  blocking collectives  347 us (83%)
  other arithmetic  17.2 us (4%)
  local copies, waits for them, and re-layouts  16.3 us (4%)
  waiting for transfers between devices  16.2 us (4%)
  matrix products  16 us (4%)
    all_to_all x3, blocking collectives, exchange_sum(): lax.all_to_all(partial.reshape((n, chunk) + partial.shape[1:]), axis, 0,...  169 us
    all_to_all x2, blocking collectives, exchange_gather(): parts = lax.all_to_all(stacked, axis, 0, 0, tiled=False)  61.7 us
    all_to_all x3, blocking collectives, col_halves(): lax.all_to_all(stacked, 'col', 0, 0, tiled=False, axis_index_groups=chip_...  55.1 us
    all_to_all x2, blocking collectives, col_sum(): lax.all_to_all(chip, 'col', 0, 0, tiled=False, axis_index_groups=chip_gro...  36.2 us
    all_to_all x2, blocking collectives, send_blocks(): lax.all_to_all(own + sent, 'col', 0, 0, tiled=False, axis_index_groups=ch...  24.9 us
    dot_general x5, matrix products, matmul(): jnp.einsum(spec, lhs, rhs, precision=PRECISE, preferred_element_type=jnp....  16 us
  transfers between devices with their start and end apart: 7, of which 7 were waited for; matrix products, arithmetic and copies ran while one was open for 0% of the time, Pallas kernels for 0%

profile of v11, /device:TPU:0, one launch (start us, length us, event | category | flops | bytes accessed | tf_op | source)
XLA Modules:
  0.0 415.1 jit_solution(6320148088831694818)
XLA Ops:
  0.7 0.8 convert_element_type.21
  1.6 0.7 convert_element_type.23
  2.5 1.0 concatenate.14
  3.6 20.5 %all_to_all.60 = f32[4,72,1024]{2,1,0:T(8,128)S(1)} all-to-all(f32[4,72,1024]{2,1,0:T(8,128)S(1)} %broadcast_in_dim.90), channel_id=1, replica_groups={{0,2,4,6},{1,3,5,7},{8,10,12,14},{9,11,13,15},{16,18,20,22},{17,19,21,2..., dimensions={0} | all-to-all | bytes 2359296 | tf_op jit(solution)/shard_map/all_to_all | solution.py:56
  24.1 0.8 copy.106
  25.1 2.7 collective-permute-done
  27.9 0.7 maximum_select_fusion
  28.6 1.2 copy.108
  30.2 7.4 %fusion.9 = f32[512,2048]{1,0:T(8,128)S(1)} fusion(f32[512,1024]{1,0:T(8,128)S(1)} %bitcast.111, f32[1024,2048]{1,0:T(8,128)S(1)} %bitcast.110), kind=kOutput, calls=%fused_computation.95 | convolution fusion | flops 6442450944 | bytes 14680064 | tf_op jit(solution)/shard_map/si,ij->sj/dot_general | solution.py:71
  37.6 59.3 %all_to_all.61 = f32[16,32,2048]{2,1,0:T(8,128)} all-to-all(f32[16,32,2048]{2,1,0:T(8,128)S(1)} %bitcast.105), channel_id=1, replica_groups=mesh['wide'=16,'col'=8] {'wide'}, dimensions={0} | all-to-all | bytes 8388608 | tf_op jit(solution)/shard_map/all_to_all | solution.py:22
  96.9 2.4 reduce_sum.63
  100.0 0.6 gather_fusion.1
  101.0 0.6 gather_fusion
  101.6 1.3 collective-permute-done.1
  102.9 1.2 fusion.1
  104.1 12.5 %all_to_all.62 = f32[4,8,32,128]{3,2,1,0:T(8,128)S(1)} all-to-all(f32[4,8,32,128]{3,2,1,0:T(8,128)S(1)} %fusion.1), channel_id=1, replica_groups={{0,2,4,6},{1,3,5,7},{8,10,12,14},{9,11,13,15},{16,18,20,22},{17,19,21,2..., dimensions={0} | all-to-all | bytes 1048576 | tf_op jit(solution)/shard_map/all_to_all | solution.py:88
  116.9 31.0 %all_to_all.63 = f32[16,32,2,512]{3,1,2,0:T(8,128)S(1)} all-to-all(f32[16,32,2,512]{3,1,2,0:T(8,128)S(1)} %broadcast_in_dim.95), channel_id=1, replica_groups=mesh['wide'=16,'col'=8] {'wide'}, dimensions={0} | all-to-all | bytes 4194304 | tf_op jit(solution)/shard_map/all_to_all | solution.py:29
  148.1 1.4 copy-done.2
  149.4 2.0 fusion.10
  151.8 2.6 collective-permute-done.2
  154.7 18.1 %all_to_all.64 = f32[4,64,2,512]{3,1,2,0:T(8,128)S(1)} all-to-all(f32[4,64,2,512]{3,1,2,0:T(8,128)S(1)} %bitcast_add_fusion.1), channel_id=1, replica_groups={{0,2,4,6},{1,3,5,7},{8,10,12,14},{9,11,13,15},{16,18,20,22},{17,19,21,2..., dimensions={0} | all-to-all | bytes 2097152 | tf_op jit(solution)/shard_map/all_to_all | solution.py:49
  172.8 0.8 reduce_sum.65
  173.6 1.1 copy_subtract_fusion.1
  174.8 17.3 %all_to_all.65 = f32[4,64,2,512]{3,1,2,0:T(8,128)S(1)} all-to-all(f32[4,64,2,512]{3,1,2,0:T(8,128)S(1)} %broadcast_in_dim.96), channel_id=1, replica_groups={{0,2,4,6},{1,3,5,7},{8,10,12,14},{9,11,13,15},{16,18,20,22},{17,19,21,2..., dimensions={0} | all-to-all | bytes 2097152 | tf_op jit(solution)/shard_map/all_to_all | solution.py:56
  192.2 2.6 collective-permute-done.3
  195.1 2.0 copy-done.1
  197.1 3.6 fusion.11
  201.3 55.1 %all_to_all.66 = f32[16,32,2,1024]{3,1,2,0:T(8,128)} all-to-all(f32[16,32,2,1024]{3,1,2,0:T(8,128)S(1)} %copy.120), channel_id=1, replica_groups=mesh['wide'=16,'col'=8] {'wide'}, dimensions={0} | all-to-all | bytes 8388608 | tf_op jit(solution)/shard_map/all_to_all | solution.py:22
  256.4 2.5 reduce_sum.66
  259.8 0.6 gather_fusion.3
  260.4 0.9 select_select_fusion
  261.5 0.6 gather_fusion.2
  262.1 1.5 collective-permute-done.4
  263.6 1.2 fusion
  264.8 12.5 %all_to_all.67 = f32[4,8,32,128]{3,2,1,0:T(8,128)S(1)} all-to-all(f32[4,8,32,128]{3,2,1,0:T(8,128)S(1)} %fusion), channel_id=1, replica_groups={{0,2,4,6},{1,3,5,7},{8,10,12,14},{9,11,13,15},{16,18,20,22},{17,19,21,2..., dimensions={0} | all-to-all | bytes 1048576 | tf_op jit(solution)/shard_map/all_to_all | solution.py:88
  277.6 30.8 %all_to_all.68 = f32[16,32,4,256]{3,1,2,0:T(8,128)S(1)} all-to-all(f32[16,32,4,256]{3,1,2,0:T(8,128)S(1)} %broadcast_in_dim.100), channel_id=1, replica_groups=mesh['wide'=16,'col'=8] {'wide'}, dimensions={0} | all-to-all | bytes 4194304 | tf_op jit(solution)/shard_map/all_to_all | solution.py:29
  308.5 1.1 copy-done.3
  309.6 1.1 fusion.12
  311.2 2.6 collective-permute-done.5
  314.0 18.1 %all_to_all.69 = f32[4,64,4,256]{3,1,2,0:T(8,128)S(1)} all-to-all(f32[4,64,4,256]{3,1,2,0:T(8,128)S(1)} %bitcast_add_fusion), channel_id=1, replica_groups={{0,2,4,6},{1,3,5,7},{8,10,12,14},{9,11,13,15},{16,18,20,22},{17,19,21,2..., dimensions={0} | all-to-all | bytes 2097152 | tf_op jit(solution)/shard_map/all_to_all | solution.py:49
  332.2 1.0 copy_subtract_fusion
  333.3 17.3 %all_to_all.70 = f32[4,64,4,256]{3,1,2,0:T(8,128)S(1)} all-to-all(f32[4,64,4,256]{3,1,2,0:T(8,128)S(1)} %broadcast_in_dim.101), channel_id=1, replica_groups={{0,2,4,6},{1,3,5,7},{8,10,12,14},{9,11,13,15},{16,18,20,22},{17,19,21,2..., dimensions={0} | all-to-all | bytes 2097152 | tf_op jit(solution)/shard_map/all_to_all | solution.py:56
  350.8 2.6 collective-permute-done.6
  353.7 1.9 fusion.13
  355.6 0.8 copy.132
  356.4 55.1 %all_to_all.71 = f32[16,32,4,512]{3,1,2,0:T(8,128)} all-to-all(f32[16,32,4,512]{3,1,2,0:T(8,128)S(1)} %copy.132), channel_id=1, replica_groups=mesh['wide'=16,'col'=8] {'wide'}, dimensions={0} | all-to-all | bytes 8388608 | tf_op jit(solution)/shard_map/all_to_all | solution.py:22
  411.5 2.6 reduce_sum.69
  414.2 0.9 copy.135
  (90 shorter events, 6.9 us)
Async XLA Ops:
  0.6 353.1 %copy-start = (f32[4,256,512]{2,1,0:T(8,128)S(1)}, f32[4,256,512]{2,1,0:T(8,128)}, u32[]{:S(2)}) copy-start(f32[4,256,512]{2,1,0:T(8,128)} %param.19) | copy-start | bytes 6291460
  24.1 6.0 %slice-start = ((s8[8388608]{0:T(1024)(128)(4,1)}), s8[4194304]{0:T(1024)(128)(4,1)S(1)}, s32[]{:S(2)}) async-start(s8[8388608]{0:T(1024)(128)(4,1)} %bitcast.109), calls=%async_computation.12 | async-start | bytes 8388608
  24.9 2.9 collective-permute-start
  27.9 2.3 slice-start.1
  99.3 0.7 copy-start.4
  100.8 2.1 collective-permute-start.1
  147.8 1.6 copy-start.2
  151.7 2.7 collective-permute-start.2
  192.1 2.7 collective-permute-start.3
  194.9 2.2 copy-start.1
  259.1 0.7 copy-start.5
  261.4 2.3 collective-permute-start.4
  308.3 1.2 copy-start.3
  310.9 3.0 collective-permute-start.5
  350.7 2.7 collective-permute-start.6

commit v12 on v11

--- a/solution.py
+++ b/solution.py
@@ -16,11 +16,17 @@
     return selected.reshape(leading, blocks.shape[0], blocks.shape[1] * BLK)
 
 
+def add_up(parts):
+    n = parts.shape[0]
+    grouped = parts.reshape((n // 4, 4) + parts.shape[1:]).sum(1)
+    return lax.optimization_barrier(grouped).sum(0)
+
+
 def exchange_sum(partial, axis):
     n = lax.axis_size(axis)
     chunk = partial.shape[0] // n
     parts = lax.all_to_all(partial.reshape((n, chunk) + partial.shape[1:]), axis, 0, 0, tiled=False)
-    return parts.sum(0)
+    return add_up(parts)
 
 
 def exchange_gather(local, axis, dim):

time: 416 us -> 410 us (0.986)
  other arithmetic: 17.2 us -> 12.8 us
    reduce_sum x3 -> x6, other arithmetic: 7.53 us -> 2.31 us  [the longest x3 1.37 us: add_up(): grouped = parts.reshape((n // 4, 4) + parts.shape[1:]).sum(1)]
where the time goes in v12:
time: 410 us; the launch traced here: 409 us
  blocking collectives  345 us (84%)
  local copies, waits for them, and re-layouts  16.8 us (4%)
  waiting for transfers between devices  16.4 us (4%)
  matrix products  16 us (4%)
  other arithmetic  12.8 us (3%)
    all_to_all x3, blocking collectives, exchange_sum(): lax.all_to_all(partial.reshape((n, chunk) + partial.shape[1:]), axis, 0,...  167 us
    all_to_all x2, blocking collectives, exchange_gather(): parts = lax.all_to_all(stacked, axis, 0, 0, tiled=False)  61.8 us
    all_to_all x3, blocking collectives, col_halves(): lax.all_to_all(stacked, 'col', 0, 0, tiled=False, axis_index_groups=chip_...  55.1 us
    all_to_all x2, blocking collectives, col_sum(): lax.all_to_all(chip, 'col', 0, 0, tiled=False, axis_index_groups=chip_gro...  36.2 us
    all_to_all x2, blocking collectives, send_blocks(): lax.all_to_all(own + sent, 'col', 0, 0, tiled=False, axis_index_groups=ch...  24.9 us
    dot_general x5, matrix products, matmul(): jnp.einsum(spec, lhs, rhs, precision=PRECISE, preferred_element_type=jnp....  16 us
  transfers between devices with their start and end apart: 7, of which 7 were waited for; matrix products, arithmetic and copies ran while one was open for 0% of the time, Pallas kernels for 0%

profile of v12, /device:TPU:0, one launch (start us, length us, event | category | flops | bytes accessed | tf_op | source)
XLA Modules:
  0.0 409.0 jit_solution(3514483953971278182)
XLA Ops:
  0.7 0.8 convert_element_type.21
  1.6 0.7 convert_element_type.23
  2.5 1.0 concatenate.14
  3.6 20.5 %all_to_all.60 = f32[4,72,1024]{2,1,0:T(8,128)S(1)} all-to-all(f32[4,72,1024]{2,1,0:T(8,128)S(1)} %broadcast_in_dim.90), channel_id=1, replica_groups={{0,2,4,6},{1,3,5,7},{8,10,12,14},{9,11,13,15},{16,18,20,22},{17,19,21,2..., dimensions={0} | all-to-all | bytes 2359296 | tf_op jit(solution)/shard_map/all_to_all | solution.py:62
  24.1 0.8 copy.127
  25.1 2.7 collective-permute-done
  27.9 0.7 maximum_select_fusion
  28.6 1.2 copy.129
  30.2 7.4 %fusion.9 = f32[512,2048]{1,0:T(8,128)S(1)} fusion(f32[512,1024]{1,0:T(8,128)S(1)} %bitcast.117, f32[1024,2048]{1,0:T(8,128)S(1)} %bitcast.116), kind=kOutput, calls=%fused_computation.98 | convolution fusion | flops 6442450944 | bytes 14680064 | tf_op jit(solution)/shard_map/si,ij->sj/dot_general | solution.py:77
  37.6 59.2 %all_to_all.61 = f32[16,32,2048]{2,1,0:T(8,128)S(1)} all-to-all(f32[16,32,2048]{2,1,0:T(8,128)S(1)} %bitcast.111), channel_id=1, replica_groups=mesh['wide'=16,'col'=8] {'wide'}, dimensions={0} | all-to-all | bytes 8388608 | tf_op jit(solution)/shard_map/all_to_all | solution.py:28
  97.4 0.6 gather_fusion.1
  98.0 0.9 select_select_fusion.2
  99.0 0.6 gather_fusion
  99.6 1.5 collective-permute-done.1
  101.2 1.2 fusion.1
  102.4 12.5 %all_to_all.62 = f32[4,8,32,128]{3,2,1,0:T(8,128)S(1)} all-to-all(f32[4,8,32,128]{3,2,1,0:T(8,128)S(1)} %fusion.1), channel_id=1, replica_groups={{0,2,4,6},{1,3,5,7},{8,10,12,14},{9,11,13,15},{16,18,20,22},{17,19,21,2..., dimensions={0} | all-to-all | bytes 1048576 | tf_op jit(solution)/shard_map/all_to_all | solution.py:94
  115.1 30.9 %all_to_all.63 = f32[16,32,2,512]{3,1,2,0:T(8,128)S(1)} all-to-all(f32[16,32,2,512]{3,1,2,0:T(8,128)S(1)} %broadcast_in_dim.95), channel_id=1, replica_groups=mesh['wide'=16,'col'=8] {'wide'}, dimensions={0} | all-to-all | bytes 4194304 | tf_op jit(solution)/shard_map/all_to_all | solution.py:35
  146.3 1.4 copy-done.2
  147.6 2.0 fusion.10
  150.0 2.6 collective-permute-done.2
  152.9 18.1 %all_to_all.64 = f32[4,64,2,512]{3,1,2,0:T(8,128)S(1)} all-to-all(f32[4,64,2,512]{3,1,2,0:T(8,128)S(1)} %bitcast_add_fusion.1), channel_id=1, replica_groups={{0,2,4,6},{1,3,5,7},{8,10,12,14},{9,11,13,15},{16,18,20,22},{17,19,21,2..., dimensions={0} | all-to-all | bytes 2097152 | tf_op jit(solution)/shard_map/all_to_all | solution.py:55
  171.0 0.8 reduce_sum.93
  171.8 1.1 copy_subtract_fusion.1
  173.0 17.3 %all_to_all.65 = f32[4,64,2,512]{3,1,2,0:T(8,128)S(1)} all-to-all(f32[4,64,2,512]{3,1,2,0:T(8,128)S(1)} %broadcast_in_dim.96), channel_id=1, replica_groups={{0,2,4,6},{1,3,5,7},{8,10,12,14},{9,11,13,15},{16,18,20,22},{17,19,21,2..., dimensions={0} | all-to-all | bytes 2097152 | tf_op jit(solution)/shard_map/all_to_all | solution.py:62
  190.4 2.6 collective-permute-done.3
  193.3 2.0 copy-done.1
  195.3 3.6 fusion.11
  199.5 54.1 %all_to_all.66 = f32[16,32,2,1024]{3,1,2,0:T(8,128)S(1)} all-to-all(f32[16,32,2,1024]{3,1,2,0:T(8,128)S(1)} %copy.141), channel_id=1, replica_groups=mesh['wide'=16,'col'=8] {'wide'}, dimensions={0} | all-to-all | bytes 8388608 | tf_op jit(solution)/shard_map/all_to_all | solution.py:28
  254.1 0.8 reduce_sum.95
  254.9 1.2 copy.155
  256.8 0.6 gather_fusion.3
  257.4 0.9 select_select_fusion
  258.5 0.6 gather_fusion.2
  259.1 1.5 collective-permute-done.4
  260.6 1.2 fusion
  261.8 12.5 %all_to_all.67 = f32[4,8,32,128]{3,2,1,0:T(8,128)S(1)} all-to-all(f32[4,8,32,128]{3,2,1,0:T(8,128)S(1)} %fusion), channel_id=1, replica_groups={{0,2,4,6},{1,3,5,7},{8,10,12,14},{9,11,13,15},{16,18,20,22},{17,19,21,2..., dimensions={0} | all-to-all | bytes 1048576 | tf_op jit(solution)/shard_map/all_to_all | solution.py:94
  274.6 30.9 %all_to_all.68 = f32[16,32,4,256]{3,1,2,0:T(8,128)S(1)} all-to-all(f32[16,32,4,256]{3,1,2,0:T(8,128)S(1)} %broadcast_in_dim.100), channel_id=1, replica_groups=mesh['wide'=16,'col'=8] {'wide'}, dimensions={0} | all-to-all | bytes 4194304 | tf_op jit(solution)/shard_map/all_to_all | solution.py:35
  305.6 1.1 copy-done.3
  306.6 1.1 fusion.12
  308.1 2.6 collective-permute-done.5
  310.9 18.1 %all_to_all.69 = f32[4,64,4,256]{3,1,2,0:T(8,128)S(1)} all-to-all(f32[4,64,4,256]{3,1,2,0:T(8,128)S(1)} %bitcast_add_fusion), channel_id=1, replica_groups={{0,2,4,6},{1,3,5,7},{8,10,12,14},{9,11,13,15},{16,18,20,22},{17,19,21,2..., dimensions={0} | all-to-all | bytes 2097152 | tf_op jit(solution)/shard_map/all_to_all | solution.py:55
  329.1 1.0 copy_subtract_fusion
  330.2 17.3 %all_to_all.70 = f32[4,64,4,256]{3,1,2,0:T(8,128)S(1)} all-to-all(f32[4,64,4,256]{3,1,2,0:T(8,128)S(1)} %broadcast_in_dim.101), channel_id=1, replica_groups={{0,2,4,6},{1,3,5,7},{8,10,12,14},{9,11,13,15},{16,18,20,22},{17,19,21,2..., dimensions={0} | all-to-all | bytes 2097152 | tf_op jit(solution)/shard_map/all_to_all | solution.py:62
  347.7 2.6 collective-permute-done.6
  350.6 1.9 fusion.13
  352.5 0.8 copy.153
  353.3 54.1 %all_to_all.71 = f32[16,32,4,512]{3,1,2,0:T(8,128)S(1)} all-to-all(f32[16,32,4,512]{3,1,2,0:T(8,128)S(1)} %copy.153), channel_id=1, replica_groups=mesh['wide'=16,'col'=8] {'wide'}, dimensions={0} | all-to-all | bytes 8388608 | tf_op jit(solution)/shard_map/all_to_all | solution.py:28
  408.1 0.9 copy.156
  (95 shorter events, 7.4 us)
Async XLA Ops:
  0.6 349.9 %copy-start = (f32[4,256,512]{2,1,0:T(8,128)S(1)}, f32[4,256,512]{2,1,0:T(8,128)}, u32[]{:S(2)}) copy-start(f32[4,256,512]{2,1,0:T(8,128)} %param.19) | copy-start | bytes 6291460
  24.1 6.0 %slice-start = ((s8[8388608]{0:T(1024)(128)(4,1)}), s8[4194304]{0:T(1024)(128)(4,1)S(1)}, s32[]{:S(2)}) async-start(s8[8388608]{0:T(1024)(128)(4,1)} %bitcast.115), calls=%async_computation.12 | async-start | bytes 8388608
  24.9 2.9 collective-permute-start
  27.9 2.3 slice-start.1
  97.2 5.1 %copy-start.4 = (f32[32,2048]{1,0:T(8,128)}, f32[32,2048]{1,0:T(8,128)S(1)}, u32[]{:S(2)}) copy-start(f32[32,2048]{1,0:T(8,128)S(1)} %reduce_sum.91) | copy-start | bytes 786436
  98.9 2.3 collective-permute-start.1
  146.0 1.6 copy-start.2
  149.9 2.7 collective-permute-start.2
  190.3 2.7 collective-permute-start.3
  193.1 2.2 copy-start.1
  256.1 0.7 copy-start.5
  258.4 2.3 collective-permute-start.4
  305.4 1.2 copy-start.3
  308.0 2.7 collective-permute-start.5
  347.6 2.7 collective-permute-start.6

commit v13 on v12

--- a/solution.py
+++ b/solution.py
@@ -77,9 +77,16 @@
     return jnp.einsum(spec, lhs, rhs, precision=PRECISE, preferred_element_type=jnp.float32)
 
 
-def level(z_local, update_partial, inverse, cores):
+def level(z_local, near_rows, panel, spec, inverse, cores):
     n = lax.axis_size("col")
-    update = col_sum(update_partial.reshape((n, -1) + update_partial.shape[1:]), cores)
+    paired = near_rows.reshape((n // 2, 2, -1) + near_rows.shape[1:])
+    other = pick_core(paired, cores[1])
+    other = matmul(other.reshape((-1,) + other.shape[2:]), panel, spec)
+    sent = lax.ppermute(other.reshape((n // 2, -1) + other.shape[1:]), "col", [(d, d ^ 1) for d in range(n)])
+    mine = pick_core(paired, cores[0])
+    mine = matmul(mine.reshape((-1,) + mine.shape[2:]), panel, spec)
+    chip = mine.reshape(sent.shape) + sent
+    update = lax.all_to_all(chip, "col", 0, 0, tiled=False, axis_index_groups=chip_groups(n)).sum(0)
     right_side = col_gather(z_local - update, cores)
     right_side = right_side.reshape((-1,) + right_side.shape[2:])
     return exchange_sum(matmul(right_side, inverse, "ski,kij->skj"), "wide")
@@ -175,7 +182,7 @@
     near_local = send_blocks(root_tiles, child_tables)
     near_local = rows_of(near_local, anc_child.shape[0], anc_child.shape[1] // n_col)
     near_rows = exchange_gather(near_local, "wide", 0)
-    x_child = level(z_child, matmul(near_rows, panel_child, "ska,kaj->skj"), inv_child, cores)
+    x_child = level(z_child, near_rows, panel_child, "ska,kaj->skj", inv_child, cores)
 
     x_child, grand_tables, cores = lax.optimization_barrier((x_child, grand_tables, cores))
     child_tiles = x_child.reshape(x_child.shape[0], kids * per_child, BLK).transpose(1, 0, 2)
@@ -183,7 +190,7 @@
     far_local = send_blocks(all_tiles, grand_tables)
     far_local = rows_of(far_local, anc_grand.shape[0], anc_grand.shape[1] // n_col)
     far_rows = exchange_gather(far_local, "wide", 0)
-    x_grand = level(z_grand, matmul(far_rows, panel_grand, "sga,gaj->sgj"), inv_grand, cores)
+    x_grand = level(z_grand, far_rows, panel_grand, "sga,gaj->sgj", inv_grand, cores)
     return (x_root, x_child, x_grand)
 
 

time: 410 us -> 409 us (level)
    dot_general x5 -> x7, matrix products: 16 us -> 16.6 us  [matmul(): jnp.einsum(spec, lhs, rhs, precision=PRECISE, preferred_element_type=jnp....]
  transfers between devices with their start and end apart: 7 -> 7, of which waited for: 7 -> 7; matrix products, arithmetic and copies ran while one was open for 0% -> 1% of each run, Pallas kernels for 0% -> 0%
where the time goes in v13:
time: 409 us; the launch traced here: 408 us
  blocking collectives  345 us (84%)
  local copies, waits for them, and re-layouts  16.9 us (4%)
  matrix products  16.6 us (4%)
  waiting for transfers between devices  14.5 us (4%)
  other arithmetic  12.8 us (3%)
    all_to_all x3, blocking collectives, exchange_sum(): lax.all_to_all(partial.reshape((n, chunk) + partial.shape[1:]), axis, 0,...  167 us
    all_to_all x2, blocking collectives, exchange_gather(): parts = lax.all_to_all(stacked, axis, 0, 0, tiled=False)  61.8 us
    all_to_all x3, blocking collectives, col_halves(): lax.all_to_all(stacked, 'col', 0, 0, tiled=False, axis_index_groups=chip_...  55.1 us
    all_to_all x2, blocking collectives, level(): lax.all_to_all(chip, 'col', 0, 0, tiled=False, axis_index_groups=chip_gro...  36.2 us
    all_to_all x2, blocking collectives, send_blocks(): lax.all_to_all(own + sent, 'col', 0, 0, tiled=False, axis_index_groups=ch...  24.9 us
    dot_general x7, matrix products, matmul(): jnp.einsum(spec, lhs, rhs, precision=PRECISE, preferred_element_type=jnp....  16.6 us
  transfers between devices with their start and end apart: 7, of which 7 were waited for; matrix products, arithmetic and copies ran while one was open for 1% of the time, Pallas kernels for 0%

profile of v13, /device:TPU:0, one launch (start us, length us, event | category | flops | bytes accessed | tf_op | source)
XLA Modules:
  0.0 407.9 jit_solution(14659262369493451693)
XLA Ops:
  0.7 0.8 convert_element_type.21
  1.6 0.7 convert_element_type.23
  2.5 1.0 concatenate.14
  3.6 20.5 %all_to_all.60 = f32[4,72,1024]{2,1,0:T(8,128)S(1)} all-to-all(f32[4,72,1024]{2,1,0:T(8,128)S(1)} %broadcast_in_dim.90), channel_id=1, replica_groups={{0,2,4,6},{1,3,5,7},{8,10,12,14},{9,11,13,15},{16,18,20,22},{17,19,21,2..., dimensions={0} | all-to-all | bytes 2359296 | tf_op jit(solution)/shard_map/all_to_all | solution.py:62
  24.1 0.8 copy.127
  25.1 2.7 collective-permute-done
  27.9 0.7 maximum_select_fusion
  28.6 1.2 copy.129
  30.2 7.4 %fusion.9 = f32[512,2048]{1,0:T(8,128)S(1)} fusion(f32[512,1024]{1,0:T(8,128)S(1)} %bitcast.120, f32[1024,2048]{1,0:T(8,128)S(1)} %bitcast.119), kind=kOutput, calls=%fused_computation.96 | convolution fusion | flops 6442450944 | bytes 14680064 | tf_op jit(solution)/shard_map/si,ij->sj/dot_general | solution.py:77
  37.6 59.2 %all_to_all.61 = f32[16,32,2048]{2,1,0:T(8,128)S(1)} all-to-all(f32[16,32,2048]{2,1,0:T(8,128)S(1)} %bitcast.115), channel_id=1, replica_groups=mesh['wide'=16,'col'=8] {'wide'}, dimensions={0} | all-to-all | bytes 8388608 | tf_op jit(solution)/shard_map/all_to_all | solution.py:28
  97.4 0.6 gather_fusion.1
  98.0 0.9 select_select_fusion.2
  99.0 0.6 gather_fusion
  99.6 1.5 collective-permute-done.1
  101.2 1.2 fusion.1
  102.4 12.5 %all_to_all.62 = f32[4,8,32,128]{3,2,1,0:T(8,128)S(1)} all-to-all(f32[4,8,32,128]{3,2,1,0:T(8,128)S(1)} %fusion.1), channel_id=1, replica_groups={{0,2,4,6},{1,3,5,7},{8,10,12,14},{9,11,13,15},{16,18,20,22},{17,19,21,2..., dimensions={0} | all-to-all | bytes 1048576 | tf_op jit(solution)/shard_map/all_to_all | solution.py:101
  115.1 30.9 %all_to_all.63 = f32[16,32,2,512]{3,1,2,0:T(8,128)S(1)} all-to-all(f32[16,32,2,512]{3,1,2,0:T(8,128)S(1)} %broadcast_in_dim.95), channel_id=1, replica_groups=mesh['wide'=16,'col'=8] {'wide'}, dimensions={0} | all-to-all | bytes 4194304 | tf_op jit(solution)/shard_map/all_to_all | solution.py:35
  146.6 1.3 copy-done.1
  147.9 1.2 fusion.11
  149.3 1.2 fusion.10
  150.4 1.5 collective-permute-done.2
  152.1 18.1 %all_to_all.64 = f32[4,64,2,512]{3,1,2,0:T(8,128)S(1)} all-to-all(f32[4,64,2,512]{3,1,2,0:T(8,128)S(1)} %copy_add_fusion.1), channel_id=1, replica_groups={{0,2,4,6},{1,3,5,7},{8,10,12,14},{9,11,13,15},{16,18,20,22},{17,19,21,2..., dimensions={0} | all-to-all | bytes 2097152 | tf_op jit(solution)/shard_map/all_to_all | solution.py:89
  170.2 0.8 reduce_sum.93
  171.0 1.1 copy_subtract_fusion.1
  172.2 17.3 %all_to_all.65 = f32[4,64,2,512]{3,1,2,0:T(8,128)S(1)} all-to-all(f32[4,64,2,512]{3,1,2,0:T(8,128)S(1)} %broadcast_in_dim.96), channel_id=1, replica_groups={{0,2,4,6},{1,3,5,7},{8,10,12,14},{9,11,13,15},{16,18,20,22},{17,19,21,2..., dimensions={0} | all-to-all | bytes 2097152 | tf_op jit(solution)/shard_map/all_to_all | solution.py:62
  189.7 2.6 collective-permute-done.3
  192.6 2.0 copy-done.3
  194.5 3.6 fusion.12
  198.7 54.1 %all_to_all.66 = f32[16,32,2,1024]{3,1,2,0:T(8,128)S(1)} all-to-all(f32[16,32,2,1024]{3,1,2,0:T(8,128)S(1)} %copy.141), channel_id=1, replica_groups=mesh['wide'=16,'col'=8] {'wide'}, dimensions={0} | all-to-all | bytes 8388608 | tf_op jit(solution)/shard_map/all_to_all | solution.py:28
  253.4 0.8 reduce_sum.95
  254.2 1.2 copy.155
  256.7 0.9 select_select_fusion
  258.3 1.5 collective-permute-done.4
  259.9 1.2 fusion
  261.0 12.5 %all_to_all.67 = f32[4,8,32,128]{3,2,1,0:T(8,128)S(1)} all-to-all(f32[4,8,32,128]{3,2,1,0:T(8,128)S(1)} %fusion), channel_id=1, replica_groups={{0,2,4,6},{1,3,5,7},{8,10,12,14},{9,11,13,15},{16,18,20,22},{17,19,21,2..., dimensions={0} | all-to-all | bytes 1048576 | tf_op jit(solution)/shard_map/all_to_all | solution.py:101
  273.8 30.9 %all_to_all.68 = f32[16,32,4,256]{3,1,2,0:T(8,128)S(1)} all-to-all(f32[16,32,4,256]{3,1,2,0:T(8,128)S(1)} %broadcast_in_dim.100), channel_id=1, replica_groups=mesh['wide'=16,'col'=8] {'wide'}, dimensions={0} | all-to-all | bytes 4194304 | tf_op jit(solution)/shard_map/all_to_all | solution.py:35
  305.2 1.0 copy-done.2
  306.1 0.7 fusion.14
  307.0 0.7 fusion.13
  307.7 2.0 collective-permute-done.5
  309.8 18.1 %all_to_all.69 = f32[4,64,4,256]{3,1,2,0:T(8,128)S(1)} all-to-all(f32[4,64,4,256]{3,1,2,0:T(8,128)S(1)} %copy_add_fusion), channel_id=1, replica_groups={{0,2,4,6},{1,3,5,7},{8,10,12,14},{9,11,13,15},{16,18,20,22},{17,19,21,2..., dimensions={0} | all-to-all | bytes 2097152 | tf_op jit(solution)/shard_map/all_to_all | solution.py:89
  328.0 1.0 copy_subtract_fusion
  329.1 17.3 %all_to_all.70 = f32[4,64,4,256]{3,1,2,0:T(8,128)S(1)} all-to-all(f32[4,64,4,256]{3,1,2,0:T(8,128)S(1)} %broadcast_in_dim.101), channel_id=1, replica_groups={{0,2,4,6},{1,3,5,7},{8,10,12,14},{9,11,13,15},{16,18,20,22},{17,19,21,2..., dimensions={0} | all-to-all | bytes 2097152 | tf_op jit(solution)/shard_map/all_to_all | solution.py:62
  346.6 2.6 collective-permute-done.6
  349.5 1.9 fusion.15
  351.4 0.8 copy.153
  352.2 54.1 %all_to_all.71 = f32[16,32,4,512]{3,1,2,0:T(8,128)S(1)} all-to-all(f32[16,32,4,512]{3,1,2,0:T(8,128)S(1)} %copy.153), channel_id=1, replica_groups=mesh['wide'=16,'col'=8] {'wide'}, dimensions={0} | all-to-all | bytes 8388608 | tf_op jit(solution)/shard_map/all_to_all | solution.py:28
  407.0 0.9 copy.156
  (97 shorter events, 8.8 us)
Async XLA Ops:
  0.6 348.9 %copy-start = (f32[4,256,512]{2,1,0:T(8,128)S(1)}, f32[4,256,512]{2,1,0:T(8,128)}, u32[]{:S(2)}) copy-start(f32[4,256,512]{2,1,0:T(8,128)} %param.19) | copy-start | bytes 6291460
  24.1 6.0 %slice-start = ((s8[8388608]{0:T(1024)(128)(4,1)}), s8[4194304]{0:T(1024)(128)(4,1)S(1)}, s32[]{:S(2)}) async-start(s8[8388608]{0:T(1024)(128)(4,1)} %bitcast.118), calls=%async_computation.12 | async-start | bytes 8388608
  24.9 2.9 collective-permute-start
  27.9 2.3 slice-start.1
  97.2 5.1 %copy-start.4 = (f32[32,2048]{1,0:T(8,128)}, f32[32,2048]{1,0:T(8,128)S(1)}, u32[]{:S(2)}) copy-start(f32[32,2048]{1,0:T(8,128)S(1)} %reduce_sum.91) | copy-start | bytes 786436
  98.9 2.3 collective-permute-start.1
  146.3 1.6 copy-start.1
  149.2 2.7 collective-permute-start.2
  189.6 2.7 collective-permute-start.3
  192.3 2.2 copy-start.3
  255.3 0.7 copy-start.5
  257.6 2.3 collective-permute-start.4
  304.9 1.2 copy-start.2
  306.9 2.7 collective-permute-start.5
  346.5 2.7 collective-permute-start.6

commit v14 on v13

--- a/solution.py
+++ b/solution.py
@@ -87,9 +87,11 @@
     mine = matmul(mine.reshape((-1,) + mine.shape[2:]), panel, spec)
     chip = mine.reshape(sent.shape) + sent
     update = lax.all_to_all(chip, "col", 0, 0, tiled=False, axis_index_groups=chip_groups(n)).sum(0)
-    right_side = col_gather(z_local - update, cores)
-    right_side = right_side.reshape((-1,) + right_side.shape[2:])
-    return exchange_sum(matmul(right_side, inverse, "ski,kij->skj"), "wide")
+    same, other = col_halves(z_local - update)
+    own = matmul(same.reshape((-1,) + same.shape[2:]), inverse, "ski,kij->skj")
+    far = matmul(other.reshape((-1,) + other.shape[2:]), inverse, "ski,kij->skj")
+    partial = col_join(own.reshape(same.shape[:2] + own.shape[1:]), far.reshape(other.shape[:2] + far.shape[1:]), cores)
+    return exchange_sum(partial.reshape((-1,) + partial.shape[2:]), "wide")
 
 
 def send_blocks(tiles, tables):

time: 409 us -> 406 us (level)
    dot_general x7 -> x9, matrix products: 16.6 us -> 18.1 us  [matmul(): jnp.einsum(spec, lhs, rhs, precision=PRECISE, preferred_element_type=jnp....]
  transfers between devices with their start and end apart: 7 -> 7, of which waited for: 7 -> 7; matrix products, arithmetic and copies ran while one was open for 1% -> 2% of each run, Pallas kernels for 0% -> 0%
where the time goes in v14:
time: 406 us; the launch traced here: 405 us
  blocking collectives  346 us (85%)
  matrix products  18.1 us (4%)
  local copies, waits for them, and re-layouts  14.5 us (4%)
  other arithmetic  14 us (3%)
  waiting for transfers between devices  10.9 us (3%)
    all_to_all x3, blocking collectives, exchange_sum(): lax.all_to_all(partial.reshape((n, chunk) + partial.shape[1:]), axis, 0,...  168 us
    all_to_all x2, blocking collectives, exchange_gather(): parts = lax.all_to_all(stacked, axis, 0, 0, tiled=False)  61.7 us
    all_to_all x3, blocking collectives, col_halves(): lax.all_to_all(stacked, 'col', 0, 0, tiled=False, axis_index_groups=chip_...  55.3 us
    all_to_all x2, blocking collectives, level(): lax.all_to_all(chip, 'col', 0, 0, tiled=False, axis_index_groups=chip_gro...  36.2 us
    all_to_all x2, blocking collectives, send_blocks(): lax.all_to_all(own + sent, 'col', 0, 0, tiled=False, axis_index_groups=ch...  24.9 us
    dot_general x9, matrix products, matmul(): jnp.einsum(spec, lhs, rhs, precision=PRECISE, preferred_element_type=jnp....  18.1 us
  transfers between devices with their start and end apart: 7, of which 7 were waited for; matrix products, arithmetic and copies ran while one was open for 2% of the time, Pallas kernels for 0%

profile of v14, /device:TPU:0, one launch (start us, length us, event | category | flops | bytes accessed | tf_op | source)
XLA Modules:
  0.0 405.0 jit_solution(6484177438452230747)
XLA Ops:
  0.7 0.8 convert_element_type.21
  1.6 0.7 convert_element_type.23
  2.5 1.0 concatenate.14
  3.6 20.5 %all_to_all.60 = f32[4,72,1024]{2,1,0:T(8,128)S(1)} all-to-all(f32[4,72,1024]{2,1,0:T(8,128)S(1)} %broadcast_in_dim.90), channel_id=1, replica_groups={{0,2,4,6},{1,3,5,7},{8,10,12,14},{9,11,13,15},{16,18,20,22},{17,19,21,2..., dimensions={0} | all-to-all | bytes 2359296 | tf_op jit(solution)/shard_map/all_to_all | solution.py:62
  24.1 0.8 copy.147
  25.1 2.7 collective-permute-done
  27.9 0.7 maximum_select_fusion.2
  28.6 1.2 copy.149
  30.2 7.4 %fusion.9 = f32[512,2048]{1,0:T(8,128)S(1)} fusion(f32[512,1024]{1,0:T(8,128)S(1)} %bitcast.138, f32[1024,2048]{1,0:T(8,128)S(1)} %bitcast.137), kind=kOutput, calls=%fused_computation.94 | convolution fusion | flops 6442450944 | bytes 14680064 | tf_op jit(solution)/shard_map/si,ij->sj/dot_general | solution.py:77
  37.6 59.2 %all_to_all.61 = f32[16,32,2048]{2,1,0:T(8,128)S(1)} all-to-all(f32[16,32,2048]{2,1,0:T(8,128)S(1)} %bitcast.133), channel_id=1, replica_groups=mesh['wide'=16,'col'=8] {'wide'}, dimensions={0} | all-to-all | bytes 8388608 | tf_op jit(solution)/shard_map/all_to_all | solution.py:28
  97.4 0.6 gather_fusion.1
  98.0 0.9 select_select_fusion.2
  99.6 1.5 collective-permute-done.1
  101.2 1.2 fusion.1
  102.4 12.5 %all_to_all.62 = f32[4,8,32,128]{3,2,1,0:T(8,128)S(1)} all-to-all(f32[4,8,32,128]{3,2,1,0:T(8,128)S(1)} %fusion.1), channel_id=1, replica_groups={{0,2,4,6},{1,3,5,7},{8,10,12,14},{9,11,13,15},{16,18,20,22},{17,19,21,2..., dimensions={0} | all-to-all | bytes 1048576 | tf_op jit(solution)/shard_map/all_to_all | solution.py:103
  115.1 30.9 %all_to_all.63 = f32[16,32,2,512]{3,1,2,0:T(8,128)S(1)} all-to-all(f32[16,32,2,512]{3,1,2,0:T(8,128)S(1)} %broadcast_in_dim.95), channel_id=1, replica_groups=mesh['wide'=16,'col'=8] {'wide'}, dimensions={0} | all-to-all | bytes 4194304 | tf_op jit(solution)/shard_map/all_to_all | solution.py:35
  146.6 1.3 copy-done.2
  147.9 1.2 fusion.11
  149.3 1.2 fusion.10
  150.4 1.5 collective-permute-done.2
  152.1 18.1 %all_to_all.64 = f32[4,64,2,512]{3,1,2,0:T(8,128)S(1)} all-to-all(f32[4,64,2,512]{3,1,2,0:T(8,128)S(1)} %copy_add_fusion.1), channel_id=1, replica_groups={{0,2,4,6},{1,3,5,7},{8,10,12,14},{9,11,13,15},{16,18,20,22},{17,19,21,2..., dimensions={0} | all-to-all | bytes 2097152 | tf_op jit(solution)/shard_map/all_to_all | solution.py:89
  170.2 0.8 reduce_sum.93
  171.0 1.1 copy_subtract_fusion.1
  172.3 17.5 %all_to_all.65 = f32[4,64,2,512]{3,1,2,0:T(8,128)S(1)} all-to-all(f32[4,64,2,512]{3,1,2,0:T(8,128)S(1)} %broadcast_in_dim.96), channel_id=1, replica_groups={{0,2,4,6},{1,3,5,7},{8,10,12,14},{9,11,13,15},{16,18,20,22},{17,19,21,2..., dimensions={0} | all-to-all | bytes 2097152 | tf_op jit(solution)/shard_map/all_to_all | solution.py:62
  189.9 2.3 fusion.12
  192.5 2.3 fusion.13
  194.9 0.8 maximum_select_fusion
  196.0 54.6 %all_to_all.66 = f32[16,32,2,1024]{3,1,2,0:T(8,128)S(1)} all-to-all(f32[16,32,2,1024]{3,1,2,0:T(8,128)S(1)} %copy.165), channel_id=1, replica_groups=mesh['wide'=16,'col'=8] {'wide'}, dimensions={0} | all-to-all | bytes 8388608 | tf_op jit(solution)/shard_map/all_to_all | solution.py:28
  251.2 0.8 reduce_sum.95
  251.9 1.2 copy.183
  254.4 0.9 select_select_fusion
  256.1 1.5 collective-permute-done.4
  257.6 1.2 fusion
  258.8 12.5 %all_to_all.67 = f32[4,8,32,128]{3,2,1,0:T(8,128)S(1)} all-to-all(f32[4,8,32,128]{3,2,1,0:T(8,128)S(1)} %fusion), channel_id=1, replica_groups={{0,2,4,6},{1,3,5,7},{8,10,12,14},{9,11,13,15},{16,18,20,22},{17,19,21,2..., dimensions={0} | all-to-all | bytes 1048576 | tf_op jit(solution)/shard_map/all_to_all | solution.py:103
  271.6 30.8 %all_to_all.68 = f32[16,32,4,256]{3,1,2,0:T(8,128)S(1)} all-to-all(f32[16,32,4,256]{3,1,2,0:T(8,128)S(1)} %broadcast_in_dim.100), channel_id=1, replica_groups=mesh['wide'=16,'col'=8] {'wide'}, dimensions={0} | all-to-all | bytes 4194304 | tf_op jit(solution)/shard_map/all_to_all | solution.py:35
  302.8 1.0 copy-done.3
  303.8 0.7 fusion.15
  304.7 0.7 fusion.14
  305.4 2.0 collective-permute-done.5
  307.5 18.1 %all_to_all.69 = f32[4,64,4,256]{3,1,2,0:T(8,128)S(1)} all-to-all(f32[4,64,4,256]{3,1,2,0:T(8,128)S(1)} %copy_add_fusion), channel_id=1, replica_groups={{0,2,4,6},{1,3,5,7},{8,10,12,14},{9,11,13,15},{16,18,20,22},{17,19,21,2..., dimensions={0} | all-to-all | bytes 2097152 | tf_op jit(solution)/shard_map/all_to_all | solution.py:89
  325.7 1.0 copy_subtract_fusion
  326.8 17.3 %all_to_all.70 = f32[4,64,4,256]{3,1,2,0:T(8,128)S(1)} all-to-all(f32[4,64,4,256]{3,1,2,0:T(8,128)S(1)} %broadcast_in_dim.101), channel_id=1, replica_groups={{0,2,4,6},{1,3,5,7},{8,10,12,14},{9,11,13,15},{16,18,20,22},{17,19,21,2..., dimensions={0} | all-to-all | bytes 2097152 | tf_op jit(solution)/shard_map/all_to_all | solution.py:62
  344.2 1.2 fusion.16
  345.4 1.4 collective-permute-done.6
  346.8 1.2 fusion.17
  348.0 0.8 maximum_select_fusion.1
  349.3 54.1 %all_to_all.71 = f32[16,32,4,512]{3,1,2,0:T(8,128)S(1)} all-to-all(f32[16,32,4,512]{3,1,2,0:T(8,128)S(1)} %copy.181), channel_id=1, replica_groups=mesh['wide'=16,'col'=8] {'wide'}, dimensions={0} | all-to-all | bytes 8388608 | tf_op jit(solution)/shard_map/all_to_all | solution.py:28
  404.2 0.9 copy.184
  (101 shorter events, 9.4 us)
Async XLA Ops:
  0.6 343.6 %copy-start = (f32[4,256,512]{2,1,0:T(8,128)S(1)}, f32[4,256,512]{2,1,0:T(8,128)}, u32[]{:S(2)}) copy-start(f32[4,256,512]{2,1,0:T(8,128)} %param.19) | copy-start | bytes 6291460
  24.1 6.0 %slice-start = ((s8[8388608]{0:T(1024)(128)(4,1)}), s8[4194304]{0:T(1024)(128)(4,1)S(1)}, s32[]{:S(2)}) async-start(s8[8388608]{0:T(1024)(128)(4,1)} %bitcast.136), calls=%async_computation.12 | async-start | bytes 8388608
  24.9 2.9 collective-permute-start
  27.9 2.3 slice-start.1
  97.2 5.1 %copy-start.4 = (f32[32,2048]{1,0:T(8,128)}, f32[32,2048]{1,0:T(8,128)S(1)}, u32[]{:S(2)}) copy-start(f32[32,2048]{1,0:T(8,128)S(1)} %reduce_sum.91) | copy-start | bytes 786436
  98.9 2.3 collective-permute-start.1
  146.3 1.6 copy-start.2
  149.2 2.7 collective-permute-start.2
  172.2 17.6 %copy-start.1 = (f32[2,512,1024]{2,1,0:T(8,128)S(1)}, f32[2,512,1024]{2,1,0:T(8,128)}, u32[]{:S(2)}) copy-start(f32[2,512,1024]{2,1,0:T(8,128)} %param.18) | copy-start | bytes 12582916
  189.8 2.7 collective-permute-start.3
  253.1 0.7 copy-start.5
  255.4 2.3 collective-permute-start.4
  302.6 1.2 copy-start.3
  304.6 2.7 collective-permute-start.5
  344.1 2.7 collective-permute-start.6

commit v15 on v14

--- a/solution.py
+++ b/solution.py
@@ -149,7 +149,7 @@
     with_lists, here, cores = lax.optimization_barrier((jnp.concatenate([z_root, extra], axis=0)[None], here, cores))
     same, other = col_halves(with_lists[0])
     rows = z_root.shape[0]
-    root_right = col_join(same[:, :rows], other[:, :rows], cores).reshape(-1, z_root.shape[1])
+    root_same, root_other = same[:, :rows], other[:, :rows]
     got = col_join(same[:, rows : rows + 2], other[:, rows : rows + 2], cores).astype(jnp.int32)
     anc_child = got[:, 0, : anc_child.size].reshape((n_col,) + anc_child.shape).transpose(1, 0, 2).reshape(anc_child.shape[0], -1)
     anc_grand = got[:, 1, : anc_grand.size].reshape((n_col,) + anc_grand.shape).transpose(1, 0, 2).reshape(anc_grand.shape[0], -1)
@@ -173,10 +173,13 @@
     child_tables = (child_tables[0], child_tables[2], child_tables[1], child_tables[3])
     grand_tables = by_core(owner, cores) + by_core(local, cores)
     grand_tables = (grand_tables[0], grand_tables[2], grand_tables[1], grand_tables[3])
-    root_right, child_tables, grand_tables, cores = lax.optimization_barrier(
-        (root_right, child_tables, grand_tables, cores)
-    )
-    x_root = exchange_sum(matmul(root_right, inv_root, "si,ij->sj"), "wide")
+    root_same, child_tables, grand_tables, cores = lax.optimization_barrier(
+        (root_same, child_tables, grand_tables, cores)
+    )
+    own = matmul(root_same.reshape(-1, root_same.shape[2]), inv_root, "si,ij->sj")
+    far = matmul(root_other.reshape(-1, root_other.shape[2]), inv_root, "si,ij->sj")
+    root_partial = col_join(own.reshape(root_same.shape[:2] + own.shape[1:]), far.reshape(root_other.shape[:2] + far.shape[1:]), cores)
+    x_root = exchange_sum(root_partial.reshape((-1,) + root_partial.shape[2:]), "wide")
     x_root, child_tables, grand_tables, cores = lax.optimization_barrier(
         (x_root, child_tables, grand_tables, cores)
     )

time: 406 us -> 406 us (level)
    dot_general x9 -> x10, matrix products: 18.1 us -> 20 us  [matmul(): jnp.einsum(spec, lhs, rhs, precision=PRECISE, preferred_element_type=jnp....]
where the time goes in v15:
time: 406 us; the launch traced here: 405 us
  blocking collectives  346 us (85%)
  matrix products  20 us (5%)
  other arithmetic  13.9 us (3%)
  local copies, waits for them, and re-layouts  13.1 us (3%)
  waiting for transfers between devices  10.8 us (3%)
    all_to_all x3, blocking collectives, exchange_sum(): lax.all_to_all(partial.reshape((n, chunk) + partial.shape[1:]), axis, 0,...  168 us
    all_to_all x2, blocking collectives, exchange_gather(): parts = lax.all_to_all(stacked, axis, 0, 0, tiled=False)  61.7 us
    all_to_all x3, blocking collectives, col_halves(): lax.all_to_all(stacked, 'col', 0, 0, tiled=False, axis_index_groups=chip_...  55.5 us
    all_to_all x2, blocking collectives, level(): lax.all_to_all(chip, 'col', 0, 0, tiled=False, axis_index_groups=chip_gro...  36.2 us
    all_to_all x2, blocking collectives, send_blocks(): lax.all_to_all(own + sent, 'col', 0, 0, tiled=False, axis_index_groups=ch...  24.9 us
    dot_general x10, matrix products, matmul(): jnp.einsum(spec, lhs, rhs, precision=PRECISE, preferred_element_type=jnp....  20 us
  transfers between devices with their start and end apart: 7, of which 7 were waited for; matrix products, arithmetic and copies ran while one was open for 2% of the time, Pallas kernels for 0%

profile of v15, /device:TPU:0, one launch (start us, length us, event | category | flops | bytes accessed | tf_op | source)
XLA Modules:
  0.0 405.5 jit_solution(1654938593451834659)
XLA Ops:
  0.7 0.8 convert_element_type.21
  1.6 0.7 convert_element_type.23
  2.5 1.0 concatenate.14
  3.6 20.8 %all_to_all.60 = f32[4,72,1024]{2,1,0:T(8,128)S(1)} all-to-all(f32[4,72,1024]{2,1,0:T(8,128)S(1)} %broadcast_in_dim.90), channel_id=1, replica_groups={{0,2,4,6},{1,3,5,7},{8,10,12,14},{9,11,13,15},{16,18,20,22},{17,19,21,2..., dimensions={0} | all-to-all | bytes 2359296 | tf_op jit(solution)/shard_map/all_to_all | solution.py:62
  24.4 0.8 copy.154
  25.4 2.7 collective-permute-done
  28.5 4.4 %fusion.4 = f32[4,1,64,2048]{3,2,0,1:T(8,128)S(1)} fusion(f32[4,64,1024]{2,1,0:T(8,128)S(1)} %slice.32, f32[1024,2048]{1,0:T(8,128)S(1)} %copy-done.1), kind=kOutput, calls=%fused_computation.14 | convolution fusion | flops 3221225472 | bytes 11534336 | tf_op jit(solution)/shard_map/si,ij->sj/dot_general | solution.py:77
  33.0 4.9 %fusion.7 = f32[4,1,64,2048]{3,2,0,1:T(8,128)S(1)} fusion(f32[1024,2048]{1,0:T(8,128)S(1)} %copy-done.1, f32[4,64,1024]{2,0,1:T(4,128)S(1)} %slice.37), kind=kOutput, calls=%fused_computation.15 | convolution fusion | flops 3221225472 | bytes 11534336 | tf_op jit(solution)/shard_map/si,ij->sj/dot_general | solution.py:77
  38.6 59.2 %all_to_all.61 = f32[16,32,2048]{2,1,0:T(8,128)S(1)} all-to-all(f32[16,32,2048]{2,1,0:T(8,128)S(1)} %bitcast.142), channel_id=1, replica_groups=mesh['wide'=16,'col'=8] {'wide'}, dimensions={0} | all-to-all | bytes 8388608 | tf_op jit(solution)/shard_map/all_to_all | solution.py:28
  98.4 0.6 gather_fusion.1
  99.0 0.9 select_select_fusion.2
  100.0 0.6 gather_fusion
  100.6 1.5 collective-permute-done.1
  102.1 1.2 fusion.12
  103.3 12.5 %all_to_all.62 = f32[4,8,32,128]{3,2,1,0:T(8,128)S(1)} all-to-all(f32[4,8,32,128]{3,2,1,0:T(8,128)S(1)} %fusion.12), channel_id=1, replica_groups={{0,2,4,6},{1,3,5,7},{8,10,12,14},{9,11,13,15},{16,18,20,22},{17,19,21,2..., dimensions={0} | all-to-all | bytes 1048576 | tf_op jit(solution)/shard_map/all_to_all | solution.py:103
  116.1 30.9 %all_to_all.63 = f32[16,32,2,512]{3,1,2,0:T(8,128)S(1)} all-to-all(f32[16,32,2,512]{3,1,2,0:T(8,128)S(1)} %broadcast_in_dim.95), channel_id=1, replica_groups=mesh['wide'=16,'col'=8] {'wide'}, dimensions={0} | all-to-all | bytes 4194304 | tf_op jit(solution)/shard_map/all_to_all | solution.py:35
  147.5 1.1 copy-done.3
  148.6 1.2 fusion.21
  150.0 1.2 fusion.20
  151.1 1.5 collective-permute-done.2
  152.8 18.1 %all_to_all.64 = f32[4,64,2,512]{3,1,2,0:T(8,128)S(1)} all-to-all(f32[4,64,2,512]{3,1,2,0:T(8,128)S(1)} %copy_add_fusion.1), channel_id=1, replica_groups={{0,2,4,6},{1,3,5,7},{8,10,12,14},{9,11,13,15},{16,18,20,22},{17,19,21,2..., dimensions={0} | all-to-all | bytes 2097152 | tf_op jit(solution)/shard_map/all_to_all | solution.py:89
  170.9 0.8 reduce_sum.93
  171.7 1.2 copy_subtract_fusion.1
  173.1 17.4 %all_to_all.65 = f32[4,64,2,512]{3,1,2,0:T(8,128)S(1)} all-to-all(f32[4,64,2,512]{3,1,2,0:T(8,128)S(1)} %broadcast_in_dim.96), channel_id=1, replica_groups={{0,2,4,6},{1,3,5,7},{8,10,12,14},{9,11,13,15},{16,18,20,22},{17,19,21,2..., dimensions={0} | all-to-all | bytes 2097152 | tf_op jit(solution)/shard_map/all_to_all | solution.py:62
  190.6 2.3 fusion.22
  193.2 2.3 fusion.23
  195.6 0.8 maximum_select_fusion.1
  196.7 54.6 %all_to_all.66 = f32[16,32,2,1024]{3,1,2,0:T(8,128)S(1)} all-to-all(f32[16,32,2,1024]{3,1,2,0:T(8,128)S(1)} %copy.172), channel_id=1, replica_groups=mesh['wide'=16,'col'=8] {'wide'}, dimensions={0} | all-to-all | bytes 8388608 | tf_op jit(solution)/shard_map/all_to_all | solution.py:28
  251.9 0.8 reduce_sum.95
  252.7 1.2 copy.190
  255.2 0.9 select_select_fusion
  256.8 1.5 collective-permute-done.4
  258.3 1.2 fusion.11
  259.5 12.5 %all_to_all.67 = f32[4,8,32,128]{3,2,1,0:T(8,128)S(1)} all-to-all(f32[4,8,32,128]{3,2,1,0:T(8,128)S(1)} %fusion.11), channel_id=1, replica_groups={{0,2,4,6},{1,3,5,7},{8,10,12,14},{9,11,13,15},{16,18,20,22},{17,19,21,2..., dimensions={0} | all-to-all | bytes 1048576 | tf_op jit(solution)/shard_map/all_to_all | solution.py:103
  272.3 30.8 %all_to_all.68 = f32[16,32,4,256]{3,1,2,0:T(8,128)S(1)} all-to-all(f32[16,32,4,256]{3,1,2,0:T(8,128)S(1)} %broadcast_in_dim.100), channel_id=1, replica_groups=mesh['wide'=16,'col'=8] {'wide'}, dimensions={0} | all-to-all | bytes 4194304 | tf_op jit(solution)/shard_map/all_to_all | solution.py:35
  303.5 0.8 copy-done.4
  304.3 0.7 fusion.25
  305.2 0.7 fusion.24
  305.9 2.0 collective-permute-done.5
  308.0 18.1 %all_to_all.69 = f32[4,64,4,256]{3,1,2,0:T(8,128)S(1)} all-to-all(f32[4,64,4,256]{3,1,2,0:T(8,128)S(1)} %copy_add_fusion), channel_id=1, replica_groups={{0,2,4,6},{1,3,5,7},{8,10,12,14},{9,11,13,15},{16,18,20,22},{17,19,21,2..., dimensions={0} | all-to-all | bytes 2097152 | tf_op jit(solution)/shard_map/all_to_all | solution.py:89
  326.1 1.0 copy_subtract_fusion
  327.3 17.3 %all_to_all.70 = f32[4,64,4,256]{3,1,2,0:T(8,128)S(1)} all-to-all(f32[4,64,4,256]{3,1,2,0:T(8,128)S(1)} %broadcast_in_dim.101), channel_id=1, replica_groups={{0,2,4,6},{1,3,5,7},{8,10,12,14},{9,11,13,15},{16,18,20,22},{17,19,21,2..., dimensions={0} | all-to-all | bytes 2097152 | tf_op jit(solution)/shard_map/all_to_all | solution.py:62
  344.7 1.2 fusion.26
  345.8 1.4 collective-permute-done.6
  347.3 1.2 fusion.27
  348.5 0.8 maximum_select_fusion.2
  349.8 54.1 %all_to_all.71 = f32[16,32,4,512]{3,1,2,0:T(8,128)S(1)} all-to-all(f32[16,32,4,512]{3,1,2,0:T(8,128)S(1)} %copy.188), channel_id=1, replica_groups=mesh['wide'=16,'col'=8] {'wide'}, dimensions={0} | all-to-all | bytes 8388608 | tf_op jit(solution)/shard_map/all_to_all | solution.py:28
  404.6 0.9 copy.191
  (99 shorter events, 9.6 us)
Async XLA Ops:
  0.6 344.0 %copy-start = (f32[4,256,512]{2,1,0:T(8,128)S(1)}, f32[4,256,512]{2,1,0:T(8,128)}, u32[]{:S(2)}) copy-start(f32[4,256,512]{2,1,0:T(8,128)} %param.19) | copy-start | bytes 6291460
  3.5 25.0 %copy-start.1 = (f32[1024,2048]{1,0:T(8,128)S(1)}, f32[1024,2048]{1,0:T(8,128)}, u32[]{:S(2)}) copy-start(f32[1024,2048]{1,0:T(8,128)} %param.17) | copy-start | bytes 25165828
  25.2 2.9 collective-permute-start
  98.2 17.9 %copy-start.5 = (f32[32,2048]{1,0:T(8,128)}, f32[32,2048]{1,0:T(8,128)S(1)}, u32[]{:S(2)}) copy-start(f32[32,2048]{1,0:T(8,128)S(1)} %reduce_sum.91) | copy-start | bytes 786436
  99.9 2.3 collective-permute-start.1
  147.0 1.6 copy-start.3
  149.9 2.7 collective-permute-start.2
  171.7 18.9 %copy-start.2 = (f32[2,512,1024]{2,1,0:T(8,128)S(1)}, f32[2,512,1024]{2,1,0:T(8,128)}, u32[]{:S(2)}) copy-start(f32[2,512,1024]{2,1,0:T(8,128)} %param.18) | copy-start | bytes 12582916
  190.5 2.7 collective-permute-start.3
  253.8 0.7 copy-start.6
  256.1 2.3 collective-permute-start.4
  303.1 1.2 copy-start.4
  305.1 2.7 collective-permute-start.5
  344.5 2.7 collective-permute-start.6
